TPU v7x, 512 devices: a whole 4x8x8 slice. The times are simulated.
512 devices in a mesh: dp: 32 (over z_lo, y, core), loop: 16 (over z_hi, x).
Axes of the slice: x: 4, y: 8, z: 8 (z_hi: 4, z_lo: 2; z = z_hi * 2 + z_lo), core: 2. Of those that a mesh axis runs over, the one named last changes fastest.
Arguments:
- tokens: bfloat16 [768, 3072], P('dp', 'loop'), may hold values from -6 to 6
- expert_ids: int32 [768, 2], P('dp'), may hold values from 0 to 7, all different within a row; in each aligned block of 24 rows (0 to 23, 24 to 47, ...) at most 10 rows name the same one
- route_logits: float32 [768, 2], P('dp'), may hold values from -8 to 8
- gate_weight: bfloat16 [32, 3072, 4096], P('dp', None, 'loop'), may hold values from -0.109375 to 0.109375
- up_weight: bfloat16 [32, 3072, 4096], P('dp', None, 'loop'), may hold values from -0.109375 to 0.109375
- down_weight: bfloat16 [32, 4096, 3072], P('dp', 'loop'), may hold values from -0.046875 to 0.046875
Outputs:
- mixed: bfloat16 [768, 3072], P('dp', 'loop')
Inputs may be any that keep to these rules, and one draw needn't show every extreme that they name: `expert_ids`: the two experts of a token differ. Among the tokens of one index of dp (aligned blocks of 24 rows) no expert is named more than 10 times, a bound that some block reaches.
All inputs are finite; a program needn't handle non-finite values.
Results may differ from a plain program's by a relative error of at most 0.02.
Values may be sent and summed in bfloat16 or wider, within the bound.
No kernel may reach another device: no remote copies, remote signals or barrier semaphores. Data moves between devices by JAX's collectives and lax.ppermute only.
A program may use at most 64 MiB of HBM per device.

v0:
```python
import jax
import jax.numpy as jnp
from jax import lax
from jax.sharding import PartitionSpec as P

EXPERTS = 8
CAP = 10


def assignment_slots(expert_ids):
    assigned = expert_ids.reshape(-1)
    onehot = (assigned[:, None] == jnp.arange(EXPERTS, dtype=jnp.int32)[None, :]).astype(jnp.int32)
    before = jnp.cumsum(onehot, axis=0) - onehot
    return (assigned, jnp.sum(before * onehot, axis=1))


def body(tokens, expert_ids, route_logits, gate_weight, up_weight, down_weight):
    groups = lax.axis_size("dp")
    copies = groups // EXPERTS
    tok_count = tokens.shape[0]
    model_width = gate_weight.shape[1]
    slice_width = model_width // lax.axis_size("loop")
    assigned, position = assignment_slots(expert_ids)
    slot_index = jnp.arange(EXPERTS * CAP, dtype=jnp.int32)
    picker = (slot_index[:, None] == (assigned * CAP + position)[None, :]).astype(jnp.bfloat16)
    picker = picker.reshape(EXPERTS * CAP, tok_count, 2).sum(axis=2)
    gate_local = gate_weight[0]
    up_local = up_weight[0]
    down_local = down_weight[0]
    packed = jnp.dot(picker, tokens, preferred_element_type=jnp.float32).astype(jnp.bfloat16)
    packed = packed.reshape(EXPERTS, CAP, tokens.shape[1])
    arrived = lax.all_to_all(
        jnp.repeat(packed, copies, axis=0), "dp", split_axis=0, concat_axis=0, tiled=True
    )
    buffer_rows = arrived.reshape(groups * CAP, arrived.shape[2])
    segment = lax.all_gather(buffer_rows, "loop", axis=1, tiled=True)
    gate_sum = jnp.dot(segment, gate_local, preferred_element_type=jnp.float32)
    up_sum = jnp.dot(segment, up_local, preferred_element_type=jnp.float32)
    hidden = (jax.nn.silu(gate_sum) * up_sum).astype(jnp.bfloat16)
    reduced = (
        lax.psum_scatter(
            lax.dot_general(
                down_local, hidden, (((0,), (1,)), ((), ())), preferred_element_type=jnp.float32
            ).astype(jnp.bfloat16),
            "loop",
            scatter_dimension=0,
            tiled=True,
        )
        .astype(jnp.float32)
        .T
    )
    expert_out = reduced.astype(jnp.bfloat16).reshape(groups, CAP, slice_width)
    returned = lax.all_to_all(expert_out, "dp", split_axis=0, concat_axis=0, tiled=True).reshape(
        groups * CAP, slice_width
    )
    column_index = jnp.arange(groups * CAP, dtype=jnp.int32)
    same_expert = (column_index // CAP // copies)[None, :] == assigned[:, None]
    same_slot = (column_index % CAP)[None, :] == position[:, None]
    collector = (same_expert & same_slot).astype(jnp.bfloat16)
    gathered = jnp.dot(collector, returned, preferred_element_type=jnp.float32).reshape(
        tok_count, 2, slice_width
    )
    weights = jax.nn.sigmoid(route_logits - route_logits[:, ::-1])
    mixed = jnp.sum(weights[:, :, None] * gathered, axis=1)
    return mixed.astype(jnp.bfloat16)


def solution(mesh):
    in_specs = (
        P("dp", "loop"),
        P("dp", None),
        P("dp", None),
        P("dp", None, "loop"),
        P("dp", None, "loop"),
        P("dp", "loop", None),
    )
    out_specs = P("dp", "loop")
    return jax.shard_map(body, mesh=mesh, in_specs=in_specs, out_specs=out_specs, check_vma=False)
```

profile of v0, /device:TPU:1, one launch (start us, length us, event | category | flops | bytes accessed | tf_op | source)
XLA Modules:
  0.0 231.0 jit_solution(16621940932775752163)
XLA Ops:
  6.5 0.0 copy-start
  6.5 0.0 copy-start.1
  6.5 0.0 all-gather.2.cloned.1.call-start
  6.5 0.9 copy.30
  7.4 0.1 eq.73
  7.5 0.1 fusion.29
  7.6 0.1 reduce_window_sum.11
  7.7 0.2 select_reduce_fusion
  7.9 0.1 eq.77
  8.0 0.1 copy.31
  8.1 0.7 multiply_add_fusion
  8.8 0.1 fusion.31
  8.8 0.9 convolution_convert_fusion.1
  9.8 0.2 reshape.104
  10.0 19.5 %all_to_all.10 = bf16[32,2,960]{2,1,0:T(2,128)(2,1)} all-to-all(bf16[32,2,960]{2,1,0:T(2,128)(2,1)S(1)} %reshape.104), channel_id=1, replica_groups=mesh['dp'=32,'loop'=16] {'dp'}, dimensions={0} | all-to-all | bytes 245760 | tf_op jit(solution)/shard_map/all_to_all | solution.py:32
  29.5 1.1 reshape.105
  30.6 0.7 reshape.98
  31.3 1.7 copy.33
  33.0 0.0 all-gather.2.cloned.1.call-update
  33.0 0.0 reduce-scatter.4.cloned.1.call-start
  33.1 65.8 %all-gather.2.cloned.1.call-done = bf16[320,3072]{0,1:T(8,128)(2,1)} async-done(((bf16[320,192]{0,1:T(8,128)(2,1)}), bf16[320,3072]{0,1:T(8,128)(2,1)}) %all-gather.2.cloned.1.call-update) | async-done | bytes 1966096 | tf_op jit(solution)/shard_map/all_gather | solution.py:36
  98.9 0.0 copy-done.1
  98.9 3.2 %fusion.4 = f32[320,256]{1,0:T(8,128)} fusion(bf16[320,3072]{0,1:T(8,128)(2,1)} %all-gather.2.cloned.1.call-done, bf16[1,3072,256]{2,1,0:T(8,128)(2,1)S(1)} %copy-done.1), kind=kOutput, calls=%fused_computation.5 | convolution fusion | flops 503316480 | bytes 3866624 | tf_op jit(solution)/shard_map/dot_general | solution.py:37
  102.1 0.0 copy-done
  102.1 4.4 %fusion = bf16[3072,320]{0,1:T(8,128)(2,1)S(1)} fusion(bf16[1,256,3072]{2,1,0:T(8,128)(2,1)S(1)} %copy-done, bf16[320,3072]{0,1:T(8,128)(2,1)} %all-gather.2.cloned.1.call-done, bf16[1,3072,256]{2,1,0:T(8,128)(2,1)} %param.10, f32[320,256]{1,0:T(8,128)} %fusion.4), kind=kOutput, calls=%fused_computation.1 | convolution fusion | flops 1008107520 | bytes 7405568 | tf_op jit(solution)/shard_map/dot_general | solution.py:42
  106.5 2.4 %copy.37 = bf16[3072,320]{1,0:T(8,128)(2,1)} copy(bf16[3072,320]{0,1:T(8,128)(2,1)S(1)} %fusion) | data formatting | bytes 3932160
  108.9 0.0 copy-start.2
  109.0 0.0 reduce-scatter.4.cloned.1.call-update
  109.0 0.0 copy-start.3
  109.0 93.5 %reduce-scatter.4.cloned.1.call-done = bf16[192,320]{1,0:T(8,128)(2,1)} async-done(((bf16[3072,320]{1,0:T(8,128)(2,1)}), bf16[192,320]{1,0:T(8,128)(2,1)}) %reduce-scatter.4.cloned.1.call-update) | async-done | bytes 122896
  202.5 1.0 copy.38
  203.5 0.1 reshape.99
  203.6 0.9 reshape.106
  204.4 9.7 %all-to-all-start.1 = ((bf16[32,2,960]{2,1,0:T(2,128)(2,1)}), bf16[32,2,960]{2,1,0:T(2,128)(2,1)S(1)}, u32[]{:S(2)}, u32[]{:S(2)}) async-start(bf16[32,2,960]{2,1,0:T(2,128)(2,1)} %reshape.106), calls=%async_computation.1 | async-start | bytes 262144 | tf_op jit(solution)/shard_map/all_to_all | solution.py:53
  214.1 0.0 copy-done.2
  214.2 8.9 %all-to-all-done.1 = bf16[32,2,960]{2,1,0:T(2,128)(2,1)S(1)} async-done(((bf16[32,2,960]{2,1,0:T(2,128)(2,1)}), bf16[32,2,960]{2,1,0:T(2,128)(2,1)S(1)}, u32[]{:S(2)}, u32[]{:S(2)}) %all-to-all-start.1) | async-done | bytes 122912 | tf_op jit(solution)/shard_map/all_to_all | solution.py:53
  223.1 0.2 reshape.107
  223.3 0.1 reshape.100
  223.4 0.0 copy-done.3
  223.4 0.8 fusion.14
  (5 shorter events, 0.1 us)
Async XLA Ops:
  6.5 95.6 %copy-start = (bf16[1,256,3072]{2,1,0:T(8,128)(2,1)S(1)}, bf16[1,256,3072]{2,1,0:T(8,128)(2,1)}, u32[]{:S(2)}) copy-start(bf16[1,256,3072]{2,1,0:T(8,128)(2,1)} %param.11) | copy-start | bytes 4718596
  6.5 92.4 %copy-start.1 = (bf16[1,3072,256]{2,1,0:T(8,128)(2,1)S(1)}, bf16[1,3072,256]{2,1,0:T(8,128)(2,1)}, u32[]{:S(2)}) copy-start(bf16[1,3072,256]{2,1,0:T(8,128)(2,1)} %param.9) | copy-start | bytes 4718596
  6.5 92.4 %all-gather.2.cloned.1.call-start = ((), (), s32[]{:S(2)}) async-start(), calls=%async_computation.3 | async-start | bytes 2506752 | tf_op jit(solution)/shard_map/all_gather | solution.py:36
  33.0 169.4 %reduce-scatter.4.cloned.1.call-start = ((), (), s32[]{:S(2)}) async-start(), calls=%async_computation.4 | async-start | bytes 2506752
  108.9 105.2 %copy-start.2 = (f32[24,2]{0,1:T(2,128)S(1)}, f32[24,2]{0,1:T(2,128)}, u32[]{:S(2)}) copy-start(f32[24,2]{0,1:T(2,128)} %param.8) | copy-start | bytes 580
  109.0 114.4 %copy-start.3 = (s32[24,2]{0,1:T(2,128)S(1)}, s32[24,2]{0,1:T(2,128)}, u32[]{:S(2)}) copy-start(s32[24,2]{0,1:T(2,128)} %param.7) | copy-start | bytes 580
  204.4 18.7 %all-to-all-start.1 = ((bf16[32,2,960]{2,1,0:T(2,128)(2,1)}), bf16[32,2,960]{2,1,0:T(2,128)(2,1)S(1)}, u32[]{:S(2)}, u32[]{:S(2)}) async-start(bf16[32,2,960]{2,1,0:T(2,128)(2,1)} %reshape.106), calls=%async_computation.1 | async-start | bytes 262144 | tf_op jit(solution)/shard_map/all_to_all | solution.py:53
Sparse Core Ops, SparseCore 0:
  33.2 65.7 all-gather.1
  109.1 93.3 reduce-scatter.3
where the time goes:
time: 231 us
  waiting for transfers between devices  168 us (73%)
  blocking collectives  19.5 us (8%)
  between operations  13.5 us (6%)
  local copies, waits for them, and re-layouts  9.7 us (4%)
  starting transfers between devices  9.7 us (4%)
  matrix products  9.28 us (4%)
    unnamed x3, waiting for transfers between devices  93.5 us
    all_gather x1, waiting for transfers between devices, body(): segment = lax.all_gather(buffer_rows, 'loop', axis=1, tiled=True)  65.8 us
    all_to_all x1, blocking collectives, body(): lax.all_to_all(jnp.repeat(packed, copies, axis=0), 'dp', split_axis=0, co...  19.5 us
    all_to_all x1, starting transfers between devices, body(): lax.all_to_all(expert_out, 'dp', split_axis=0, concat_axis=0, tiled=True)  9.66 us
    all_to_all x1, waiting for transfers between devices, body(): lax.all_to_all(expert_out, 'dp', split_axis=0, concat_axis=0, tiled=True)  8.92 us
    unnamed x15, local copies, waits for them, and re-layouts  6.75 us
  transfers between devices with their start and end apart: 3, of which 3 were waited for; matrix products, arithmetic and copies ran while one was open for 0% of the time, Pallas kernels for 0%

commit v1 on v0

v1 whole, which is shorter than its diff:
```python
import jax
import jax.numpy as jnp
from jax import lax
from jax.sharding import Mesh
from jax.sharding import PartitionSpec as P

EXPERTS = 8
CAP = 10
GROUP_AXES = ("zl", "yh", "yl")
LOOP_AXES = ("zh", "x")


def assignment_slots(expert_ids):
    assigned = expert_ids.reshape(-1)
    onehot = (assigned[:, None] == jnp.arange(EXPERTS, dtype=jnp.int32)[None, :]).astype(jnp.int32)
    before = jnp.cumsum(onehot, axis=0) - onehot
    return (assigned, jnp.sum(before * onehot, axis=1))


def swap_cores(x):
    return lax.ppermute(x, "c", [(0, 1), (1, 0)])


def body(tokens, expert_ids, route_logits, gate_weight, up_weight, down_weight):
    peers = lax.axis_size(GROUP_AXES)
    n_loop = lax.axis_size(LOOP_AXES)
    halves = peers // EXPERTS
    tok_count, slice_width = tokens.shape
    model_width = gate_weight.shape[1]
    hidden_width = gate_weight.shape[2]
    rows = peers * CAP
    assigned, position = assignment_slots(expert_ids)
    slot_index = jnp.arange(EXPERTS * CAP, dtype=jnp.int32)
    picker = (slot_index[:, None] == (assigned * CAP + position)[None, :]).astype(jnp.bfloat16)
    picker = picker.reshape(EXPERTS * CAP, tok_count, 2).sum(axis=2)
    packed = jnp.dot(picker, tokens, preferred_element_type=jnp.float32).astype(jnp.bfloat16)
    packed = packed.reshape(EXPERTS, CAP, slice_width)
    arrived = lax.all_to_all(
        jnp.repeat(packed, halves, axis=0), GROUP_AXES, split_axis=0, concat_axis=0, tiled=True
    )
    lane = 128
    dense = arrived.reshape(rows * slice_width // lane, lane)
    spread = lax.all_to_all(
        jnp.broadcast_to(dense[None], (n_loop,) + dense.shape), LOOP_AXES, 0, 0, tiled=True
    )
    own = spread.reshape(n_loop, rows, slice_width)
    other = swap_cores(spread).reshape(n_loop, rows, slice_width)
    segment = jnp.concatenate([own, other], axis=1)
    segment = segment.transpose(1, 0, 2).reshape(2 * rows, model_width)
    gate_sum = jnp.dot(segment, gate_weight[0], preferred_element_type=jnp.float32)
    up_sum = jnp.dot(segment, up_weight[0], preferred_element_type=jnp.float32)
    hidden = (jax.nn.silu(gate_sum) * up_sum).astype(jnp.bfloat16)
    partial = jnp.dot(hidden, down_weight[0], preferred_element_type=jnp.float32)
    partner_part = swap_cores(partial[rows:].astype(jnp.bfloat16))
    pair_sum = (partial[:rows] + partner_part.astype(jnp.float32)).astype(jnp.bfloat16)
    by_slice = pair_sum.reshape(rows, n_loop, slice_width).transpose(1, 0, 2)
    by_slice = by_slice.reshape(n_loop, rows * slice_width // lane, lane)
    summed = lax.all_to_all(by_slice, LOOP_AXES, 0, 0, tiled=True)
    summed = summed.reshape(n_loop, rows, slice_width).astype(jnp.float32).sum(axis=0)
    expert_out = summed.astype(jnp.bfloat16).reshape(peers, CAP, slice_width)
    returned = lax.all_to_all(expert_out, GROUP_AXES, split_axis=0, concat_axis=0, tiled=True).reshape(
        rows, slice_width
    )
    column_index = jnp.arange(rows, dtype=jnp.int32)
    same_expert = (column_index // CAP // halves)[None, :] == assigned[:, None]
    same_slot = (column_index % CAP)[None, :] == position[:, None]
    collector = (same_expert & same_slot).astype(jnp.bfloat16)
    gathered = jnp.dot(collector, returned, preferred_element_type=jnp.float32).reshape(
        tok_count, 2, slice_width
    )
    weights = jax.nn.sigmoid(route_logits - route_logits[:, ::-1])
    mixed = jnp.sum(weights[:, :, None] * gathered, axis=1)
    return mixed.astype(jnp.bfloat16)


def solution(mesh):
    dp, loop = mesh.shape["dp"], mesh.shape["loop"]
    fine = Mesh(
        mesh.devices.reshape(2, dp // 8, 2, 2, loop // 4, 4), GROUP_AXES + ("c",) + LOOP_AXES
    )
    dp_axes = GROUP_AXES + ("c",)
    in_specs = (
        P(dp_axes, LOOP_AXES),
        P(dp_axes, None),
        P(dp_axes, None),
        P(dp_axes, None, LOOP_AXES),
        P(dp_axes, None, LOOP_AXES),
        P(dp_axes, LOOP_AXES, None),
    )
    out_specs = P(dp_axes, LOOP_AXES)
    return jax.shard_map(body, mesh=fine, in_specs=in_specs, out_specs=out_specs, check_vma=False)
```

time: 231 us -> 148 us (0.64)
  waiting for transfers between devices: 168 us -> 37.7 us
  blocking collectives: 19.5 us -> 54.6 us
  between operations: 13.5 us -> 0.18 us
  local copies, waits for them, and re-layouts: 9.7 us -> 22.2 us
  other arithmetic: 1.13 us -> 7.33 us
  starting transfers between devices: 9.7 us -> 14.4 us
    unnamed x3 -> x0, waiting for transfers between devices: 93.5 us -> none
    all_gather x1 -> x0, waiting for transfers between devices: 65.8 us -> none  [body(): segment = lax.all_gather(buffer_rows, 'loop', axis=1, tiled=True)]
    all_to_all x1 -> x2, blocking collectives: 19.5 us -> 54.6 us  [the longest x1 37.9 us: body(): lax.all_to_all(jnp.broadcast_to(dense[None], (n_loop,) + dense.shape), LO...]
    all_to_all x1 -> x2, waiting for transfers between devices: 8.92 us -> 35.5 us  [the longest x1 28.2 us: body(): summed = lax.all_to_all(by_slice, LOOP_AXES, 0, 0, tiled=True)]
    reshape x5 -> x8, local copies, waits for them, and re-layouts: 2.63 us -> 13.5 us  [the longest x2 4.08 us: body(): by_slice = pair_sum.reshape(rows, n_loop, slice_width).transpose(1, 0, 2)]
    ppermute x0 -> x2, starting transfers between devices: none -> 6.41 us  [swap_cores(): return lax.ppermute(x, 'c', [(0, 1), (1, 0)])]
    unnamed x15 -> x13, local copies, waits for them, and re-layouts: 6.75 us -> 2.02 us
    transpose x0 -> x1, local copies, waits for them, and re-layouts: none -> 4.42 us  [body(): segment = segment.transpose(1, 0, 2).reshape(2 * rows, model_width)]
  transfers between devices with their start and end apart: 3 -> 4, of which waited for: 3 -> 3; matrix products, arithmetic and copies ran while one was open for 0% -> 2% of each run, Pallas kernels for 0% -> 0%
where the time goes in v1:
time: 148 us; the launch traced here: 147 us
  blocking collectives  54.6 us (37%)
  waiting for transfers between devices  37.7 us (25%)
  local copies, waits for them, and re-layouts  22.2 us (15%)
  starting transfers between devices  14.4 us (10%)
  matrix products  10.5 us (7%)
  other arithmetic  7.33 us (5%)
    all_to_all x1, blocking collectives, body(): lax.all_to_all(jnp.broadcast_to(dense[None], (n_loop,) + dense.shape), LO...  37.9 us
    all_to_all x1, waiting for transfers between devices, body(): summed = lax.all_to_all(by_slice, LOOP_AXES, 0, 0, tiled=True)  28.2 us
    all_to_all x1, blocking collectives, body(): lax.all_to_all(jnp.repeat(packed, halves, axis=0), GROUP_AXES, split_axis...  16.7 us
    all_to_all x1, waiting for transfers between devices, body(): lax.all_to_all(expert_out, GROUP_AXES, split_axis=0, concat_axis=0, tiled...  7.3 us
    ppermute x2, starting transfers between devices, swap_cores(): return lax.ppermute(x, 'c', [(0, 1), (1, 0)])  6.41 us
    dot_general x1, matrix products, body(): jnp.dot(hidden, down_weight[0], preferred_element_type=jnp.float32)  5.78 us
    all_to_all x1, starting transfers between devices, body(): summed = lax.all_to_all(by_slice, LOOP_AXES, 0, 0, tiled=True)  4.48 us
    transpose x1, local copies, waits for them, and re-layouts, body(): segment = segment.transpose(1, 0, 2).reshape(2 * rows, model_width)  4.42 us
  transfers between devices with their start and end apart: 4, of which 3 were waited for; matrix products, arithmetic and copies ran while one was open for 2% of the time, Pallas kernels for 0%

profile of v1, /device:TPU:1, one launch (start us, length us, event | category | flops | bytes accessed | tf_op | source)
XLA Modules:
  0.0 146.9 jit_solution(4980719666542735517)
XLA Ops:
  0.0 0.0 copy-start
  0.0 0.9 copy.29
  0.9 0.1 eq.73
  1.0 0.1 fusion.26
  1.1 0.1 reduce_window_sum.11
  1.1 0.2 select_reduce_fusion
  1.3 0.1 eq.77
  1.4 0.1 copy.30
  1.5 0.7 multiply_add_fusion
  2.2 0.1 fusion.31
  2.3 0.9 convolution_convert_fusion
  3.2 0.1 reshape.123
  3.3 16.7 %all_to_all.20 = bf16[16,2,960]{2,1,0:T(2,128)(2,1)S(1)} all-to-all(bf16[16,2,960]{2,1,0:T(2,128)(2,1)S(1)} %reshape.123), channel_id=1, replica_groups=mesh['zl'=2,'yh'=4,'yl'=2,'c'=2,'zh'=4,'x'=4] {'zl','yh','yl'}, dimensions={0} | all-to-all | bytes 122880 | tf_op jit(solution)/shard_map/all_to_all | solution.py:38
  20.1 0.1 reshape.124
  20.2 0.1 broadcast_in_dim.7
  20.3 0.1 broadcast_in_dim.8
  20.5 37.9 %all_to_all.21 = bf16[16,240,128]{2,1,0:T(8,128)(2,1)} all-to-all(bf16[16,240,128]{2,1,0:T(8,128)(2,1)S(1)} %broadcast_in_dim.8), channel_id=1, replica_groups=mesh['zl'=2,'yh'=4,'yl'=2,'c'=2,'zh'=4,'x'=4] {'zh','x'}, dimensions={0} | all-to-all | bytes 1966080 | tf_op jit(solution)/shard_map/all_to_all | solution.py:43
  58.4 4.1 %collective-permute-start = (bf16[16,240,128]{2,1,0:T(8,128)(2,1)}, bf16[16,240,128]{2,1,0:T(8,128)(2,1)}, u32[]{:S(2)}, u32[]{:S(2)}) collective-permute-start(bf16[16,240,128]{2,1,0:T(8,128)(2,1)} %all_to_all.21), channel_id=1, source_target_pairs={{0,16},{16,0},{1,17},{17,1},{2,18},{18,2},{3,19},{19,3},{4,20},{20... | collective-permute-start | bytes 2949128 | tf_op jit(solution)/shard_map/ppermute | solution.py:21
  62.5 2.5 %reshape.114 = bf16[16,160,192]{2,1,0:T(8,128)(2,1)S(1)} reshape(bf16[16,240,128]{2,1,0:T(8,128)(2,1)} %all_to_all.21) | data formatting | bytes 1966080 | tf_op jit(solution)/shard_map/reshape | solution.py:46
  65.0 0.0 collective-permute-done
  65.0 3.2 %reshape.115 = bf16[16,160,192]{2,1,0:T(8,128)(2,1)} reshape(bf16[16,240,128]{2,1,0:T(8,128)(2,1)} %collective-permute-done) | data formatting | bytes 1966080 | tf_op jit(solution)/shard_map/reshape | solution.py:47
  68.2 3.3 %maximum_bitcast_fusion = bf16[320,16,192]{2,0,1:T(8,128)(2,1)} fusion(bf16[16,160,192]{2,1,0:T(8,128)(2,1)} %reshape.115, bf16[16,160,192]{2,1,0:T(8,128)(2,1)S(1)} %reshape.114), kind=kLoop, calls=%fused_computation | loop fusion | flops 3932160 | bytes 3932160 | tf_op jit(solution)/shard_map/transpose | solution.py:49
  71.5 4.4 %copy.32 = bf16[320,16,192]{0,2,1:T(8,128)(2,1)} copy(bf16[320,16,192]{2,0,1:T(8,128)(2,1)} %maximum_bitcast_fusion) | data formatting | bytes 3932160 | tf_op jit(solution)/shard_map/transpose | solution.py:49
  75.9 0.0 copy-start.1
  75.9 3.0 %fusion.5 = f32[320,256]{1,0:T(8,128)S(1)} fusion(bf16[320,3072]{0,1:T(8,128)(2,1)} %bitcast.27, bf16[1,3072,256]{2,1,0:T(8,128)(2,1)} %param.9), kind=kOutput, calls=%fused_computation.8 | convolution fusion | flops 503316480 | bytes 3866624 | tf_op jit(solution)/shard_map/dot_general | solution.py:50
  79.0 0.0 copy-done
  79.0 0.0 copy-done.1
  79.0 5.8 %fusion.1 = f32[320,3072]{1,0:T(8,128)} fusion(bf16[1,256,3072]{2,1,0:T(8,128)(2,1)S(1)} %copy-done, bf16[320,3072]{0,1:T(8,128)(2,1)} %bitcast.28, bf16[1,3072,256]{2,1,0:T(8,128)(2,1)S(1)} %copy-done.1, f32[320,256]{1,0:T(8,128)S(1)} %fusion.5), kind=kOutput, calls=%fused_computation.4 | convolution fusion | flops 1007124480 | bytes 9371648 | tf_op jit(solution)/shard_map/dot_general | solution.py:53
  84.8 1.7 %slice.15 = bf16[160,3072]{1,0:T(8,128)(2,1)S(1)} slice(f32[320,3072]{1,0:T(8,128)} %fusion.1), slice={[160:320], [0:3072]} | slice | bytes 1966080 | tf_op jit(solution)/shard_map/slice | solution.py:54
  86.4 2.3 %collective-permute-start.1 = (bf16[160,3072]{1,0:T(8,128)(2,1)S(1)}, bf16[160,3072]{1,0:T(8,128)(2,1)S(1)}, u32[]{:S(2)}, u32[]{:S(2)}) collective-permute-start(bf16[160,3072]{1,0:T(8,128)(2,1)S(1)} %slice.15), channel_id=1, source_target_pairs={{0,16},{16,0},{1,17},{17,1},{2,18},{18,2},{3,19},{19,3},{4,20},{20... | collective-permute-start | bytes 2949128 | tf_op jit(solution)/shard_map/ppermute | solution.py:21
  88.7 2.2 %collective-permute-done.1 = bf16[160,3072]{1,0:T(8,128)(2,1)S(1)} collective-permute-done((bf16[160,3072]{1,0:T(8,128)(2,1)S(1)}, bf16[160,3072]{1,0:T(8,128)(2,1)S(1)}, u32[]{:S(2)}, u32[]{:S(2)}) %collective-permute-start.1) | collective-permute-done | bytes 983072 | tf_op jit(solution)/shard_map/ppermute | solution.py:21
  90.9 2.8 %fusion = bf16[160,3072]{1,0:T(8,128)(2,1)} fusion(f32[320,3072]{1,0:T(8,128)} %fusion.1, bf16[160,3072]{1,0:T(8,128)(2,1)S(1)} %collective-permute-done.1), kind=kLoop, calls=%fused_computation.3 | loop fusion | flops 1474560 | bytes 3932160 | tf_op jit(solution)/shard_map/convert_element_type | solution.py:55
  93.7 2.6 %reshape.117 = bf16[160,16,192]{2,1,0:T(8,128)(2,1)S(1)} reshape(bf16[160,3072]{1,0:T(8,128)(2,1)} %fusion) | data formatting | bytes 1966080 | tf_op jit(solution)/shard_map/reshape | solution.py:56
  96.3 1.5 %copy.35 = bf16[160,16,192]{2,0,1:T(8,128)(2,1)} copy(bf16[160,16,192]{2,1,0:T(8,128)(2,1)S(1)} %reshape.117) | data formatting | bytes 1966080 | tf_op jit(solution)/shard_map/reshape | solution.py:56
  97.7 0.0 copy-start.2
  97.8 3.6 %reshape.118 = bf16[16,240,128]{2,1,0:T(8,128)(2,1)} reshape(bf16[16,160,192]{2,1,0:T(8,128)(2,1)} %bitcast.29) | data formatting | bytes 1966080 | tf_op jit(solution)/shard_map/reshape | solution.py:57
  101.4 4.5 %all-to-all-start.2 = ((bf16[16,240,128]{2,1,0:T(8,128)(2,1)}), bf16[16,240,128]{2,1,0:T(8,128)(2,1)S(1)}, u32[]{:S(2)}, u32[]{:S(2)}) async-start(bf16[16,240,128]{2,1,0:T(8,128)(2,1)} %reshape.118), calls=%async_computation.2 | async-start | bytes 1966080 | tf_op jit(solution)/shard_map/all_to_all | solution.py:58
  105.9 0.0 copy-done.2
  105.9 28.2 %all-to-all-done.2 = bf16[16,240,128]{2,1,0:T(8,128)(2,1)S(1)} async-done(((bf16[16,240,128]{2,1,0:T(8,128)(2,1)}), bf16[16,240,128]{2,1,0:T(8,128)(2,1)S(1)}, u32[]{:S(2)}, u32[]{:S(2)}) %all-to-all-start.2) | async-done | bytes 983072 | tf_op jit(solution)/shard_map/all_to_all | solution.py:58
  134.1 0.1 reduce_sum.44
  134.2 0.1 reshape.119
  134.3 0.7 reshape.125
  135.1 3.5 %all-to-all-start.3 = ((bf16[16,2,960]{2,1,0:T(2,128)(2,1)}), bf16[16,2,960]{2,1,0:T(2,128)(2,1)S(1)}, u32[]{:S(2)}, u32[]{:S(2)}) async-start(bf16[16,2,960]{2,1,0:T(2,128)(2,1)} %reshape.125), calls=%async_computation.3 | async-start | bytes 131072 | tf_op jit(solution)/shard_map/all_to_all | solution.py:61
  138.6 7.3 %all-to-all-done.3 = bf16[16,2,960]{2,1,0:T(2,128)(2,1)S(1)} async-done(((bf16[16,2,960]{2,1,0:T(2,128)(2,1)}), bf16[16,2,960]{2,1,0:T(2,128)(2,1)S(1)}, u32[]{:S(2)}, u32[]{:S(2)}) %all-to-all-start.3) | async-done | bytes 61472 | tf_op jit(solution)/shard_map/all_to_all | solution.py:61
  145.9 0.1 reshape.126
  146.1 0.1 reshape.121
  146.1 0.0 copy-done.3
  146.1 0.8 fusion.15
  (6 shorter events, 0.1 us)
Async XLA Ops:
  0.0 79.0 %copy-start = (bf16[1,256,3072]{2,1,0:T(8,128)(2,1)S(1)}, bf16[1,256,3072]{2,1,0:T(8,128)(2,1)}, u32[]{:S(2)}) copy-start(bf16[1,256,3072]{2,1,0:T(8,128)(2,1)} %param.11) | copy-start | bytes 4718596
  58.4 6.7 %collective-permute-start = (bf16[16,240,128]{2,1,0:T(8,128)(2,1)}, bf16[16,240,128]{2,1,0:T(8,128)(2,1)}, u32[]{:S(2)}, u32[]{:S(2)}) collective-permute-start(bf16[16,240,128]{2,1,0:T(8,128)(2,1)} %all_to_all.21), channel_id=1, source_target_pairs={{0,16},{16,0},{1,17},{17,1},{2,18},{18,2},{3,19},{19,3},{4,20},{20... | collective-permute-start | bytes 2949128 | tf_op jit(solution)/shard_map/ppermute | solution.py:21
  75.9 3.1 %copy-start.1 = (bf16[1,3072,256]{2,1,0:T(8,128)(2,1)S(1)}, bf16[1,3072,256]{2,1,0:T(8,128)(2,1)}, u32[]{:S(2)}) copy-start(bf16[1,3072,256]{2,1,0:T(8,128)(2,1)} %param.10) | copy-start | bytes 4718596
  86.4 4.5 %collective-permute-start.1 = (bf16[160,3072]{1,0:T(8,128)(2,1)S(1)}, bf16[160,3072]{1,0:T(8,128)(2,1)S(1)}, u32[]{:S(2)}, u32[]{:S(2)}) collective-permute-start(bf16[160,3072]{1,0:T(8,128)(2,1)S(1)} %slice.15), channel_id=1, source_target_pairs={{0,16},{16,0},{1,17},{17,1},{2,18},{18,2},{3,19},{19,3},{4,20},{20... | collective-permute-start | bytes 2949128 | tf_op jit(solution)/shard_map/ppermute | solution.py:21
  97.7 8.1 %copy-start.2 = (f32[24,2]{0,1:T(2,128)S(1)}, f32[24,2]{0,1:T(2,128)}, u32[]{:S(2)}) copy-start(f32[24,2]{0,1:T(2,128)} %param.8) | copy-start | bytes 580
  101.4 44.7 %copy-start.3 = (s32[24,2]{0,1:T(2,128)S(1)}, s32[24,2]{0,1:T(2,128)}, u32[]{:S(2)}) copy-start(s32[24,2]{0,1:T(2,128)} %param.7) | copy-start | bytes 580
  101.4 32.7 %all-to-all-start.2 = ((bf16[16,240,128]{2,1,0:T(8,128)(2,1)}), bf16[16,240,128]{2,1,0:T(8,128)(2,1)S(1)}, u32[]{:S(2)}, u32[]{:S(2)}) async-start(bf16[16,240,128]{2,1,0:T(8,128)(2,1)} %reshape.118), calls=%async_computation.2 | async-start | bytes 1966080 | tf_op jit(solution)/shard_map/all_to_all | solution.py:58
  135.1 10.8 %all-to-all-start.3 = ((bf16[16,2,960]{2,1,0:T(2,128)(2,1)}), bf16[16,2,960]{2,1,0:T(2,128)(2,1)S(1)}, u32[]{:S(2)}, u32[]{:S(2)}) async-start(bf16[16,2,960]{2,1,0:T(2,128)(2,1)} %reshape.125), calls=%async_computation.3 | async-start | bytes 131072 | tf_op jit(solution)/shard_map/all_to_all | solution.py:61

commit v2 on v1

--- a/solution.py
+++ b/solution.py
@@ -38,25 +38,19 @@
     arrived = lax.all_to_all(
         jnp.repeat(packed, halves, axis=0), GROUP_AXES, split_axis=0, concat_axis=0, tiled=True
     )
-    lane = 128
-    dense = arrived.reshape(rows * slice_width // lane, lane)
     spread = lax.all_to_all(
-        jnp.broadcast_to(dense[None], (n_loop,) + dense.shape), LOOP_AXES, 0, 0, tiled=True
-    )
-    own = spread.reshape(n_loop, rows, slice_width)
-    other = swap_cores(spread).reshape(n_loop, rows, slice_width)
-    segment = jnp.concatenate([own, other], axis=1)
-    segment = segment.transpose(1, 0, 2).reshape(2 * rows, model_width)
+        jnp.broadcast_to(arrived.reshape(1, rows, slice_width), (n_loop, rows, slice_width)),
+        LOOP_AXES, 0, 2, tiled=True,
+    ).reshape(rows, model_width)
+    segment = jnp.concatenate([spread, swap_cores(spread)], axis=0)
     gate_sum = jnp.dot(segment, gate_weight[0], preferred_element_type=jnp.float32)
     up_sum = jnp.dot(segment, up_weight[0], preferred_element_type=jnp.float32)
     hidden = (jax.nn.silu(gate_sum) * up_sum).astype(jnp.bfloat16)
     partial = jnp.dot(hidden, down_weight[0], preferred_element_type=jnp.float32)
     partner_part = swap_cores(partial[rows:].astype(jnp.bfloat16))
     pair_sum = (partial[:rows] + partner_part.astype(jnp.float32)).astype(jnp.bfloat16)
-    by_slice = pair_sum.reshape(rows, n_loop, slice_width).transpose(1, 0, 2)
-    by_slice = by_slice.reshape(n_loop, rows * slice_width // lane, lane)
-    summed = lax.all_to_all(by_slice, LOOP_AXES, 0, 0, tiled=True)
-    summed = summed.reshape(n_loop, rows, slice_width).astype(jnp.float32).sum(axis=0)
+    summed = lax.all_to_all(pair_sum.reshape(1, rows, model_width), LOOP_AXES, 2, 0, tiled=True)
+    summed = summed.astype(jnp.float32).sum(axis=0)
     expert_out = summed.astype(jnp.bfloat16).reshape(peers, CAP, slice_width)
     returned = lax.all_to_all(expert_out, GROUP_AXES, split_axis=0, concat_axis=0, tiled=True).reshape(
         rows, slice_width

time: 148 us -> 179 us (1.21)
  other arithmetic: 7.33 us -> 21.8 us
  local copies, waits for them, and re-layouts: 22.2 us -> 32.9 us
  blocking collectives: 54.6 us -> 61.6 us
  matrix products: 10.5 us -> 8.65 us
    unnamed x0 -> x1, other arithmetic: none -> 18.1 us
    all_to_all x0 -> x3, local copies, waits for them, and re-layouts: none -> 10.5 us  [the longest x2 9.78 us: body(): lax.all_to_all(pair_sum.reshape(1, rows, model_width), LOOP_AXES, 2, 0, t...]
    unnamed x13 -> x17, local copies, waits for them, and re-layouts: 2.02 us -> 11.5 us
    all_to_all x1, blocking collectives: 37.9 us -> 44.9 us  [body(): lax.all_to_all(jnp.broadcast_to(arrived.reshape(1, rows, slice_width), (n...]
    reshape x5 -> x2, local copies, waits for them, and re-layouts: 13.3 us -> 8.55 us  [the longest x1 6.3 us: body(): pair_sum.reshape(1, rows, model_width)]
    transpose x1 -> x0, local copies, waits for them, and re-layouts: 4.42 us -> none  [body(): segment = segment.transpose(1, 0, 2).reshape(2 * rows, model_width)]
    transpose x1 -> x0, other arithmetic: 3.29 us -> none  [body(): segment = segment.transpose(1, 0, 2).reshape(2 * rows, model_width)]
    convert_element_type x1 -> x0, other arithmetic: 2.77 us -> none  [body(): (partial[:rows] + partner_part.astype(jnp.float32)).astype(jnp.bfloat16)]
  transfers between devices with their start and end apart: 4 -> 4, of which waited for: 3 -> 4; matrix products, arithmetic and copies ran while one was open for 2% -> 1% of each run, Pallas kernels for 0% -> 0%
where the time goes in v2:
time: 179 us; the launch traced here: 178 us
  blocking collectives  61.6 us (34%)
  waiting for transfers between devices  38.7 us (22%)
  local copies, waits for them, and re-layouts  32.9 us (18%)
  other arithmetic  21.8 us (12%)
  starting transfers between devices  14.3 us (8%)
  matrix products  8.65 us (5%)
    all_to_all x1, blocking collectives, body(): lax.all_to_all(jnp.broadcast_to(arrived.reshape(1, rows, slice_width), (n...  44.9 us
    all_to_all x1, waiting for transfers between devices, body(): lax.all_to_all(pair_sum.reshape(1, rows, model_width), LOOP_AXES, 2, 0, t...  28.2 us
    unnamed x1, other arithmetic  18.1 us
    all_to_all x1, blocking collectives, body(): lax.all_to_all(jnp.repeat(packed, halves, axis=0), GROUP_AXES, split_axis...  16.7 us
    unnamed x17, local copies, waits for them, and re-layouts  11.5 us
    all_to_all x2, local copies, waits for them, and re-layouts, body(): lax.all_to_all(pair_sum.reshape(1, rows, model_width), LOOP_AXES, 2, 0, t...  9.78 us
    all_to_all x1, waiting for transfers between devices, body(): lax.all_to_all(expert_out, GROUP_AXES, split_axis=0, concat_axis=0, tiled...  7.3 us
    ppermute x2, starting transfers between devices, swap_cores(): return lax.ppermute(x, 'c', [(0, 1), (1, 0)])  6.71 us
  transfers between devices with their start and end apart: 4, of which 4 were waited for; matrix products, arithmetic and copies ran while one was open for 1% of the time, Pallas kernels for 0%

profile of v2, /device:TPU:1, one launch (start us, length us, event | category | flops | bytes accessed | tf_op | source)
XLA Modules:
  0.0 178.2 jit_solution(15132466046945493250)
XLA Ops:
  0.0 0.0 copy-start
  0.0 0.9 copy.36
  0.9 0.1 eq.73
  1.0 0.1 fusion.18
  1.1 0.1 reduce_window_sum.11
  1.1 0.2 select_reduce_fusion
  1.3 0.1 eq.77
  1.4 0.1 copy.37
  1.5 0.7 multiply_add_fusion
  2.2 0.1 fusion.23
  2.3 0.9 convolution_convert_fusion
  3.2 0.1 reshape.111
  3.3 16.7 %all_to_all.37 = bf16[16,2,960]{2,1,0:T(2,128)(2,1)S(1)} all-to-all(bf16[16,2,960]{2,1,0:T(2,128)(2,1)S(1)} %reshape.111), channel_id=1, replica_groups=mesh['zl'=2,'yh'=4,'yl'=2,'c'=2,'zh'=4,'x'=4] {'zl','yh','yl'}, dimensions={0} | all-to-all | bytes 122880 | tf_op jit(solution)/shard_map/all_to_all | solution.py:38
  20.1 0.1 reshape.112
  20.2 0.1 broadcast_in_dim.7
  20.3 0.1 broadcast_in_dim.8
  20.4 44.9 %all_to_all.38 = bf16[16,160,192]{2,1,0:T(8,128)(2,1)S(1)} all-to-all(bf16[16,160,192]{2,1,0:T(8,128)(2,1)S(1)} %broadcast_in_dim.8), channel_id=1, replica_groups=mesh['zl'=2,'yh'=4,'yl'=2,'c'=2,'zh'=4,'x'=4] {'zh','x'}, dimensions={0} | all-to-all | bytes 1966080 | tf_op jit(solution)/shard_map/all_to_all | solution.py:41
  65.3 0.7 copy.39
  66.0 2.2 %reshape.105 = bf16[160,3072]{1,0:T(8,128)(2,1)} reshape(bf16[1,160,16,192]{3,2,1,0:T(8,128)(2,1)S(1)} %copy.39) | data formatting | bytes 1966080 | tf_op jit(solution)/shard_map/reshape | solution.py:44
  68.3 4.4 %collective-permute-start = (bf16[160,3072]{1,0:T(8,128)(2,1)}, bf16[160,3072]{1,0:T(8,128)(2,1)S(1)}, u32[]{:S(2)}, u32[]{:S(2)}) collective-permute-start(bf16[160,3072]{1,0:T(8,128)(2,1)} %reshape.105), channel_id=1, source_target_pairs={{0,16},{16,0},{1,17},{17,1},{2,18},{18,2},{3,19},{19,3},{4,20},{20... | collective-permute-start | bytes 2949128 | tf_op jit(solution)/shard_map/ppermute | solution.py:21
  72.7 1.3 constant_dynamic-update-slice_fusion.1
  74.0 1.1 collective-permute-done
  75.1 0.1 constant_dynamic-update-slice_fusion
  75.2 0.0 copy-done.3
  75.2 1.4 fusion.3
  76.6 5.6 %fusion.1 = f32[320,3072]{1,0:T(8,128)} fusion(bf16[1,256,3072]{2,1,0:T(8,128)(2,1)S(1)} %copy-done, f32[320,256]{1,0:T(8,128)} %fusion.3, bf16[320,3072]{1,0:T(8,128)(2,1)S(1)} %constant_dynamic-update-slice_fusion, bf16[1,3072,256]{2,1,0:T(8,128)(2,1)} %param.9), kind=kOutput, calls=%fused_computation.3 | convolution fusion | flops 1007124480 | bytes 9371648 | tf_op jit(solution)/shard_map/dot_general | solution.py:49
  82.1 1.7 slice.17
  83.8 2.3 %collective-permute-start.1 = (bf16[160,3072]{1,0:T(8,128)(2,1)S(1)}, bf16[160,3072]{1,0:T(8,128)(2,1)S(1)}, u32[]{:S(2)}, u32[]{:S(2)}) collective-permute-start(bf16[160,3072]{1,0:T(8,128)(2,1)S(1)} %slice.17), channel_id=1, source_target_pairs={{0,16},{16,0},{1,17},{17,1},{2,18},{18,2},{3,19},{19,3},{4,20},{20... | collective-permute-start | bytes 2949128 | tf_op jit(solution)/shard_map/ppermute | solution.py:21
  86.1 2.2 %collective-permute-done.1 = bf16[160,3072]{1,0:T(8,128)(2,1)S(1)} collective-permute-done((bf16[160,3072]{1,0:T(8,128)(2,1)S(1)}, bf16[160,3072]{1,0:T(8,128)(2,1)S(1)}, u32[]{:S(2)}, u32[]{:S(2)}) %collective-permute-start.1) | collective-permute-done | bytes 983072 | tf_op jit(solution)/shard_map/ppermute | solution.py:21
  88.3 1.8 %fusion.8 = bf16[1,160,3072]{2,1,0:T(8,128)(2,1)S(1)} fusion(bf16[160,3072]{1,0:T(8,128)(2,1)S(1)} %collective-permute-done.1, f32[320,3072]{1,0:T(8,128)} %fusion.1), kind=kLoop, calls=%fused_computation.12 | loop fusion | flops 1474560 | bytes 3932160 | tf_op jit(solution)/shard_map/reshape | solution.py:52
  90.1 6.3 %copy.40 = bf16[1,160,3072]{1,0,2:T(2,128)(2,1)} copy(bf16[1,160,3072]{2,1,0:T(8,128)(2,1)S(1)} %fusion.8) | data formatting | bytes 1966080 | tf_op jit(solution)/shard_map/reshape | solution.py:52
  96.4 0.5 broadcast.117
  96.9 18.1 %reduce.5 = bf16[3072,160]{1,0:T(8,128)(2,1)S(1)} reduce(bf16[3072,1,160]{2,1,0:T(2,128)(2,1)} %bitcast.28, bf16[]{:T(256)} %broadcast.117), dimensions={1}, to_apply=%bitcast.21.reduce_sub_computation | reduce | bytes 1966082
  115.0 0.0 copy-start.1
  115.1 3.2 %reshape.113 = bf16[16,2,15360]{2,1,0:T(2,128)(2,1)} reshape(bf16[3072,160]{1,0:T(8,128)(2,1)S(1)} %reduce.5) | data formatting | bytes 1966080
  118.2 4.1 %all-to-all-start.2 = ((bf16[16,2,15360]{2,1,0:T(2,128)(2,1)}), bf16[16,2,15360]{2,1,0:T(2,128)(2,1)S(1)}, u32[]{:S(2)}, u32[]{:S(2)}) async-start(bf16[16,2,15360]{2,1,0:T(2,128)(2,1)} %reshape.113), calls=%async_computation.2 | async-start | bytes 1966080 | tf_op jit(solution)/shard_map/all_to_all | solution.py:52
  122.3 0.0 copy-done.1
  122.4 28.2 %all-to-all-done.2 = bf16[16,2,15360]{2,1,0:T(2,128)(2,1)S(1)} async-done(((bf16[16,2,15360]{2,1,0:T(2,128)(2,1)}), bf16[16,2,15360]{2,1,0:T(2,128)(2,1)S(1)}, u32[]{:S(2)}, u32[]{:S(2)}) %all-to-all-start.2) | async-done | bytes 983072 | tf_op jit(solution)/shard_map/all_to_all | solution.py:52
  150.5 4.6 %reshape.114 = bf16[3072,1,160]{2,1,0:T(2,128)(2,1)} reshape(bf16[16,2,15360]{2,1,0:T(2,128)(2,1)S(1)} %all-to-all-done.2) | data formatting | bytes 1966080
  155.1 7.2 %copy.41 = bf16[1,160,3072]{2,1,0:T(8,128)(2,1)} copy(bf16[1,160,3072]{1,0,2:T(2,128)(2,1)} %bitcast.29) | data formatting | bytes 1966080 | tf_op jit(solution)/shard_map/all_to_all | solution.py:52
  162.3 2.6 %all_to_all.31 = bf16[160,16,192]{2,1,0:T(8,128)(2,1)S(1)} reshape(bf16[1,160,3072]{2,1,0:T(8,128)(2,1)} %copy.41) | data formatting | bytes 1966080 | tf_op jit(solution)/shard_map/all_to_all | solution.py:52
  164.9 0.7 reduce_sum.44
  165.6 0.7 reshape.115
  166.3 3.5 %all-to-all-start.3 = ((bf16[16,2,960]{2,1,0:T(2,128)(2,1)}), bf16[16,2,960]{2,1,0:T(2,128)(2,1)S(1)}, u32[]{:S(2)}, u32[]{:S(2)}) async-start(bf16[16,2,960]{2,1,0:T(2,128)(2,1)} %reshape.115), calls=%async_computation.3 | async-start | bytes 131072 | tf_op jit(solution)/shard_map/all_to_all | solution.py:55
  169.9 7.3 %all-to-all-done.3 = bf16[16,2,960]{2,1,0:T(2,128)(2,1)S(1)} async-done(((bf16[16,2,960]{2,1,0:T(2,128)(2,1)}), bf16[16,2,960]{2,1,0:T(2,128)(2,1)S(1)}, u32[]{:S(2)}, u32[]{:S(2)}) %all-to-all-start.3) | async-done | bytes 61472 | tf_op jit(solution)/shard_map/all_to_all | solution.py:55
  177.2 0.1 reshape.116
  177.3 0.1 reshape.109
  177.4 0.8 fusion.7
  (10 shorter events, 0.1 us)
Async XLA Ops:
  0.0 76.6 %copy-start = (bf16[1,256,3072]{2,1,0:T(8,128)(2,1)S(1)}, bf16[1,256,3072]{2,1,0:T(8,128)(2,1)}, u32[]{:S(2)}) copy-start(bf16[1,256,3072]{2,1,0:T(8,128)(2,1)} %param.11) | copy-start | bytes 4718596
  68.3 6.9 %copy-start.3 = (bf16[1,3072,256]{2,1,0:T(8,128)(2,1)S(1)}, bf16[1,3072,256]{2,1,0:T(8,128)(2,1)}, u32[]{:S(2)}) copy-start(bf16[1,3072,256]{2,1,0:T(8,128)(2,1)} %param.10) | copy-start | bytes 4718596
  68.3 6.8 %collective-permute-start = (bf16[160,3072]{1,0:T(8,128)(2,1)}, bf16[160,3072]{1,0:T(8,128)(2,1)S(1)}, u32[]{:S(2)}, u32[]{:S(2)}) collective-permute-start(bf16[160,3072]{1,0:T(8,128)(2,1)} %reshape.105), channel_id=1, source_target_pairs={{0,16},{16,0},{1,17},{17,1},{2,18},{18,2},{3,19},{19,3},{4,20},{20... | collective-permute-start | bytes 2949128 | tf_op jit(solution)/shard_map/ppermute | solution.py:21
  83.8 4.5 %collective-permute-start.1 = (bf16[160,3072]{1,0:T(8,128)(2,1)S(1)}, bf16[160,3072]{1,0:T(8,128)(2,1)S(1)}, u32[]{:S(2)}, u32[]{:S(2)}) collective-permute-start(bf16[160,3072]{1,0:T(8,128)(2,1)S(1)} %slice.17), channel_id=1, source_target_pairs={{0,16},{16,0},{1,17},{17,1},{2,18},{18,2},{3,19},{19,3},{4,20},{20... | collective-permute-start | bytes 2949128 | tf_op jit(solution)/shard_map/ppermute | solution.py:21
  115.0 7.3 %copy-start.1 = (f32[24,2]{0,1:T(2,128)S(1)}, f32[24,2]{0,1:T(2,128)}, u32[]{:S(2)}) copy-start(f32[24,2]{0,1:T(2,128)} %param.8) | copy-start | bytes 580
  118.2 32.3 %all-to-all-start.2 = ((bf16[16,2,15360]{2,1,0:T(2,128)(2,1)}), bf16[16,2,15360]{2,1,0:T(2,128)(2,1)S(1)}, u32[]{:S(2)}, u32[]{:S(2)}) async-start(bf16[16,2,15360]{2,1,0:T(2,128)(2,1)} %reshape.113), calls=%async_computation.2 | async-start | bytes 1966080 | tf_op jit(solution)/shard_map/all_to_all | solution.py:52
  162.3 15.1 %copy-start.2 = (s32[24,2]{0,1:T(2,128)S(1)}, s32[24,2]{0,1:T(2,128)}, u32[]{:S(2)}) copy-start(s32[24,2]{0,1:T(2,128)} %param.7) | copy-start | bytes 580
  166.3 10.8 %all-to-all-start.3 = ((bf16[16,2,960]{2,1,0:T(2,128)(2,1)}), bf16[16,2,960]{2,1,0:T(2,128)(2,1)S(1)}, u32[]{:S(2)}, u32[]{:S(2)}) async-start(bf16[16,2,960]{2,1,0:T(2,128)(2,1)} %reshape.115), calls=%async_computation.3 | async-start | bytes 131072 | tf_op jit(solution)/shard_map/all_to_all | solution.py:55

commit v3 on v1

--- a/solution.py
+++ b/solution.py
@@ -43,20 +43,20 @@
     spread = lax.all_to_all(
         jnp.broadcast_to(dense[None], (n_loop,) + dense.shape), LOOP_AXES, 0, 0, tiled=True
     )
-    own = spread.reshape(n_loop, rows, slice_width)
-    other = swap_cores(spread).reshape(n_loop, rows, slice_width)
-    segment = jnp.concatenate([own, other], axis=1)
+    other = swap_cores(spread)
+    segment = jnp.concatenate([spread, other], axis=1).reshape(n_loop, 2 * rows, slice_width)
     segment = segment.transpose(1, 0, 2).reshape(2 * rows, model_width)
     gate_sum = jnp.dot(segment, gate_weight[0], preferred_element_type=jnp.float32)
     up_sum = jnp.dot(segment, up_weight[0], preferred_element_type=jnp.float32)
     hidden = (jax.nn.silu(gate_sum) * up_sum).astype(jnp.bfloat16)
-    partial = jnp.dot(hidden, down_weight[0], preferred_element_type=jnp.float32)
-    partner_part = swap_cores(partial[rows:].astype(jnp.bfloat16))
-    pair_sum = (partial[:rows] + partner_part.astype(jnp.float32)).astype(jnp.bfloat16)
-    by_slice = pair_sum.reshape(rows, n_loop, slice_width).transpose(1, 0, 2)
-    by_slice = by_slice.reshape(n_loop, rows * slice_width // lane, lane)
+    down_t = (((0,), (1,)), ((), ()))
+    own_t = lax.dot_general(down_weight[0], hidden[:rows], down_t, preferred_element_type=jnp.float32)
+    other_t = lax.dot_general(down_weight[0], hidden[rows:], down_t, preferred_element_type=jnp.float32)
+    partner_t = swap_cores(other_t.astype(jnp.bfloat16))
+    pair_t = (own_t + partner_t.astype(jnp.float32)).astype(jnp.bfloat16)
+    by_slice = pair_t.reshape(n_loop, slice_width * rows // lane, lane)
     summed = lax.all_to_all(by_slice, LOOP_AXES, 0, 0, tiled=True)
-    summed = summed.reshape(n_loop, rows, slice_width).astype(jnp.float32).sum(axis=0)
+    summed = summed.astype(jnp.float32).sum(axis=0).reshape(slice_width, rows).T
     expert_out = summed.astype(jnp.bfloat16).reshape(peers, CAP, slice_width)
     returned = lax.all_to_all(expert_out, GROUP_AXES, split_axis=0, concat_axis=0, tiled=True).reshape(
         rows, slice_width

time: 148 us -> 133 us (0.90)
  local copies, waits for them, and re-layouts: 22.2 us -> 15.6 us
  other arithmetic: 7.33 us -> 1.39 us
  matrix products: 10.5 us -> 7.06 us
  waiting for transfers between devices: 37.7 us -> 39.8 us
    reshape x5 -> x2, local copies, waits for them, and re-layouts: 13.3 us -> 6.28 us  [the longest x1 3.39 us: body(): by_slice = pair_t.reshape(n_loop, slice_width * rows // lane, lane)]
    transpose x1 -> x0, other arithmetic: 3.29 us -> none  [body(): segment = segment.transpose(1, 0, 2).reshape(2 * rows, model_width)]
    dot_general x1 -> x3, matrix products: 5.78 us -> 2.75 us  [the longest x1 1.39 us: body(): lax.dot_general(down_weight[0], hidden[:rows], down_t, preferred_element_...]
    convert_element_type x1 -> x0, other arithmetic: 2.77 us -> none  [body(): (partial[:rows] + partner_part.astype(jnp.float32)).astype(jnp.bfloat16)]
    ppermute x2, waiting for transfers between devices: 2.22 us -> 4.35 us  [swap_cores(): return lax.ppermute(x, 'c', [(0, 1), (1, 0)])]
    convert_element_type x0 -> x3, local copies, waits for them, and re-layouts: none -> 1.84 us  [the longest x1 1.6 us: body(): pair_t = (own_t + partner_t.astype(jnp.float32)).astype(jnp.bfloat16)]
    slice x1 -> x0, local copies, waits for them, and re-layouts: 1.66 us -> none  [body(): partner_part = swap_cores(partial[rows:].astype(jnp.bfloat16))]
  transfers between devices with their start and end apart: 4 -> 4, of which waited for: 3 -> 4; matrix products, arithmetic and copies ran while one was open for 2% -> 0% of each run, Pallas kernels for 0% -> 0%
where the time goes in v3:
time: 133 us
  blocking collectives  54.5 us (41%)
  waiting for transfers between devices  39.8 us (30%)
  local copies, waits for them, and re-layouts  15.6 us (12%)
  starting transfers between devices  14.4 us (11%)
  matrix products  7.06 us (5%)
  other arithmetic  1.39 us (1%)
    all_to_all x1, blocking collectives, body(): lax.all_to_all(jnp.broadcast_to(dense[None], (n_loop,) + dense.shape), LO...  37.8 us
    all_to_all x1, waiting for transfers between devices, body(): summed = lax.all_to_all(by_slice, LOOP_AXES, 0, 0, tiled=True)  28.2 us
    all_to_all x1, blocking collectives, body(): lax.all_to_all(jnp.repeat(packed, halves, axis=0), GROUP_AXES, split_axis...  16.7 us
    all_to_all x1, waiting for transfers between devices, body(): lax.all_to_all(expert_out, GROUP_AXES, split_axis=0, concat_axis=0, tiled...  7.3 us
    ppermute x2, starting transfers between devices, swap_cores(): return lax.ppermute(x, 'c', [(0, 1), (1, 0)])  6.41 us
    transpose x1, local copies, waits for them, and re-layouts, body(): segment = segment.transpose(1, 0, 2).reshape(2 * rows, model_width)  4.54 us
    all_to_all x1, starting transfers between devices, body(): summed = lax.all_to_all(by_slice, LOOP_AXES, 0, 0, tiled=True)  4.48 us
    ppermute x2, waiting for transfers between devices, swap_cores(): return lax.ppermute(x, 'c', [(0, 1), (1, 0)])  4.35 us
  transfers between devices with their start and end apart: 4, of which 4 were waited for; matrix products, arithmetic and copies ran while one was open for 0% of the time, Pallas kernels for 0%

profile of v3, /device:TPU:1, one launch (start us, length us, event | category | flops | bytes accessed | tf_op | source)
XLA Modules:
  0.0 132.9 jit_solution(14057438813653653842)
XLA Ops:
  0.0 0.0 copy-start
  0.0 0.9 copy.26
  0.9 0.1 eq.73
  1.0 0.1 fusion.22
  1.1 0.1 reduce_window_sum.11
  1.1 0.2 select_reduce_fusion
  1.3 0.1 eq.77
  1.4 0.1 copy.27
  1.5 0.7 multiply_add_fusion
  2.2 0.1 fusion.27
  2.3 0.9 convolution_convert_fusion.1
  3.2 0.1 reshape.114
  3.3 16.7 %all_to_all.20 = bf16[16,2,960]{2,1,0:T(2,128)(2,1)S(1)} all-to-all(bf16[16,2,960]{2,1,0:T(2,128)(2,1)S(1)} %reshape.114), channel_id=1, replica_groups=mesh['zl'=2,'yh'=4,'yl'=2,'c'=2,'zh'=4,'x'=4] {'zl','yh','yl'}, dimensions={0} | all-to-all | bytes 122880 | tf_op jit(solution)/shard_map/all_to_all | solution.py:38
  20.1 0.1 reshape.115
  20.2 0.1 broadcast_in_dim.7
  20.3 0.1 broadcast_in_dim.8
  20.5 37.8 %all_to_all.21 = bf16[16,240,128]{2,1,0:T(8,128)(2,1)S(1)} all-to-all(bf16[16,240,128]{2,1,0:T(8,128)(2,1)S(1)} %broadcast_in_dim.8), channel_id=1, replica_groups=mesh['zl'=2,'yh'=4,'yl'=2,'c'=2,'zh'=4,'x'=4] {'zh','x'}, dimensions={0} | all-to-all | bytes 1966080 | tf_op jit(solution)/shard_map/all_to_all | solution.py:43
  58.3 4.1 %collective-permute-start = (bf16[16,240,128]{2,1,0:T(8,128)(2,1)S(1)}, bf16[16,240,128]{2,1,0:T(8,128)(2,1)S(1)}, u32[]{:S(2)}, u32[]{:S(2)}) collective-permute-start(bf16[16,240,128]{2,1,0:T(8,128)(2,1)S(1)} %all_to_all.21), channel_id=1, source_target_pairs={{0,16},{16,0},{1,17},{17,1},{2,18},{18,2},{3,19},{19,3},{4,20},{20... | collective-permute-start | bytes 2949128 | tf_op jit(solution)/shard_map/ppermute | solution.py:21
  62.4 2.2 %collective-permute-done = bf16[16,240,128]{2,1,0:T(8,128)(2,1)S(1)} collective-permute-done((bf16[16,240,128]{2,1,0:T(8,128)(2,1)S(1)}, bf16[16,240,128]{2,1,0:T(8,128)(2,1)S(1)}, u32[]{:S(2)}, u32[]{:S(2)}) %collective-permute-start) | collective-permute-done | bytes 983072 | tf_op jit(solution)/shard_map/ppermute | solution.py:21
  64.6 0.1 pad_maximum_fusion
  64.7 2.9 %reshape.107 = bf16[16,320,192]{2,1,0:T(8,128)(2,1)} reshape(bf16[16,480,128]{2,1,0:T(8,128)(2,1)S(1)} %pad_maximum_fusion) | data formatting | bytes 3932160 | tf_op jit(solution)/shard_map/reshape | solution.py:47
  67.6 4.5 %copy.29 = bf16[320,16,192]{0,2,1:T(8,128)(2,1)} copy(bf16[320,16,192]{2,0,1:T(8,128)(2,1)} %bitcast.32) | data formatting | bytes 3932160 | tf_op jit(solution)/shard_map/transpose | solution.py:48
  72.1 0.0 copy-done.2
  72.1 2.6 %fusion.7 = f32[320,256]{1,0:T(8,128)S(1)} fusion(bf16[320,3072]{0,1:T(8,128)(2,1)} %bitcast.33, bf16[1,3072,256]{2,1,0:T(8,128)(2,1)S(1)} %copy-done.2), kind=kOutput, calls=%fused_computation.9 | convolution fusion | flops 503316480 | bytes 3866624 | tf_op jit(solution)/shard_map/dot_general | solution.py:49
  74.8 0.0 copy-done.1
  74.8 0.2 copy-done.5
  75.0 0.9 fusion.12
  75.9 0.0 copy-done
  75.9 0.4 fusion
  76.4 2.3 %collective-permute-start.1 = (bf16[3072,160]{0,1:T(8,128)(2,1)S(1)}, bf16[3072,160]{0,1:T(8,128)(2,1)S(1)}, u32[]{:S(2)}, u32[]{:S(2)}) collective-permute-start(bf16[3072,160]{0,1:T(8,128)(2,1)S(1)} %fusion), channel_id=1, source_target_pairs={{0,16},{16,0},{1,17},{17,1},{2,18},{18,2},{3,19},{19,3},{4,20},{20... | collective-permute-start | bytes 2949128 | tf_op jit(solution)/shard_map/ppermute | solution.py:21
  78.6 2.2 %collective-permute-done.1 = bf16[3072,160]{0,1:T(8,128)(2,1)S(1)} collective-permute-done((bf16[3072,160]{0,1:T(8,128)(2,1)S(1)}, bf16[3072,160]{0,1:T(8,128)(2,1)S(1)}, u32[]{:S(2)}, u32[]{:S(2)}) %collective-permute-start.1) | collective-permute-done | bytes 983072 | tf_op jit(solution)/shard_map/ppermute | solution.py:21
  80.8 1.4 %add_convert_fusion = bf16[3072,160]{0,1:T(8,128)(2,1)} fusion(bf16[3072,160]{0,1:T(8,128)(2,1)S(1)} %collective-permute-done.1, bf16[1,256,3072]{2,1,0:T(8,128)(2,1)S(1)} %copy-done, bf16[320,256]{1,0:T(8,128)(2,1)S(1)} %fusion.12), kind=kOutput, calls=%fused_computation.4 | convolution fusion | flops 253132800 | bytes 3620864 | tf_op jit(solution)/shard_map/dot_general | solution.py:53
  82.2 1.6 %copy.30 = bf16[3072,160]{1,0:T(8,128)(2,1)S(1)} copy(bf16[3072,160]{0,1:T(8,128)(2,1)} %add_convert_fusion) | data formatting | bytes 1966080 | tf_op jit(solution)/shard_map/convert_element_type | solution.py:56
  83.8 0.0 copy-start.3
  83.8 3.4 %reshape.109 = bf16[16,240,128]{2,1,0:T(8,128)(2,1)} reshape(bf16[3072,160]{1,0:T(8,128)(2,1)S(1)} %copy.30) | data formatting | bytes 1966080 | tf_op jit(solution)/shard_map/reshape | solution.py:57
  87.2 4.5 %all-to-all-start.2 = ((bf16[16,240,128]{2,1,0:T(8,128)(2,1)}), bf16[16,240,128]{2,1,0:T(8,128)(2,1)S(1)}, u32[]{:S(2)}, u32[]{:S(2)}) async-start(bf16[16,240,128]{2,1,0:T(8,128)(2,1)} %reshape.109), calls=%async_computation.2 | async-start | bytes 1966080 | tf_op jit(solution)/shard_map/all_to_all | solution.py:58
  91.7 0.0 copy-done.3
  91.7 28.2 %all-to-all-done.2 = bf16[16,240,128]{2,1,0:T(8,128)(2,1)S(1)} async-done(((bf16[16,240,128]{2,1,0:T(8,128)(2,1)}), bf16[16,240,128]{2,1,0:T(8,128)(2,1)S(1)}, u32[]{:S(2)}, u32[]{:S(2)}) %all-to-all-start.2) | async-done | bytes 983072 | tf_op jit(solution)/shard_map/all_to_all | solution.py:58
  119.9 0.1 reduce_sum.44
  120.0 0.1 convert_element_type.47
  120.2 0.1 copy.31
  120.3 0.7 reshape.116
  121.1 3.5 %all-to-all-start.3 = ((bf16[16,2,960]{2,1,0:T(2,128)(2,1)}), bf16[16,2,960]{2,1,0:T(2,128)(2,1)S(1)}, u32[]{:S(2)}, u32[]{:S(2)}) async-start(bf16[16,2,960]{2,1,0:T(2,128)(2,1)} %reshape.116), calls=%async_computation.3 | async-start | bytes 131072 | tf_op jit(solution)/shard_map/all_to_all | solution.py:61
  124.6 7.3 %all-to-all-done.3 = bf16[16,2,960]{2,1,0:T(2,128)(2,1)S(1)} async-done(((bf16[16,2,960]{2,1,0:T(2,128)(2,1)}), bf16[16,2,960]{2,1,0:T(2,128)(2,1)S(1)}, u32[]{:S(2)}, u32[]{:S(2)}) %all-to-all-start.3) | async-done | bytes 61472 | tf_op jit(solution)/shard_map/all_to_all | solution.py:61
  131.9 0.1 reshape.117
  132.1 0.1 reshape.112
  132.1 0.0 copy-done.4
  132.1 0.8 fusion.15
  (10 shorter events, 0.1 us)
Async XLA Ops:
  0.0 75.9 %copy-start = (bf16[1,256,3072]{2,1,0:T(8,128)(2,1)S(1)}, bf16[1,256,3072]{2,1,0:T(8,128)(2,1)}, u32[]{:S(2)}) copy-start(bf16[1,256,3072]{2,1,0:T(8,128)(2,1)} %param.11) | copy-start | bytes 4718596
  58.3 6.3 %collective-permute-start = (bf16[16,240,128]{2,1,0:T(8,128)(2,1)S(1)}, bf16[16,240,128]{2,1,0:T(8,128)(2,1)S(1)}, u32[]{:S(2)}, u32[]{:S(2)}) collective-permute-start(bf16[16,240,128]{2,1,0:T(8,128)(2,1)S(1)} %all_to_all.21), channel_id=1, source_target_pairs={{0,16},{16,0},{1,17},{17,1},{2,18},{18,2},{3,19},{19,3},{4,20},{20... | collective-permute-start | bytes 2949128 | tf_op jit(solution)/shard_map/ppermute | solution.py:21
  67.6 4.5 %copy-start.2 = (bf16[1,3072,256]{2,1,0:T(8,128)(2,1)S(1)}, bf16[1,3072,256]{2,1,0:T(8,128)(2,1)}, u32[]{:S(2)}) copy-start(bf16[1,3072,256]{2,1,0:T(8,128)(2,1)} %param.9) | copy-start | bytes 4718596
  72.1 2.6 %copy-start.1 = (bf16[320,16,192]{0,2,1:T(8,128)(2,1)S(1)}, bf16[320,16,192]{0,2,1:T(8,128)(2,1)}, u32[]{:S(2)}) copy-start(bf16[320,16,192]{0,2,1:T(8,128)(2,1)} %copy.29) | copy-start | bytes 5898244
  72.1 2.8 %copy-start.5 = (bf16[1,3072,256]{2,1,0:T(8,128)(2,1)S(1)}, bf16[1,3072,256]{2,1,0:T(8,128)(2,1)}, u32[]{:S(2)}) copy-start(bf16[1,3072,256]{2,1,0:T(8,128)(2,1)} %param.10) | copy-start | bytes 4718596
  76.4 4.5 %collective-permute-start.1 = (bf16[3072,160]{0,1:T(8,128)(2,1)S(1)}, bf16[3072,160]{0,1:T(8,128)(2,1)S(1)}, u32[]{:S(2)}, u32[]{:S(2)}) collective-permute-start(bf16[3072,160]{0,1:T(8,128)(2,1)S(1)} %fusion), channel_id=1, source_target_pairs={{0,16},{16,0},{1,17},{17,1},{2,18},{18,2},{3,19},{19,3},{4,20},{20... | collective-permute-start | bytes 2949128 | tf_op jit(solution)/shard_map/ppermute | solution.py:21
  83.8 7.9 %copy-start.3 = (f32[24,2]{0,1:T(2,128)S(1)}, f32[24,2]{0,1:T(2,128)}, u32[]{:S(2)}) copy-start(f32[24,2]{0,1:T(2,128)} %param.8) | copy-start | bytes 580
  87.2 44.9 %copy-start.4 = (s32[24,2]{0,1:T(2,128)S(1)}, s32[24,2]{0,1:T(2,128)}, u32[]{:S(2)}) copy-start(s32[24,2]{0,1:T(2,128)} %param.7) | copy-start | bytes 580
  87.2 32.7 %all-to-all-start.2 = ((bf16[16,240,128]{2,1,0:T(8,128)(2,1)}), bf16[16,240,128]{2,1,0:T(8,128)(2,1)S(1)}, u32[]{:S(2)}, u32[]{:S(2)}) async-start(bf16[16,240,128]{2,1,0:T(8,128)(2,1)} %reshape.109), calls=%async_computation.2 | async-start | bytes 1966080 | tf_op jit(solution)/shard_map/all_to_all | solution.py:58
  121.1 10.8 %all-to-all-start.3 = ((bf16[16,2,960]{2,1,0:T(2,128)(2,1)}), bf16[16,2,960]{2,1,0:T(2,128)(2,1)S(1)}, u32[]{:S(2)}, u32[]{:S(2)}) async-start(bf16[16,2,960]{2,1,0:T(2,128)(2,1)} %reshape.116), calls=%async_computation.3 | async-start | bytes 131072 | tf_op jit(solution)/shard_map/all_to_all | solution.py:61

commit v4 on v3

--- a/solution.py
+++ b/solution.py
@@ -45,9 +45,13 @@
     )
     other = swap_cores(spread)
     segment = jnp.concatenate([spread, other], axis=1).reshape(n_loop, 2 * rows, slice_width)
-    segment = segment.transpose(1, 0, 2).reshape(2 * rows, model_width)
-    gate_sum = jnp.dot(segment, gate_weight[0], preferred_element_type=jnp.float32)
-    up_sum = jnp.dot(segment, up_weight[0], preferred_element_type=jnp.float32)
+    by_block = (n_loop, slice_width, hidden_width)
+    gate_sum = jnp.einsum(
+        "lrf,lfh->rh", segment, gate_weight[0].reshape(by_block), preferred_element_type=jnp.float32
+    )
+    up_sum = jnp.einsum(
+        "lrf,lfh->rh", segment, up_weight[0].reshape(by_block), preferred_element_type=jnp.float32
+    )
     hidden = (jax.nn.silu(gate_sum) * up_sum).astype(jnp.bfloat16)
     down_t = (((0,), (1,)), ((), ()))
     own_t = lax.dot_general(down_weight[0], hidden[:rows], down_t, preferred_element_type=jnp.float32)

time: 133 us -> 129 us (0.970)
  local copies, waits for them, and re-layouts: 15.6 us -> 11.2 us
    transpose x1 -> x0, local copies, waits for them, and re-layouts: 4.54 us -> none  [body(): segment = segment.transpose(1, 0, 2).reshape(2 * rows, model_width)]
where the time goes in v4:
time: 129 us
  blocking collectives  54.5 us (42%)
  waiting for transfers between devices  39.8 us (31%)
  starting transfers between devices  14.4 us (11%)
  local copies, waits for them, and re-layouts  11.2 us (9%)
  matrix products  7.31 us (6%)
  other arithmetic  1.39 us (1%)
    all_to_all x1, blocking collectives, body(): lax.all_to_all(jnp.broadcast_to(dense[None], (n_loop,) + dense.shape), LO...  37.8 us
    all_to_all x1, waiting for transfers between devices, body(): summed = lax.all_to_all(by_slice, LOOP_AXES, 0, 0, tiled=True)  28.2 us
    all_to_all x1, blocking collectives, body(): lax.all_to_all(jnp.repeat(packed, halves, axis=0), GROUP_AXES, split_axis...  16.7 us
    all_to_all x1, waiting for transfers between devices, body(): lax.all_to_all(expert_out, GROUP_AXES, split_axis=0, concat_axis=0, tiled...  7.3 us
    ppermute x2, starting transfers between devices, swap_cores(): return lax.ppermute(x, 'c', [(0, 1), (1, 0)])  6.41 us
    all_to_all x1, starting transfers between devices, body(): summed = lax.all_to_all(by_slice, LOOP_AXES, 0, 0, tiled=True)  4.48 us
    ppermute x2, waiting for transfers between devices, swap_cores(): return lax.ppermute(x, 'c', [(0, 1), (1, 0)])  4.34 us
    all_to_all x1, starting transfers between devices, body(): lax.all_to_all(expert_out, GROUP_AXES, split_axis=0, concat_axis=0, tiled...  3.5 us
  transfers between devices with their start and end apart: 4, of which 4 were waited for; matrix products, arithmetic and copies ran while one was open for 0% of the time, Pallas kernels for 0%

profile of v4, /device:TPU:1, one launch (start us, length us, event | category | flops | bytes accessed | tf_op | source)
XLA Modules:
  0.0 128.9 jit_solution(16164182906708016455)
XLA Ops:
  0.0 0.0 copy-start
  0.0 0.9 copy.28
  0.9 0.1 eq.73
  1.0 0.1 fusion.12
  1.1 0.1 reduce_window_sum.11
  1.1 0.2 select_reduce_fusion
  1.3 0.1 eq.77
  1.4 0.1 copy.29
  1.5 0.7 multiply_add_fusion
  2.2 0.1 fusion.17
  2.3 0.9 convolution_convert_fusion.1
  3.2 0.1 reshape.112
  3.3 16.7 %all_to_all.20 = bf16[16,2,960]{2,1,0:T(2,128)(2,1)S(1)} all-to-all(bf16[16,2,960]{2,1,0:T(2,128)(2,1)S(1)} %reshape.112), channel_id=1, replica_groups=mesh['zl'=2,'yh'=4,'yl'=2,'c'=2,'zh'=4,'x'=4] {'zl','yh','yl'}, dimensions={0} | all-to-all | bytes 122880 | tf_op jit(solution)/shard_map/all_to_all | solution.py:38
  20.1 0.1 reshape.113
  20.2 0.1 broadcast_in_dim.7
  20.3 0.1 broadcast_in_dim.8
  20.5 37.8 %all_to_all.21 = bf16[16,240,128]{2,1,0:T(8,128)(2,1)S(1)} all-to-all(bf16[16,240,128]{2,1,0:T(8,128)(2,1)S(1)} %broadcast_in_dim.8), channel_id=1, replica_groups=mesh['zl'=2,'yh'=4,'yl'=2,'c'=2,'zh'=4,'x'=4] {'zh','x'}, dimensions={0} | all-to-all | bytes 1966080 | tf_op jit(solution)/shard_map/all_to_all | solution.py:43
  58.3 4.1 %collective-permute-start = (bf16[16,240,128]{2,1,0:T(8,128)(2,1)S(1)}, bf16[16,240,128]{2,1,0:T(8,128)(2,1)S(1)}, u32[]{:S(2)}, u32[]{:S(2)}) collective-permute-start(bf16[16,240,128]{2,1,0:T(8,128)(2,1)S(1)} %all_to_all.21), channel_id=1, source_target_pairs={{0,16},{16,0},{1,17},{17,1},{2,18},{18,2},{3,19},{19,3},{4,20},{20... | collective-permute-start | bytes 2949128 | tf_op jit(solution)/shard_map/ppermute | solution.py:21
  62.4 2.2 %collective-permute-done = bf16[16,240,128]{2,1,0:T(8,128)(2,1)S(1)} collective-permute-done((bf16[16,240,128]{2,1,0:T(8,128)(2,1)S(1)}, bf16[16,240,128]{2,1,0:T(8,128)(2,1)S(1)}, u32[]{:S(2)}, u32[]{:S(2)}) %collective-permute-start) | collective-permute-done | bytes 983072 | tf_op jit(solution)/shard_map/ppermute | solution.py:21
  64.6 0.1 pad_maximum_fusion
  64.7 2.9 %reshape.104 = bf16[16,320,192]{2,1,0:T(8,128)(2,1)} reshape(bf16[16,480,128]{2,1,0:T(8,128)(2,1)S(1)} %pad_maximum_fusion) | data formatting | bytes 3932160 | tf_op jit(solution)/shard_map/reshape | solution.py:47
  67.6 0.0 copy-start.1
  67.6 0.0 copy-start.4
  67.6 3.1 %convolution_bitcast_fusion.2 = f32[320,256]{1,0:T(8,128)S(1)} fusion(bf16[16,320,192]{2,1,0:T(8,128)(2,1)} %reshape.104, bf16[16,192,256]{2,1,0:T(8,128)(2,1)} %bitcast.30), kind=kOutput, calls=%fused_computation.8 | convolution fusion | flops 503316480 | bytes 3866624 | tf_op jit(solution)/shard_map/lrf,lfh->rh/dot_general | solution.py:49
  70.7 0.0 copy-done.1
  70.7 0.4 copy-done.4
  71.1 0.7 multiply_convert_fusion
  71.8 0.0 copy-done
  71.8 0.4 fusion
  72.3 2.3 %collective-permute-start.1 = (bf16[3072,160]{0,1:T(8,128)(2,1)S(1)}, bf16[3072,160]{0,1:T(8,128)(2,1)S(1)}, u32[]{:S(2)}, u32[]{:S(2)}) collective-permute-start(bf16[3072,160]{0,1:T(8,128)(2,1)S(1)} %fusion), channel_id=1, source_target_pairs={{0,16},{16,0},{1,17},{17,1},{2,18},{18,2},{3,19},{19,3},{4,20},{20... | collective-permute-start | bytes 2949128 | tf_op jit(solution)/shard_map/ppermute | solution.py:21
  74.5 2.2 %collective-permute-done.1 = bf16[3072,160]{0,1:T(8,128)(2,1)S(1)} collective-permute-done((bf16[3072,160]{0,1:T(8,128)(2,1)S(1)}, bf16[3072,160]{0,1:T(8,128)(2,1)S(1)}, u32[]{:S(2)}, u32[]{:S(2)}) %collective-permute-start.1) | collective-permute-done | bytes 983072 | tf_op jit(solution)/shard_map/ppermute | solution.py:21
  76.7 1.4 %add_convert_fusion = bf16[3072,160]{0,1:T(8,128)(2,1)} fusion(bf16[3072,160]{0,1:T(8,128)(2,1)S(1)} %collective-permute-done.1, bf16[1,256,3072]{2,1,0:T(8,128)(2,1)S(1)} %copy-done, bf16[320,256]{1,0:T(8,128)(2,1)S(1)} %multiply_convert_fusion), kind=kOutput, calls=%fused_computation.4 | convolution fusion | flops 253132800 | bytes 3620864 | tf_op jit(solution)/shard_map/dot_general | solution.py:57
  78.1 1.6 %copy.33 = bf16[3072,160]{1,0:T(8,128)(2,1)S(1)} copy(bf16[3072,160]{0,1:T(8,128)(2,1)} %add_convert_fusion) | data formatting | bytes 1966080 | tf_op jit(solution)/shard_map/convert_element_type | solution.py:60
  79.7 0.0 copy-start.2
  79.7 3.4 %reshape.105 = bf16[16,240,128]{2,1,0:T(8,128)(2,1)} reshape(bf16[3072,160]{1,0:T(8,128)(2,1)S(1)} %copy.33) | data formatting | bytes 1966080 | tf_op jit(solution)/shard_map/reshape | solution.py:61
  83.1 4.5 %all-to-all-start.2 = ((bf16[16,240,128]{2,1,0:T(8,128)(2,1)}), bf16[16,240,128]{2,1,0:T(8,128)(2,1)S(1)}, u32[]{:S(2)}, u32[]{:S(2)}) async-start(bf16[16,240,128]{2,1,0:T(8,128)(2,1)} %reshape.105), calls=%async_computation.2 | async-start | bytes 1966080 | tf_op jit(solution)/shard_map/all_to_all | solution.py:62
  87.6 0.0 copy-done.2
  87.7 28.2 %all-to-all-done.2 = bf16[16,240,128]{2,1,0:T(8,128)(2,1)S(1)} async-done(((bf16[16,240,128]{2,1,0:T(8,128)(2,1)}), bf16[16,240,128]{2,1,0:T(8,128)(2,1)S(1)}, u32[]{:S(2)}, u32[]{:S(2)}) %all-to-all-start.2) | async-done | bytes 983072 | tf_op jit(solution)/shard_map/all_to_all | solution.py:62
  115.8 0.1 reduce_sum.44
  116.0 0.1 convert_element_type.47
  116.1 0.1 copy.34
  116.3 0.7 reshape.114
  117.0 3.5 %all-to-all-start.3 = ((bf16[16,2,960]{2,1,0:T(2,128)(2,1)}), bf16[16,2,960]{2,1,0:T(2,128)(2,1)S(1)}, u32[]{:S(2)}, u32[]{:S(2)}) async-start(bf16[16,2,960]{2,1,0:T(2,128)(2,1)} %reshape.114), calls=%async_computation.3 | async-start | bytes 131072 | tf_op jit(solution)/shard_map/all_to_all | solution.py:65
  120.6 7.3 %all-to-all-done.3 = bf16[16,2,960]{2,1,0:T(2,128)(2,1)S(1)} async-done(((bf16[16,2,960]{2,1,0:T(2,128)(2,1)}), bf16[16,2,960]{2,1,0:T(2,128)(2,1)S(1)}, u32[]{:S(2)}, u32[]{:S(2)}) %all-to-all-start.3) | async-done | bytes 61472 | tf_op jit(solution)/shard_map/all_to_all | solution.py:65
  127.8 0.1 reshape.115
  128.0 0.1 reshape.110
  128.0 0.0 copy-done.3
  128.0 0.8 fusion.5
  (7 shorter events, 0.1 us)
Async XLA Ops:
  0.0 71.8 %copy-start = (bf16[1,256,3072]{2,1,0:T(8,128)(2,1)S(1)}, bf16[1,256,3072]{2,1,0:T(8,128)(2,1)}, u32[]{:S(2)}) copy-start(bf16[1,256,3072]{2,1,0:T(8,128)(2,1)} %param.11) | copy-start | bytes 4718596
  58.3 6.3 %collective-permute-start = (bf16[16,240,128]{2,1,0:T(8,128)(2,1)S(1)}, bf16[16,240,128]{2,1,0:T(8,128)(2,1)S(1)}, u32[]{:S(2)}, u32[]{:S(2)}) collective-permute-start(bf16[16,240,128]{2,1,0:T(8,128)(2,1)S(1)} %all_to_all.21), channel_id=1, source_target_pairs={{0,16},{16,0},{1,17},{17,1},{2,18},{18,2},{3,19},{19,3},{4,20},{20... | collective-permute-start | bytes 2949128 | tf_op jit(solution)/shard_map/ppermute | solution.py:21
  67.6 3.1 %copy-start.1 = (bf16[16,320,192]{2,1,0:T(8,128)(2,1)S(1)}, bf16[16,320,192]{2,1,0:T(8,128)(2,1)}, u32[]{:S(2)}) copy-start(bf16[16,320,192]{2,1,0:T(8,128)(2,1)} %reshape.104) | copy-start | bytes 5898244
  67.6 3.5 %copy-start.4 = (bf16[1,3072,256]{2,1,0:T(8,128)(2,1)S(1)}, bf16[1,3072,256]{2,1,0:T(8,128)(2,1)}, u32[]{:S(2)}) copy-start(bf16[1,3072,256]{2,1,0:T(8,128)(2,1)} %param.10) | copy-start | bytes 4718596
  72.3 4.5 %collective-permute-start.1 = (bf16[3072,160]{0,1:T(8,128)(2,1)S(1)}, bf16[3072,160]{0,1:T(8,128)(2,1)S(1)}, u32[]{:S(2)}, u32[]{:S(2)}) collective-permute-start(bf16[3072,160]{0,1:T(8,128)(2,1)S(1)} %fusion), channel_id=1, source_target_pairs={{0,16},{16,0},{1,17},{17,1},{2,18},{18,2},{3,19},{19,3},{4,20},{20... | collective-permute-start | bytes 2949128 | tf_op jit(solution)/shard_map/ppermute | solution.py:21
  79.7 7.9 %copy-start.2 = (f32[24,2]{0,1:T(2,128)S(1)}, f32[24,2]{0,1:T(2,128)}, u32[]{:S(2)}) copy-start(f32[24,2]{0,1:T(2,128)} %param.8) | copy-start | bytes 580
  83.1 44.9 %copy-start.3 = (s32[24,2]{0,1:T(2,128)S(1)}, s32[24,2]{0,1:T(2,128)}, u32[]{:S(2)}) copy-start(s32[24,2]{0,1:T(2,128)} %param.7) | copy-start | bytes 580
  83.1 32.7 %all-to-all-start.2 = ((bf16[16,240,128]{2,1,0:T(8,128)(2,1)}), bf16[16,240,128]{2,1,0:T(8,128)(2,1)S(1)}, u32[]{:S(2)}, u32[]{:S(2)}) async-start(bf16[16,240,128]{2,1,0:T(8,128)(2,1)} %reshape.105), calls=%async_computation.2 | async-start | bytes 1966080 | tf_op jit(solution)/shard_map/all_to_all | solution.py:62
  117.0 10.8 %all-to-all-start.3 = ((bf16[16,2,960]{2,1,0:T(2,128)(2,1)}), bf16[16,2,960]{2,1,0:T(2,128)(2,1)S(1)}, u32[]{:S(2)}, u32[]{:S(2)}) async-start(bf16[16,2,960]{2,1,0:T(2,128)(2,1)} %reshape.114), calls=%async_computation.3 | async-start | bytes 131072 | tf_op jit(solution)/shard_map/all_to_all | solution.py:65

commit v5 on v3

--- a/solution.py
+++ b/solution.py
@@ -44,15 +44,20 @@
         jnp.broadcast_to(dense[None], (n_loop,) + dense.shape), LOOP_AXES, 0, 0, tiled=True
     )
     other = swap_cores(spread)
-    segment = jnp.concatenate([spread, other], axis=1).reshape(n_loop, 2 * rows, slice_width)
-    segment = segment.transpose(1, 0, 2).reshape(2 * rows, model_width)
-    gate_sum = jnp.dot(segment, gate_weight[0], preferred_element_type=jnp.float32)
-    up_sum = jnp.dot(segment, up_weight[0], preferred_element_type=jnp.float32)
-    hidden = (jax.nn.silu(gate_sum) * up_sum).astype(jnp.bfloat16)
+    by_block = (n_loop, slice_width, hidden_width)
+    gate_blocks = gate_weight[0].reshape(by_block)
+    up_blocks = up_weight[0].reshape(by_block)
     down_t = (((0,), (1,)), ((), ()))
-    own_t = lax.dot_general(down_weight[0], hidden[:rows], down_t, preferred_element_type=jnp.float32)
-    other_t = lax.dot_general(down_weight[0], hidden[rows:], down_t, preferred_element_type=jnp.float32)
-    partner_t = swap_cores(other_t.astype(jnp.bfloat16))
+
+    def project(gathered):
+        segment = gathered.reshape(n_loop, rows, slice_width)
+        gate_sum = jnp.einsum("lrf,lfh->rh", segment, gate_blocks, preferred_element_type=jnp.float32)
+        up_sum = jnp.einsum("lrf,lfh->rh", segment, up_blocks, preferred_element_type=jnp.float32)
+        hidden = (jax.nn.silu(gate_sum) * up_sum).astype(jnp.bfloat16)
+        return lax.dot_general(down_weight[0], hidden, down_t, preferred_element_type=jnp.float32)
+
+    partner_t = swap_cores(project(other).astype(jnp.bfloat16))
+    own_t = project(spread)
     pair_t = (own_t + partner_t.astype(jnp.float32)).astype(jnp.bfloat16)
     by_slice = pair_t.reshape(n_loop, slice_width * rows // lane, lane)
     summed = lax.all_to_all(by_slice, LOOP_AXES, 0, 0, tiled=True)

time: 133 us -> 134 us (level)
  matrix products: 7.06 us -> 12.1 us
  local copies, waits for them, and re-layouts: 15.6 us -> 12.9 us
  waiting for transfers between devices: 39.8 us -> 37.7 us
    dot_general x4, matrix products: 5.37 us -> 10.4 us  [the longest x2 8.06 us: project(): lax.dot_general(down_weight[0], hidden, down_t, preferred_element_type=jn...]
    transpose x1 -> x0, local copies, waits for them, and re-layouts: 4.54 us -> none  [body(): segment = segment.transpose(1, 0, 2).reshape(2 * rows, model_width)]
    ppermute x2, waiting for transfers between devices: 4.35 us -> 2.3 us  [swap_cores(): return lax.ppermute(x, 'c', [(0, 1), (1, 0)])]
    reshape x1 -> x2, local copies, waits for them, and re-layouts: 2.89 us -> 4.91 us  [project(): segment = gathered.reshape(n_loop, rows, slice_width)]
  transfers between devices with their start and end apart: 4 -> 4, of which waited for: 4 -> 3; matrix products, arithmetic and copies ran while one was open for 0% -> 2% of each run, Pallas kernels for 0% -> 0%
where the time goes in v5:
time: 134 us; the launch traced here: 133 us
  blocking collectives  54.5 us (41%)
  waiting for transfers between devices  37.7 us (28%)
  starting transfers between devices  14.4 us (11%)
  local copies, waits for them, and re-layouts  12.9 us (10%)
  matrix products  12.1 us (9%)
    all_to_all x1, blocking collectives, body(): lax.all_to_all(jnp.broadcast_to(dense[None], (n_loop,) + dense.shape), LO...  37.8 us
    all_to_all x1, waiting for transfers between devices, body(): summed = lax.all_to_all(by_slice, LOOP_AXES, 0, 0, tiled=True)  28.1 us
    all_to_all x1, blocking collectives, body(): lax.all_to_all(jnp.repeat(packed, halves, axis=0), GROUP_AXES, split_axis...  16.7 us
    dot_general x2, matrix products, project(): lax.dot_general(down_weight[0], hidden, down_t, preferred_element_type=jn...  8.06 us
    all_to_all x1, waiting for transfers between devices, body(): lax.all_to_all(expert_out, GROUP_AXES, split_axis=0, concat_axis=0, tiled...  7.3 us
    ppermute x2, starting transfers between devices, swap_cores(): return lax.ppermute(x, 'c', [(0, 1), (1, 0)])  6.4 us
    reshape x2, local copies, waits for them, and re-layouts, project(): segment = gathered.reshape(n_loop, rows, slice_width)  4.91 us
    all_to_all x1, starting transfers between devices, body(): summed = lax.all_to_all(by_slice, LOOP_AXES, 0, 0, tiled=True)  4.48 us
  transfers between devices with their start and end apart: 4, of which 3 were waited for; matrix products, arithmetic and copies ran while one was open for 2% of the time, Pallas kernels for 0%

profile of v5, /device:TPU:1, one launch (start us, length us, event | category | flops | bytes accessed | tf_op | source)
XLA Modules:
  0.0 133.0 jit_solution(12154859314199169760)
XLA Ops:
  0.0 0.0 copy-start
  0.0 0.9 copy.24
  0.9 0.1 eq.73
  1.0 0.1 fusion.19
  1.1 0.1 reduce_window_sum.11
  1.1 0.2 select_reduce_fusion
  1.3 0.1 eq.77
  1.4 0.1 copy.25
  1.5 0.7 multiply_add_fusion
  2.2 0.1 fusion.24
  2.3 0.9 convolution_convert_fusion.1
  3.2 0.1 reshape.118
  3.3 16.7 %all_to_all.20 = bf16[16,2,960]{2,1,0:T(2,128)(2,1)S(1)} all-to-all(bf16[16,2,960]{2,1,0:T(2,128)(2,1)S(1)} %reshape.118), channel_id=1, replica_groups=mesh['zl'=2,'yh'=4,'yl'=2,'c'=2,'zh'=4,'x'=4] {'zl','yh','yl'}, dimensions={0} | all-to-all | bytes 122880 | tf_op jit(solution)/shard_map/all_to_all | solution.py:38
  20.1 0.1 reshape.119
  20.2 0.1 broadcast_in_dim.7
  20.3 0.1 broadcast_in_dim.8
  20.5 37.8 %all_to_all.21 = bf16[16,240,128]{2,1,0:T(8,128)(2,1)S(1)} all-to-all(bf16[16,240,128]{2,1,0:T(8,128)(2,1)S(1)} %broadcast_in_dim.8), channel_id=1, replica_groups=mesh['zl'=2,'yh'=4,'yl'=2,'c'=2,'zh'=4,'x'=4] {'zh','x'}, dimensions={0} | all-to-all | bytes 1966080 | tf_op jit(solution)/shard_map/all_to_all | solution.py:43
  58.3 0.0 copy-start.1
  58.3 4.1 %collective-permute-start = (bf16[16,240,128]{2,1,0:T(8,128)(2,1)S(1)}, bf16[16,240,128]{2,1,0:T(8,128)(2,1)}, u32[]{:S(2)}, u32[]{:S(2)}) collective-permute-start(bf16[16,240,128]{2,1,0:T(8,128)(2,1)S(1)} %all_to_all.21), channel_id=1, source_target_pairs={{0,16},{16,0},{1,17},{17,1},{2,18},{18,2},{3,19},{19,3},{4,20},{20... | collective-permute-start | bytes 2949128 | tf_op jit(solution)/shard_map/ppermute | solution.py:21
  62.4 0.0 copy-done.1
  62.4 2.3 %collective-permute-done = bf16[16,240,128]{2,1,0:T(8,128)(2,1)} collective-permute-done((bf16[16,240,128]{2,1,0:T(8,128)(2,1)S(1)}, bf16[16,240,128]{2,1,0:T(8,128)(2,1)}, u32[]{:S(2)}, u32[]{:S(2)}) %collective-permute-start) | collective-permute-done | bytes 983072 | tf_op jit(solution)/shard_map/ppermute | solution.py:21
  64.7 2.5 %reshape.108 = bf16[16,160,192]{2,1,0:T(8,128)(2,1)S(1)} reshape(bf16[16,240,128]{2,1,0:T(8,128)(2,1)} %collective-permute-done) | data formatting | bytes 1966080 | tf_op jit(solution)/shard_map/reshape | solution.py:53
  67.2 1.9 %convolution_bitcast_fusion.1 = f32[160,256]{1,0:T(8,128)S(1)} fusion(bf16[16,160,192]{2,1,0:T(8,128)(2,1)S(1)} %reshape.108, bf16[16,192,256]{2,1,0:T(8,128)(2,1)} %bitcast.48), kind=kOutput, calls=%fused_computation.6 | convolution fusion | flops 251658240 | bytes 2719744 | tf_op jit(solution)/shard_map/lrf,lfh->rh/dot_general | solution.py:55
  69.0 0.0 copy-done
  69.0 3.7 %fusion = bf16[3072,160]{0,1:T(8,128)(2,1)} fusion(bf16[1,256,3072]{2,1,0:T(8,128)(2,1)} %param.11, f32[160,256]{1,0:T(8,128)S(1)} %convolution_bitcast_fusion.1, bf16[16,160,192]{2,1,0:T(8,128)(2,1)S(1)} %reshape.108, bf16[16,192,256]{2,1,0:T(8,128)(2,1)S(1)} %bitcast.47), kind=kOutput, calls=%fused_computation.2 | convolution fusion | flops 504053760 | bytes 5275648 | tf_op jit(solution)/shard_map/dot_general | solution.py:57
  72.7 2.3 %collective-permute-start.1 = (bf16[3072,160]{0,1:T(8,128)(2,1)}, bf16[3072,160]{0,1:T(8,128)(2,1)}, u32[]{:S(2)}, u32[]{:S(2)}) collective-permute-start(bf16[3072,160]{0,1:T(8,128)(2,1)} %fusion), channel_id=1, source_target_pairs={{0,16},{16,0},{1,17},{17,1},{2,18},{18,2},{3,19},{19,3},{4,20},{20... | collective-permute-start | bytes 2949128 | tf_op jit(solution)/shard_map/ppermute | solution.py:21
  75.0 2.5 %reshape.107 = bf16[16,160,192]{2,1,0:T(8,128)(2,1)S(1)} reshape(bf16[16,240,128]{2,1,0:T(8,128)(2,1)} %copy-done.1) | data formatting | bytes 1966080 | tf_op jit(solution)/shard_map/reshape | solution.py:53
  77.5 0.5 convolution_bitcast_fusion.4
  78.0 0.0 collective-permute-done.1
  78.0 4.4 %add_convert_fusion = bf16[3072,160]{0,1:T(8,128)(2,1)} fusion(bf16[3072,160]{0,1:T(8,128)(2,1)} %collective-permute-done.1, bf16[1,256,3072]{2,1,0:T(8,128)(2,1)} %param.11, bf16[16,160,192]{2,1,0:T(8,128)(2,1)S(1)} %reshape.107, bf16[16,192,256]{2,1,0:T(8,128)(2,1)} %bitcast.49, f32[160,256]{1,0:T(8,128)S(1)} %convolution_bitcast_fusion.4), kind=kOutput, calls=%fused_computation.3 | convolution fusion | flops 505036800 | bytes 6258688 | tf_op jit(solution)/shard_map/dot_general | solution.py:57
  82.3 1.6 %copy.27 = bf16[3072,160]{1,0:T(8,128)(2,1)S(1)} copy(bf16[3072,160]{0,1:T(8,128)(2,1)} %add_convert_fusion) | data formatting | bytes 1966080 | tf_op jit(solution)/shard_map/convert_element_type | solution.py:61
  84.0 3.4 %reshape.109 = bf16[16,240,128]{2,1,0:T(8,128)(2,1)} reshape(bf16[3072,160]{1,0:T(8,128)(2,1)S(1)} %copy.27) | data formatting | bytes 1966080 | tf_op jit(solution)/shard_map/reshape | solution.py:62
  87.3 0.0 copy-start.2
  87.3 4.5 %all-to-all-start.2 = ((bf16[16,240,128]{2,1,0:T(8,128)(2,1)}), bf16[16,240,128]{2,1,0:T(8,128)(2,1)S(1)}, u32[]{:S(2)}, u32[]{:S(2)}) async-start(bf16[16,240,128]{2,1,0:T(8,128)(2,1)} %reshape.109), calls=%async_computation.2 | async-start | bytes 1966080 | tf_op jit(solution)/shard_map/all_to_all | solution.py:63
  91.8 0.0 copy-done.2
  91.8 0.0 copy-start.3
  91.9 28.1 %all-to-all-done.2 = bf16[16,240,128]{2,1,0:T(8,128)(2,1)S(1)} async-done(((bf16[16,240,128]{2,1,0:T(8,128)(2,1)}), bf16[16,240,128]{2,1,0:T(8,128)(2,1)S(1)}, u32[]{:S(2)}, u32[]{:S(2)}) %all-to-all-start.2) | async-done | bytes 983072 | tf_op jit(solution)/shard_map/all_to_all | solution.py:63
  120.0 0.1 reduce_sum.44
  120.2 0.1 convert_element_type.51
  120.3 0.1 copy.28
  120.5 0.7 reshape.120
  121.2 3.5 %all-to-all-start.3 = ((bf16[16,2,960]{2,1,0:T(2,128)(2,1)}), bf16[16,2,960]{2,1,0:T(2,128)(2,1)S(1)}, u32[]{:S(2)}, u32[]{:S(2)}) async-start(bf16[16,2,960]{2,1,0:T(2,128)(2,1)} %reshape.120), calls=%async_computation.3 | async-start | bytes 131072 | tf_op jit(solution)/shard_map/all_to_all | solution.py:66
  124.7 7.3 %all-to-all-done.3 = bf16[16,2,960]{2,1,0:T(2,128)(2,1)S(1)} async-done(((bf16[16,2,960]{2,1,0:T(2,128)(2,1)}), bf16[16,2,960]{2,1,0:T(2,128)(2,1)S(1)}, u32[]{:S(2)}, u32[]{:S(2)}) %all-to-all-start.3) | async-done | bytes 61472 | tf_op jit(solution)/shard_map/all_to_all | solution.py:66
  132.0 0.1 reshape.121
  132.2 0.1 reshape.116
  132.2 0.0 copy-done.3
  132.2 0.8 fusion.7
  (6 shorter events, 0.1 us)
Async XLA Ops:
  0.0 69.0 %copy-start = (bf16[1,3072,256]{2,1,0:T(8,128)(2,1)S(1)}, bf16[1,3072,256]{2,1,0:T(8,128)(2,1)}, u32[]{:S(2)}) copy-start(bf16[1,3072,256]{2,1,0:T(8,128)(2,1)} %param.9) | copy-start | bytes 4718596
  58.3 4.1 %copy-start.1 = (bf16[16,240,128]{2,1,0:T(8,128)(2,1)}, bf16[16,240,128]{2,1,0:T(8,128)(2,1)S(1)}, u32[]{:S(2)}) copy-start(bf16[16,240,128]{2,1,0:T(8,128)(2,1)S(1)} %all_to_all.21) | copy-start | bytes 2949124
  58.3 6.4 %collective-permute-start = (bf16[16,240,128]{2,1,0:T(8,128)(2,1)S(1)}, bf16[16,240,128]{2,1,0:T(8,128)(2,1)}, u32[]{:S(2)}, u32[]{:S(2)}) collective-permute-start(bf16[16,240,128]{2,1,0:T(8,128)(2,1)S(1)} %all_to_all.21), channel_id=1, source_target_pairs={{0,16},{16,0},{1,17},{17,1},{2,18},{18,2},{3,19},{19,3},{4,20},{20... | collective-permute-start | bytes 2949128 | tf_op jit(solution)/shard_map/ppermute | solution.py:21
  72.7 5.2 %collective-permute-start.1 = (bf16[3072,160]{0,1:T(8,128)(2,1)}, bf16[3072,160]{0,1:T(8,128)(2,1)}, u32[]{:S(2)}, u32[]{:S(2)}) collective-permute-start(bf16[3072,160]{0,1:T(8,128)(2,1)} %fusion), channel_id=1, source_target_pairs={{0,16},{16,0},{1,17},{17,1},{2,18},{18,2},{3,19},{19,3},{4,20},{20... | collective-permute-start | bytes 2949128 | tf_op jit(solution)/shard_map/ppermute | solution.py:21
  87.3 4.5 %copy-start.2 = (f32[24,2]{0,1:T(2,128)S(1)}, f32[24,2]{0,1:T(2,128)}, u32[]{:S(2)}) copy-start(f32[24,2]{0,1:T(2,128)} %param.8) | copy-start | bytes 580
  87.3 32.7 %all-to-all-start.2 = ((bf16[16,240,128]{2,1,0:T(8,128)(2,1)}), bf16[16,240,128]{2,1,0:T(8,128)(2,1)S(1)}, u32[]{:S(2)}, u32[]{:S(2)}) async-start(bf16[16,240,128]{2,1,0:T(8,128)(2,1)} %reshape.109), calls=%async_computation.2 | async-start | bytes 1966080 | tf_op jit(solution)/shard_map/all_to_all | solution.py:63
  91.8 40.4 %copy-start.3 = (s32[24,2]{0,1:T(2,128)S(1)}, s32[24,2]{0,1:T(2,128)}, u32[]{:S(2)}) copy-start(s32[24,2]{0,1:T(2,128)} %param.7) | copy-start | bytes 580
  121.2 10.8 %all-to-all-start.3 = ((bf16[16,2,960]{2,1,0:T(2,128)(2,1)}), bf16[16,2,960]{2,1,0:T(2,128)(2,1)S(1)}, u32[]{:S(2)}, u32[]{:S(2)}) async-start(bf16[16,2,960]{2,1,0:T(2,128)(2,1)} %reshape.120), calls=%async_computation.3 | async-start | bytes 131072 | tf_op jit(solution)/shard_map/all_to_all | solution.py:66

commit v6 on v4

--- a/solution.py
+++ b/solution.py
@@ -40,17 +40,21 @@
     )
     lane = 128
     dense = arrived.reshape(rows * slice_width // lane, lane)
+    n_z, n_x = lax.axis_size(LOOP_AXES[0]), lax.axis_size(LOOP_AXES[1])
+    planes = lax.all_to_all(
+        jnp.broadcast_to(dense[None], (n_z,) + dense.shape), LOOP_AXES[0], 0, 0, tiled=True
+    )
     spread = lax.all_to_all(
-        jnp.broadcast_to(dense[None], (n_loop,) + dense.shape), LOOP_AXES, 0, 0, tiled=True
+        jnp.broadcast_to(planes[None], (n_x,) + planes.shape), LOOP_AXES[1], 0, 0, tiled=True
     )
     other = swap_cores(spread)
-    segment = jnp.concatenate([spread, other], axis=1).reshape(n_loop, 2 * rows, slice_width)
-    by_block = (n_loop, slice_width, hidden_width)
+    segment = jnp.concatenate([spread, other], axis=2).reshape(n_x, n_z, 2 * rows, slice_width)
+    by_block = (n_z, n_x, slice_width, hidden_width)
     gate_sum = jnp.einsum(
-        "lrf,lfh->rh", segment, gate_weight[0].reshape(by_block), preferred_element_type=jnp.float32
+        "xzrf,zxfh->rh", segment, gate_weight[0].reshape(by_block), preferred_element_type=jnp.float32
     )
     up_sum = jnp.einsum(
-        "lrf,lfh->rh", segment, up_weight[0].reshape(by_block), preferred_element_type=jnp.float32
+        "xzrf,zxfh->rh", segment, up_weight[0].reshape(by_block), preferred_element_type=jnp.float32
     )
     hidden = (jax.nn.silu(gate_sum) * up_sum).astype(jnp.bfloat16)
     down_t = (((0,), (1,)), ((), ()))

time: 129 us -> 126 us (0.977)
  blocking collectives: 54.5 us -> 48.1 us
  starting transfers between devices: 14.4 us -> 20 us
  waiting for transfers between devices: 39.8 us -> 36.7 us
    all_to_all x1 -> x2, blocking collectives: 37.8 us -> 31.4 us  [the longest x1 17.2 us: body(): lax.all_to_all(jnp.broadcast_to(dense[None], (n_z,) + dense.shape), LOOP_...]
    all_to_all x1, starting transfers between devices: 3.5 us -> 7.05 us  [body(): lax.all_to_all(expert_out, GROUP_AXES, split_axis=0, concat_axis=0, tiled...]
    all_to_all x1, waiting for transfers between devices: 28.2 us -> 25 us  [body(): summed = lax.all_to_all(by_slice, LOOP_AXES, 0, 0, tiled=True)]
    ppermute x2, starting transfers between devices: 6.41 us -> 9.15 us  [swap_cores(): return lax.ppermute(x, 'c', [(0, 1), (1, 0)])]
where the time goes in v6:
time: 126 us; the launch traced here: 125 us
  blocking collectives  48.1 us (38%)
  waiting for transfers between devices  36.7 us (29%)
  starting transfers between devices  20 us (16%)
  local copies, waits for them, and re-layouts  11.3 us (9%)
  matrix products  7.31 us (6%)
  other arithmetic  1.39 us (1%)
    all_to_all x1, waiting for transfers between devices, body(): summed = lax.all_to_all(by_slice, LOOP_AXES, 0, 0, tiled=True)  25 us
    all_to_all x1, blocking collectives, body(): lax.all_to_all(jnp.broadcast_to(dense[None], (n_z,) + dense.shape), LOOP_...  17.2 us
    all_to_all x1, blocking collectives, body(): lax.all_to_all(jnp.repeat(packed, halves, axis=0), GROUP_AXES, split_axis...  16.7 us
    all_to_all x1, blocking collectives, body(): lax.all_to_all(jnp.broadcast_to(planes[None], (n_x,) + planes.shape), LOO...  14.2 us
    ppermute x2, starting transfers between devices, swap_cores(): return lax.ppermute(x, 'c', [(0, 1), (1, 0)])  9.15 us
    all_to_all x1, waiting for transfers between devices, body(): lax.all_to_all(expert_out, GROUP_AXES, split_axis=0, concat_axis=0, tiled...  7.44 us
    all_to_all x1, starting transfers between devices, body(): lax.all_to_all(expert_out, GROUP_AXES, split_axis=0, concat_axis=0, tiled...  7.05 us
    ppermute x2, waiting for transfers between devices, swap_cores(): return lax.ppermute(x, 'c', [(0, 1), (1, 0)])  4.34 us
  transfers between devices with their start and end apart: 4, of which 4 were waited for; matrix products, arithmetic and copies ran while one was open for 0% of the time, Pallas kernels for 0%

profile of v6, /device:TPU:1, one launch (start us, length us, event | category | flops | bytes accessed | tf_op | source)
XLA Modules:
  0.0 125.0 jit_solution(14569808396543429637)
XLA Ops:
  0.0 0.0 copy-start
  0.0 0.9 copy.34
  0.9 0.1 eq.73
  1.0 0.1 fusion.22
  1.1 0.1 reduce_window_sum.11
  1.1 0.2 select_reduce_fusion
  1.3 0.1 eq.77
  1.4 0.1 copy.35
  1.5 0.7 multiply_add_fusion
  2.2 0.1 fusion.27
  2.3 0.9 convolution_convert_fusion.1
  3.2 0.1 reshape.113
  3.3 16.7 %all_to_all.25 = bf16[16,2,960]{2,1,0:T(2,128)(2,1)S(1)} all-to-all(bf16[16,2,960]{2,1,0:T(2,128)(2,1)S(1)} %reshape.113), channel_id=1, replica_groups=mesh['zl'=2,'yh'=4,'yl'=2,'c'=2,'zh'=4,'x'=4] {'zl','yh','yl'}, dimensions={0} | all-to-all | bytes 122880 | tf_op jit(solution)/shard_map/all_to_all | solution.py:38
  20.1 0.1 reshape.114
  20.2 0.1 broadcast_in_dim.9
  20.4 17.2 %all_to_all.26 = bf16[4,240,128]{2,1,0:T(8,128)(2,1)S(1)} all-to-all(bf16[4,240,128]{2,1,0:T(8,128)(2,1)S(1)} %broadcast_in_dim.10), channel_id=1, replica_groups=mesh['zl'=2,'yh'=4,'yl'=2,'c'=2,'zh'=4,'x'=4] {'zh'}, dimensions={0} | all-to-all | bytes 491520 | tf_op jit(solution)/shard_map/all_to_all | solution.py:44
  37.6 0.1 broadcast_in_dim.11
  37.7 14.2 %all_to_all.27 = bf16[4,4,240,128]{3,2,1,0:T(8,128)(2,1)S(1)} all-to-all(bf16[4,4,240,128]{3,2,1,0:T(8,128)(2,1)S(1)} %broadcast_in_dim.11), channel_id=1, replica_groups=mesh['zl'=2,'yh'=4,'yl'=2,'c'=2,'zh'=4,'x'=4] {'x'}, dimensions={0} | all-to-all | bytes 1966080 | tf_op jit(solution)/shard_map/all_to_all | solution.py:47
  51.9 6.9 %collective-permute-start = (bf16[4,4,240,128]{3,2,1,0:T(8,128)(2,1)S(1)}, bf16[4,4,240,128]{3,2,1,0:T(8,128)(2,1)S(1)}, u32[]{:S(2)}, u32[]{:S(2)}) collective-permute-start(bf16[4,4,240,128]{3,2,1,0:T(8,128)(2,1)S(1)} %all_to_all.27), channel_id=1, source_target_pairs={{0,16},{16,0},{1,17},{17,1},{2,18},{18,2},{3,19},{19,3},{4,20},{20... | collective-permute-start | bytes 2949128 | tf_op jit(solution)/shard_map/ppermute | solution.py:21
  58.8 2.2 %collective-permute-done = bf16[4,4,240,128]{3,2,1,0:T(8,128)(2,1)S(1)} collective-permute-done((bf16[4,4,240,128]{3,2,1,0:T(8,128)(2,1)S(1)}, bf16[4,4,240,128]{3,2,1,0:T(8,128)(2,1)S(1)}, u32[]{:S(2)}, u32[]{:S(2)}) %collective-permute-start) | collective-permute-done | bytes 983072 | tf_op jit(solution)/shard_map/ppermute | solution.py:21
  61.0 0.1 pad_maximum_fusion
  61.1 2.9 %reshape.105 = bf16[4,4,320,192]{3,2,1,0:T(8,128)(2,1)} reshape(bf16[4,4,480,128]{3,2,1,0:T(8,128)(2,1)S(1)} %pad_maximum_fusion) | data formatting | bytes 3932160 | tf_op jit(solution)/shard_map/reshape | solution.py:51
  64.0 0.0 copy-start.1
  64.0 3.1 %fusion.9 = f32[320,256]{1,0:T(8,128)S(1)} fusion(bf16[4,4,320,192]{3,2,1,0:T(8,128)(2,1)} %reshape.105, bf16[4,4,192,256]{3,2,1,0:T(8,128)(2,1)} %bitcast.34), kind=kOutput, calls=%fused_computation.11 | convolution fusion | flops 503316480 | bytes 3866624 | tf_op jit(solution)/shard_map/xzrf,zxfh->rh/dot_general | solution.py:53
  67.1 0.0 copy-done.1
  67.1 0.4 copy-done.4
  67.5 0.7 multiply_convert_fusion
  68.2 0.0 copy-done
  68.2 0.4 fusion
  68.7 2.3 %collective-permute-start.1 = (bf16[3072,160]{0,1:T(8,128)(2,1)S(1)}, bf16[3072,160]{0,1:T(8,128)(2,1)S(1)}, u32[]{:S(2)}, u32[]{:S(2)}) collective-permute-start(bf16[3072,160]{0,1:T(8,128)(2,1)S(1)} %fusion), channel_id=1, source_target_pairs={{0,16},{16,0},{1,17},{17,1},{2,18},{18,2},{3,19},{19,3},{4,20},{20... | collective-permute-start | bytes 2949128 | tf_op jit(solution)/shard_map/ppermute | solution.py:21
  71.0 2.2 %collective-permute-done.1 = bf16[3072,160]{0,1:T(8,128)(2,1)S(1)} collective-permute-done((bf16[3072,160]{0,1:T(8,128)(2,1)S(1)}, bf16[3072,160]{0,1:T(8,128)(2,1)S(1)}, u32[]{:S(2)}, u32[]{:S(2)}) %collective-permute-start.1) | collective-permute-done | bytes 983072 | tf_op jit(solution)/shard_map/ppermute | solution.py:21
  73.1 1.4 %add_convert_fusion = bf16[3072,160]{0,1:T(8,128)(2,1)} fusion(bf16[3072,160]{0,1:T(8,128)(2,1)S(1)} %collective-permute-done.1, bf16[1,256,3072]{2,1,0:T(8,128)(2,1)S(1)} %copy-done, bf16[320,256]{1,0:T(8,128)(2,1)S(1)} %multiply_convert_fusion), kind=kOutput, calls=%fused_computation.4 | convolution fusion | flops 253132800 | bytes 3620864 | tf_op jit(solution)/shard_map/dot_general | solution.py:61
  74.5 1.6 %copy.41 = bf16[3072,160]{1,0:T(8,128)(2,1)S(1)} copy(bf16[3072,160]{0,1:T(8,128)(2,1)} %add_convert_fusion) | data formatting | bytes 1966080 | tf_op jit(solution)/shard_map/convert_element_type | solution.py:64
  76.1 0.0 copy-start.2
  76.1 3.4 %reshape.106 = bf16[16,240,128]{2,1,0:T(8,128)(2,1)} reshape(bf16[3072,160]{1,0:T(8,128)(2,1)S(1)} %copy.41) | data formatting | bytes 1966080 | tf_op jit(solution)/shard_map/reshape | solution.py:65
  79.5 3.8 %all-to-all-start.3 = ((bf16[16,240,128]{2,1,0:T(8,128)(2,1)}), bf16[16,240,128]{2,1,0:T(8,128)(2,1)S(1)}, u32[]{:S(2)}, u32[]{:S(2)}) async-start(bf16[16,240,128]{2,1,0:T(8,128)(2,1)} %reshape.106), calls=%async_computation.3 | async-start | bytes 1966080 | tf_op jit(solution)/shard_map/all_to_all | solution.py:66
  83.3 0.0 copy-done.2
  83.4 25.0 %all-to-all-done.3 = bf16[16,240,128]{2,1,0:T(8,128)(2,1)S(1)} async-done(((bf16[16,240,128]{2,1,0:T(8,128)(2,1)}), bf16[16,240,128]{2,1,0:T(8,128)(2,1)S(1)}, u32[]{:S(2)}, u32[]{:S(2)}) %all-to-all-start.3) | async-done | bytes 983072 | tf_op jit(solution)/shard_map/all_to_all | solution.py:66
  108.3 0.1 reduce_sum.44
  108.5 0.1 convert_element_type.47
  108.6 0.1 copy.42
  108.8 0.7 reshape.115
  109.5 7.0 %all-to-all-start.4 = ((bf16[16,2,960]{2,1,0:T(2,128)(2,1)}), bf16[16,2,960]{2,1,0:T(2,128)(2,1)S(1)}, u32[]{:S(2)}, u32[]{:S(2)}) async-start(bf16[16,2,960]{2,1,0:T(2,128)(2,1)} %reshape.115), calls=%async_computation.4 | async-start | bytes 131072 | tf_op jit(solution)/shard_map/all_to_all | solution.py:69
  116.6 7.4 %all-to-all-done.4 = bf16[16,2,960]{2,1,0:T(2,128)(2,1)S(1)} async-done(((bf16[16,2,960]{2,1,0:T(2,128)(2,1)}), bf16[16,2,960]{2,1,0:T(2,128)(2,1)S(1)}, u32[]{:S(2)}, u32[]{:S(2)}) %all-to-all-start.4) | async-done | bytes 61472 | tf_op jit(solution)/shard_map/all_to_all | solution.py:69
  124.0 0.1 reshape.116
  124.2 0.1 reshape.111
  124.2 0.0 copy-done.3
  124.2 0.8 fusion.15
  (9 shorter events, 0.2 us)
Async XLA Ops:
  0.0 68.2 %copy-start = (bf16[1,256,3072]{2,1,0:T(8,128)(2,1)S(1)}, bf16[1,256,3072]{2,1,0:T(8,128)(2,1)}, u32[]{:S(2)}) copy-start(bf16[1,256,3072]{2,1,0:T(8,128)(2,1)} %param.11) | copy-start | bytes 4718596
  51.9 9.1 %collective-permute-start = (bf16[4,4,240,128]{3,2,1,0:T(8,128)(2,1)S(1)}, bf16[4,4,240,128]{3,2,1,0:T(8,128)(2,1)S(1)}, u32[]{:S(2)}, u32[]{:S(2)}) collective-permute-start(bf16[4,4,240,128]{3,2,1,0:T(8,128)(2,1)S(1)} %all_to_all.27), channel_id=1, source_target_pairs={{0,16},{16,0},{1,17},{17,1},{2,18},{18,2},{3,19},{19,3},{4,20},{20... | collective-permute-start | bytes 2949128 | tf_op jit(solution)/shard_map/ppermute | solution.py:21
  64.0 3.1 %copy-start.1 = (bf16[4,4,320,192]{3,2,1,0:T(8,128)(2,1)S(1)}, bf16[4,4,320,192]{3,2,1,0:T(8,128)(2,1)}, u32[]{:S(2)}) copy-start(bf16[4,4,320,192]{3,2,1,0:T(8,128)(2,1)} %reshape.105) | copy-start | bytes 5898244
  64.0 3.5 %copy-start.4 = (bf16[1,3072,256]{2,1,0:T(8,128)(2,1)S(1)}, bf16[1,3072,256]{2,1,0:T(8,128)(2,1)}, u32[]{:S(2)}) copy-start(bf16[1,3072,256]{2,1,0:T(8,128)(2,1)} %param.10) | copy-start | bytes 4718596
  68.7 4.5 %collective-permute-start.1 = (bf16[3072,160]{0,1:T(8,128)(2,1)S(1)}, bf16[3072,160]{0,1:T(8,128)(2,1)S(1)}, u32[]{:S(2)}, u32[]{:S(2)}) collective-permute-start(bf16[3072,160]{0,1:T(8,128)(2,1)S(1)} %fusion), channel_id=1, source_target_pairs={{0,16},{16,0},{1,17},{17,1},{2,18},{18,2},{3,19},{19,3},{4,20},{20... | collective-permute-start | bytes 2949128 | tf_op jit(solution)/shard_map/ppermute | solution.py:21
  76.1 7.2 %copy-start.2 = (f32[24,2]{0,1:T(2,128)S(1)}, f32[24,2]{0,1:T(2,128)}, u32[]{:S(2)}) copy-start(f32[24,2]{0,1:T(2,128)} %param.8) | copy-start | bytes 580
  79.5 44.7 %copy-start.3 = (s32[24,2]{0,1:T(2,128)S(1)}, s32[24,2]{0,1:T(2,128)}, u32[]{:S(2)}) copy-start(s32[24,2]{0,1:T(2,128)} %param.7) | copy-start | bytes 580
  79.5 28.8 %all-to-all-start.3 = ((bf16[16,240,128]{2,1,0:T(8,128)(2,1)}), bf16[16,240,128]{2,1,0:T(8,128)(2,1)S(1)}, u32[]{:S(2)}, u32[]{:S(2)}) async-start(bf16[16,240,128]{2,1,0:T(8,128)(2,1)} %reshape.106), calls=%async_computation.3 | async-start | bytes 1966080 | tf_op jit(solution)/shard_map/all_to_all | solution.py:66
  109.5 14.5 %all-to-all-start.4 = ((bf16[16,2,960]{2,1,0:T(2,128)(2,1)}), bf16[16,2,960]{2,1,0:T(2,128)(2,1)S(1)}, u32[]{:S(2)}, u32[]{:S(2)}) async-start(bf16[16,2,960]{2,1,0:T(2,128)(2,1)} %reshape.115), calls=%async_computation.4 | async-start | bytes 131072 | tf_op jit(solution)/shard_map/all_to_all | solution.py:69

commit v7 on v6

--- a/solution.py
+++ b/solution.py
@@ -62,8 +62,10 @@
     other_t = lax.dot_general(down_weight[0], hidden[rows:], down_t, preferred_element_type=jnp.float32)
     partner_t = swap_cores(other_t.astype(jnp.bfloat16))
     pair_t = (own_t + partner_t.astype(jnp.float32)).astype(jnp.bfloat16)
-    by_slice = pair_t.reshape(n_loop, slice_width * rows // lane, lane)
-    summed = lax.all_to_all(by_slice, LOOP_AXES, 0, 0, tiled=True)
+    by_slice = pair_t.reshape(n_z, n_x, slice_width * rows // lane, lane)
+    x_sum = lax.all_to_all(by_slice, LOOP_AXES[1], 1, 1, tiled=True)
+    x_sum = x_sum.astype(jnp.float32).sum(axis=1).astype(jnp.bfloat16)
+    summed = lax.all_to_all(x_sum, LOOP_AXES[0], 0, 0, tiled=True)
     summed = summed.astype(jnp.float32).sum(axis=0).reshape(slice_width, rows).T
     expert_out = summed.astype(jnp.bfloat16).reshape(peers, CAP, slice_width)
     returned = lax.all_to_all(expert_out, GROUP_AXES, split_axis=0, concat_axis=0, tiled=True).reshape(

time: 126 us -> 125 us (level)
  the two profiles are of different devices: /device:TPU:1 before, /device:TPU:8 now
where the time goes in v7:
time: 125 us
  blocking collectives  68.5 us (55%)
  waiting for transfers between devices  22.3 us (18%)
  local copies, waits for them, and re-layouts  12.6 us (10%)
  starting transfers between devices  11.8 us (9%)
  matrix products  7.3 us (6%)
  other arithmetic  2.16 us (2%)
    all_to_all x1, blocking collectives, body(): lax.all_to_all(jnp.broadcast_to(dense[None], (n_z,) + dense.shape), LOOP_...  19 us
    all_to_all x1, blocking collectives, body(): x_sum = lax.all_to_all(by_slice, LOOP_AXES[1], 1, 1, tiled=True)  17.4 us
    all_to_all x1, blocking collectives, body(): lax.all_to_all(jnp.repeat(packed, halves, axis=0), GROUP_AXES, split_axis...  16.8 us
    all_to_all x1, blocking collectives, body(): lax.all_to_all(jnp.broadcast_to(planes[None], (n_x,) + planes.shape), LOO...  15.4 us
    all_to_all x1, waiting for transfers between devices, body(): summed = lax.all_to_all(x_sum, LOOP_AXES[0], 0, 0, tiled=True)  9.77 us
    all_to_all x1, waiting for transfers between devices, body(): lax.all_to_all(expert_out, GROUP_AXES, split_axis=0, concat_axis=0, tiled...  7.58 us
    ppermute x2, waiting for transfers between devices, swap_cores(): return lax.ppermute(x, 'c', [(0, 1), (1, 0)])  4.94 us
    reshape x2, local copies, waits for them, and re-layouts, body(): by_slice = pair_t.reshape(n_z, n_x, slice_width * rows // lane, lane)  4.66 us
  transfers between devices with their start and end apart: 4, of which 4 were waited for; matrix products, arithmetic and copies ran while one was open for 0% of the time, Pallas kernels for 0%

profile of v7, /device:TPU:8, one launch (start us, length us, event | category | flops | bytes accessed | tf_op | source)
XLA Modules:
  0.0 124.8 jit_solution(8399473455528711469)
XLA Ops:
  0.0 0.0 copy-start
  0.0 0.9 copy.46
  0.9 0.1 eq.73
  1.0 0.1 fusion.22
  1.1 0.1 reduce_window_sum.11
  1.1 0.2 select_reduce_fusion
  1.3 0.1 eq.77
  1.4 0.1 copy.47
  1.5 0.7 multiply_add_fusion
  2.2 0.1 fusion.27
  2.3 0.9 convolution_convert_fusion.1
  3.2 0.1 reshape.113
  3.3 16.8 %all_to_all.30 = bf16[16,2,960]{2,1,0:T(2,128)(2,1)S(1)} all-to-all(bf16[16,2,960]{2,1,0:T(2,128)(2,1)S(1)} %reshape.113), channel_id=1, replica_groups=mesh['zl'=2,'yh'=4,'yl'=2,'c'=2,'zh'=4,'x'=4] {'zl','yh','yl'}, dimensions={0} | all-to-all | bytes 122880 | tf_op jit(solution)/shard_map/all_to_all | solution.py:38
  20.1 0.1 reshape.114
  20.2 0.1 broadcast_in_dim.9
  20.4 19.0 %all_to_all.31 = bf16[4,240,128]{2,1,0:T(8,128)(2,1)S(1)} all-to-all(bf16[4,240,128]{2,1,0:T(8,128)(2,1)S(1)} %broadcast_in_dim.10), channel_id=1, replica_groups=mesh['zl'=2,'yh'=4,'yl'=2,'c'=2,'zh'=4,'x'=4] {'zh'}, dimensions={0} | all-to-all | bytes 491520 | tf_op jit(solution)/shard_map/all_to_all | solution.py:44
  39.4 0.1 broadcast_in_dim.11
  39.5 15.4 %all_to_all.32 = bf16[4,4,240,128]{3,2,1,0:T(8,128)(2,1)S(1)} all-to-all(bf16[4,4,240,128]{3,2,1,0:T(8,128)(2,1)S(1)} %broadcast_in_dim.11), channel_id=1, replica_groups=mesh['zl'=2,'yh'=4,'yl'=2,'c'=2,'zh'=4,'x'=4] {'x'}, dimensions={0} | all-to-all | bytes 1966080 | tf_op jit(solution)/shard_map/all_to_all | solution.py:47
  54.9 1.9 %collective-permute-start = (bf16[4,4,240,128]{3,2,1,0:T(8,128)(2,1)S(1)}, bf16[4,4,240,128]{3,2,1,0:T(8,128)(2,1)S(1)}, u32[]{:S(2)}, u32[]{:S(2)}) collective-permute-start(bf16[4,4,240,128]{3,2,1,0:T(8,128)(2,1)S(1)} %all_to_all.32), channel_id=1, source_target_pairs={{0,16},{16,0},{1,17},{17,1},{2,18},{18,2},{3,19},{19,3},{4,20},{20... | collective-permute-start | bytes 2949128 | tf_op jit(solution)/shard_map/ppermute | solution.py:21
  56.8 2.5 %collective-permute-done = bf16[4,4,240,128]{3,2,1,0:T(8,128)(2,1)S(1)} collective-permute-done((bf16[4,4,240,128]{3,2,1,0:T(8,128)(2,1)S(1)}, bf16[4,4,240,128]{3,2,1,0:T(8,128)(2,1)S(1)}, u32[]{:S(2)}, u32[]{:S(2)}) %collective-permute-start) | collective-permute-done | bytes 983072 | tf_op jit(solution)/shard_map/ppermute | solution.py:21
  59.4 0.1 pad_maximum_fusion
  59.5 2.9 %reshape.105 = bf16[4,4,320,192]{3,2,1,0:T(8,128)(2,1)} reshape(bf16[4,4,480,128]{3,2,1,0:T(8,128)(2,1)S(1)} %pad_maximum_fusion) | data formatting | bytes 3932160 | tf_op jit(solution)/shard_map/reshape | solution.py:51
  62.4 3.1 %fusion.9 = f32[320,256]{1,0:T(8,128)S(1)} fusion(bf16[4,4,320,192]{3,2,1,0:T(8,128)(2,1)} %reshape.105, bf16[4,4,192,256]{3,2,1,0:T(8,128)(2,1)} %bitcast.34), kind=kOutput, calls=%fused_computation.11 | convolution fusion | flops 503316480 | bytes 3866624 | tf_op jit(solution)/shard_map/xzrf,zxfh->rh/dot_general | solution.py:53
  65.5 0.0 copy-done.1
  65.5 0.4 copy-done.4
  65.9 0.7 multiply_convert_fusion
  66.6 0.0 copy-done
  66.6 0.4 fusion
  67.1 2.0 %collective-permute-start.1 = (bf16[3072,160]{0,1:T(8,128)(2,1)S(1)}, bf16[3072,160]{0,1:T(8,128)(2,1)S(1)}, u32[]{:S(2)}, u32[]{:S(2)}) collective-permute-start(bf16[3072,160]{0,1:T(8,128)(2,1)S(1)} %fusion), channel_id=1, source_target_pairs={{0,16},{16,0},{1,17},{17,1},{2,18},{18,2},{3,19},{19,3},{4,20},{20... | collective-permute-start | bytes 2949128 | tf_op jit(solution)/shard_map/ppermute | solution.py:21
  69.1 2.4 %collective-permute-done.1 = bf16[3072,160]{0,1:T(8,128)(2,1)S(1)} collective-permute-done((bf16[3072,160]{0,1:T(8,128)(2,1)S(1)}, bf16[3072,160]{0,1:T(8,128)(2,1)S(1)}, u32[]{:S(2)}, u32[]{:S(2)}) %collective-permute-start.1) | collective-permute-done | bytes 983072 | tf_op jit(solution)/shard_map/ppermute | solution.py:21
  71.5 1.4 %add_convert_fusion = bf16[3072,160]{0,1:T(8,128)(2,1)} fusion(bf16[3072,160]{0,1:T(8,128)(2,1)S(1)} %collective-permute-done.1, bf16[1,256,3072]{2,1,0:T(8,128)(2,1)S(1)} %copy-done, bf16[320,256]{1,0:T(8,128)(2,1)S(1)} %multiply_convert_fusion), kind=kOutput, calls=%fused_computation.4 | convolution fusion | flops 253132800 | bytes 3620864 | tf_op jit(solution)/shard_map/dot_general | solution.py:61
  72.9 1.6 %copy.53 = bf16[3072,160]{1,0:T(8,128)(2,1)S(1)} copy(bf16[3072,160]{0,1:T(8,128)(2,1)} %add_convert_fusion) | data formatting | bytes 1966080 | tf_op jit(solution)/shard_map/convert_element_type | solution.py:64
  74.5 3.4 %reshape.106 = bf16[4,4,240,128]{3,2,1,0:T(8,128)(2,1)} reshape(bf16[3072,160]{1,0:T(8,128)(2,1)S(1)} %copy.53) | data formatting | bytes 1966080 | tf_op jit(solution)/shard_map/reshape | solution.py:65
  77.9 1.3 %copy.54 = bf16[4,4,240,128]{3,2,0,1:T(8,128)(2,1)S(1)} copy(bf16[4,4,240,128]{3,2,1,0:T(8,128)(2,1)} %reshape.106) | data formatting | bytes 1966080 | tf_op jit(solution)/shard_map/reshape | solution.py:65
  79.2 0.0 copy-start.2
  79.2 17.4 %all_to_all.33 = bf16[4,4,240,128]{3,2,0,1:T(8,128)(2,1)S(1)} all-to-all(bf16[4,4,240,128]{3,2,0,1:T(8,128)(2,1)S(1)} %copy.54), channel_id=1, replica_groups=mesh['zl'=2,'yh'=4,'yl'=2,'c'=2,'zh'=4,'x'=4] {'x'}, dimensions={1} | all-to-all | bytes 1966080 | tf_op jit(solution)/shard_map/all_to_all | solution.py:66
  96.6 0.9 reduce_sum.56
  97.4 3.4 %all-to-all-start.4 = ((bf16[4,240,128]{2,1,0:T(8,128)(2,1)}), bf16[4,240,128]{2,1,0:T(8,128)(2,1)S(1)}, u32[]{:S(2)}, u32[]{:S(2)}) async-start(bf16[4,240,128]{2,1,0:T(8,128)(2,1)} %reduce_sum.56), calls=%async_computation.4 | async-start | bytes 491520 | tf_op jit(solution)/shard_map/all_to_all | solution.py:68
  100.8 0.0 copy-done.2
  100.9 9.8 %all-to-all-done.4 = bf16[4,240,128]{2,1,0:T(8,128)(2,1)S(1)} async-done(((bf16[4,240,128]{2,1,0:T(8,128)(2,1)}), bf16[4,240,128]{2,1,0:T(8,128)(2,1)S(1)}, u32[]{:S(2)}, u32[]{:S(2)}) %all-to-all-start.4) | async-done | bytes 245792 | tf_op jit(solution)/shard_map/all_to_all | solution.py:68
  110.7 0.1 convert_element_type.49
  110.8 0.1 copy.55
  111.0 0.7 reshape.115
  111.7 4.5 %all-to-all-start.5 = ((bf16[16,2,960]{2,1,0:T(2,128)(2,1)}), bf16[16,2,960]{2,1,0:T(2,128)(2,1)S(1)}, u32[]{:S(2)}, u32[]{:S(2)}) async-start(bf16[16,2,960]{2,1,0:T(2,128)(2,1)} %reshape.115), calls=%async_computation.5 | async-start | bytes 131072 | tf_op jit(solution)/shard_map/all_to_all | solution.py:71
  116.3 7.6 %all-to-all-done.5 = bf16[16,2,960]{2,1,0:T(2,128)(2,1)S(1)} async-done(((bf16[16,2,960]{2,1,0:T(2,128)(2,1)}), bf16[16,2,960]{2,1,0:T(2,128)(2,1)S(1)}, u32[]{:S(2)}, u32[]{:S(2)}) %all-to-all-start.5) | async-done | bytes 61472 | tf_op jit(solution)/shard_map/all_to_all | solution.py:71
  123.8 0.1 reshape.116
  124.0 0.1 reshape.111
  124.0 0.8 fusion.15
  (12 shorter events, 0.2 us)
Async XLA Ops:
  0.0 66.6 %copy-start = (bf16[1,256,3072]{2,1,0:T(8,128)(2,1)S(1)}, bf16[1,256,3072]{2,1,0:T(8,128)(2,1)}, u32[]{:S(2)}) copy-start(bf16[1,256,3072]{2,1,0:T(8,128)(2,1)} %param.11) | copy-start | bytes 4718596
  54.9 4.4 %collective-permute-start = (bf16[4,4,240,128]{3,2,1,0:T(8,128)(2,1)S(1)}, bf16[4,4,240,128]{3,2,1,0:T(8,128)(2,1)S(1)}, u32[]{:S(2)}, u32[]{:S(2)}) collective-permute-start(bf16[4,4,240,128]{3,2,1,0:T(8,128)(2,1)S(1)} %all_to_all.32), channel_id=1, source_target_pairs={{0,16},{16,0},{1,17},{17,1},{2,18},{18,2},{3,19},{19,3},{4,20},{20... | collective-permute-start | bytes 2949128 | tf_op jit(solution)/shard_map/ppermute | solution.py:21
  62.4 3.1 %copy-start.1 = (bf16[4,4,320,192]{3,2,1,0:T(8,128)(2,1)S(1)}, bf16[4,4,320,192]{3,2,1,0:T(8,128)(2,1)}, u32[]{:S(2)}) copy-start(bf16[4,4,320,192]{3,2,1,0:T(8,128)(2,1)} %reshape.105) | copy-start | bytes 5898244
  62.4 3.5 %copy-start.4 = (bf16[1,3072,256]{2,1,0:T(8,128)(2,1)S(1)}, bf16[1,3072,256]{2,1,0:T(8,128)(2,1)}, u32[]{:S(2)}) copy-start(bf16[1,3072,256]{2,1,0:T(8,128)(2,1)} %param.10) | copy-start | bytes 4718596
  67.1 4.5 %collective-permute-start.1 = (bf16[3072,160]{0,1:T(8,128)(2,1)S(1)}, bf16[3072,160]{0,1:T(8,128)(2,1)S(1)}, u32[]{:S(2)}, u32[]{:S(2)}) collective-permute-start(bf16[3072,160]{0,1:T(8,128)(2,1)S(1)} %fusion), channel_id=1, source_target_pairs={{0,16},{16,0},{1,17},{17,1},{2,18},{18,2},{3,19},{19,3},{4,20},{20... | collective-permute-start | bytes 2949128 | tf_op jit(solution)/shard_map/ppermute | solution.py:21
  79.2 21.7 %copy-start.2 = (f32[24,2]{0,1:T(2,128)S(1)}, f32[24,2]{0,1:T(2,128)}, u32[]{:S(2)}) copy-start(f32[24,2]{0,1:T(2,128)} %param.8) | copy-start | bytes 580
  96.6 27.5 %copy-start.3 = (s32[24,2]{0,1:T(2,128)S(1)}, s32[24,2]{0,1:T(2,128)}, u32[]{:S(2)}) copy-start(s32[24,2]{0,1:T(2,128)} %param.7) | copy-start | bytes 580
  97.4 13.2 %all-to-all-start.4 = ((bf16[4,240,128]{2,1,0:T(8,128)(2,1)}), bf16[4,240,128]{2,1,0:T(8,128)(2,1)S(1)}, u32[]{:S(2)}, u32[]{:S(2)}) async-start(bf16[4,240,128]{2,1,0:T(8,128)(2,1)} %reduce_sum.56), calls=%async_computation.4 | async-start | bytes 491520 | tf_op jit(solution)/shard_map/all_to_all | solution.py:68
  111.7 12.1 %all-to-all-start.5 = ((bf16[16,2,960]{2,1,0:T(2,128)(2,1)}), bf16[16,2,960]{2,1,0:T(2,128)(2,1)S(1)}, u32[]{:S(2)}, u32[]{:S(2)}) async-start(bf16[16,2,960]{2,1,0:T(2,128)(2,1)} %reshape.115), calls=%async_computation.5 | async-start | bytes 131072 | tf_op jit(solution)/shard_map/all_to_all | solution.py:71

commit v8 on v4

--- a/solution.py
+++ b/solution.py
@@ -33,24 +33,26 @@
     slot_index = jnp.arange(EXPERTS * CAP, dtype=jnp.int32)
     picker = (slot_index[:, None] == (assigned * CAP + position)[None, :]).astype(jnp.bfloat16)
     picker = picker.reshape(EXPERTS * CAP, tok_count, 2).sum(axis=2)
-    packed = jnp.dot(picker, tokens, preferred_element_type=jnp.float32).astype(jnp.bfloat16)
-    packed = packed.reshape(EXPERTS, CAP, slice_width)
+    n_z, n_x = lax.axis_size(LOOP_AXES[0]), lax.axis_size(LOOP_AXES[1])
+    plane_tokens = lax.all_to_all(
+        jnp.broadcast_to(tokens[None], (n_z,) + tokens.shape), LOOP_AXES[0], 0, 0, tiled=True
+    )
+    packed = jnp.einsum("st,ztf->szf", picker, plane_tokens, preferred_element_type=jnp.float32)
+    packed = packed.astype(jnp.bfloat16).reshape(EXPERTS, CAP, n_z * slice_width)
     arrived = lax.all_to_all(
         jnp.repeat(packed, halves, axis=0), GROUP_AXES, split_axis=0, concat_axis=0, tiled=True
-    )
-    lane = 128
-    dense = arrived.reshape(rows * slice_width // lane, lane)
+    ).reshape(rows, n_z * slice_width)
     spread = lax.all_to_all(
-        jnp.broadcast_to(dense[None], (n_loop,) + dense.shape), LOOP_AXES, 0, 0, tiled=True
+        jnp.broadcast_to(arrived[None], (n_x,) + arrived.shape), LOOP_AXES[1], 0, 0, tiled=True
     )
     other = swap_cores(spread)
-    segment = jnp.concatenate([spread, other], axis=1).reshape(n_loop, 2 * rows, slice_width)
-    by_block = (n_loop, slice_width, hidden_width)
+    segment = jnp.concatenate([spread, other], axis=1).reshape(n_x, 2 * rows, n_z, slice_width)
+    by_block = (n_z, n_x, slice_width, hidden_width)
     gate_sum = jnp.einsum(
-        "lrf,lfh->rh", segment, gate_weight[0].reshape(by_block), preferred_element_type=jnp.float32
+        "xrzf,zxfh->rh", segment, gate_weight[0].reshape(by_block), preferred_element_type=jnp.float32
     )
     up_sum = jnp.einsum(
-        "lrf,lfh->rh", segment, up_weight[0].reshape(by_block), preferred_element_type=jnp.float32
+        "xrzf,zxfh->rh", segment, up_weight[0].reshape(by_block), preferred_element_type=jnp.float32
     )
     hidden = (jax.nn.silu(gate_sum) * up_sum).astype(jnp.bfloat16)
     down_t = (((0,), (1,)), ((), ()))
@@ -58,6 +60,7 @@
     other_t = lax.dot_general(down_weight[0], hidden[rows:], down_t, preferred_element_type=jnp.float32)
     partner_t = swap_cores(other_t.astype(jnp.bfloat16))
     pair_t = (own_t + partner_t.astype(jnp.float32)).astype(jnp.bfloat16)
+    lane = 128
     by_slice = pair_t.reshape(n_loop, slice_width * rows // lane, lane)
     summed = lax.all_to_all(by_slice, LOOP_AXES, 0, 0, tiled=True)
     summed = summed.astype(jnp.float32).sum(axis=0).reshape(slice_width, rows).T

time: 129 us -> 128 us (level)
  blocking collectives: 54.5 us -> 29.9 us
  starting transfers between devices: 14.4 us -> 33.2 us
  waiting for transfers between devices: 39.8 us -> 44.1 us
    all_to_all x1, blocking collectives: 37.8 us -> 13.3 us  [body(): lax.all_to_all(jnp.broadcast_to(arrived[None], (n_x,) + arrived.shape), L...]
    all_to_all x0 -> x1, starting transfers between devices: none -> 10.8 us  [body(): lax.all_to_all(jnp.broadcast_to(tokens[None], (n_z,) + tokens.shape), LOO...]
    all_to_all x1, starting transfers between devices: 3.5 us -> 8.56 us  [body(): lax.all_to_all(expert_out, GROUP_AXES, split_axis=0, concat_axis=0, tiled...]
    all_to_all x0 -> x1, waiting for transfers between devices: none -> 4.91 us  [body(): lax.all_to_all(jnp.broadcast_to(tokens[None], (n_z,) + tokens.shape), LOO...]
    ppermute x2, starting transfers between devices: 6.41 us -> 9.99 us  [swap_cores(): return lax.ppermute(x, 'c', [(0, 1), (1, 0)])]
    reshape x2 -> x1, local copies, waits for them, and re-layouts: 2.95 us -> 0.21 us  [body(): packed.astype(jnp.bfloat16).reshape(EXPERTS, CAP, n_z * slice_width)]
    concatenate x0 -> x1, local copies, waits for them, and re-layouts: none -> 2.44 us  [body(): jnp.concatenate([spread, other], axis=1)]
    broadcast_in_dim x2 -> x3, local copies, waits for them, and re-layouts: 0.27 us -> 1.6 us  [the longest x1 1.45 us: body(): jnp.broadcast_to(tokens[None], (n_z,) + tokens.shape)]
  transfers between devices with their start and end apart: 4 -> 5, of which waited for: 4 -> 5; matrix products, arithmetic and copies ran while one was open for 0% -> 2% of each run, Pallas kernels for 0% -> 0%
where the time goes in v8:
time: 128 us; the launch traced here: 127 us
  waiting for transfers between devices  44.1 us (34%)
  starting transfers between devices  33.2 us (26%)
  blocking collectives  29.9 us (23%)
  local copies, waits for them, and re-layouts  11.9 us (9%)
  matrix products  6.86 us (5%)
  other arithmetic  1.39 us (1%)
    all_to_all x1, waiting for transfers between devices, body(): summed = lax.all_to_all(by_slice, LOOP_AXES, 0, 0, tiled=True)  27.4 us
    all_to_all x1, blocking collectives, body(): lax.all_to_all(jnp.repeat(packed, halves, axis=0), GROUP_AXES, split_axis...  16.6 us
    all_to_all x1, blocking collectives, body(): lax.all_to_all(jnp.broadcast_to(arrived[None], (n_x,) + arrived.shape), L...  13.3 us
    all_to_all x1, starting transfers between devices, body(): lax.all_to_all(jnp.broadcast_to(tokens[None], (n_z,) + tokens.shape), LOO...  10.8 us
    ppermute x2, starting transfers between devices, swap_cores(): return lax.ppermute(x, 'c', [(0, 1), (1, 0)])  9.99 us
    all_to_all x1, starting transfers between devices, body(): lax.all_to_all(expert_out, GROUP_AXES, split_axis=0, concat_axis=0, tiled...  8.56 us
    all_to_all x1, waiting for transfers between devices, body(): lax.all_to_all(expert_out, GROUP_AXES, split_axis=0, concat_axis=0, tiled...  7.44 us
    all_to_all x1, waiting for transfers between devices, body(): lax.all_to_all(jnp.broadcast_to(tokens[None], (n_z,) + tokens.shape), LOO...  4.91 us
  transfers between devices with their start and end apart: 5, of which 5 were waited for; matrix products, arithmetic and copies ran while one was open for 2% of the time, Pallas kernels for 0%

profile of v8, /device:TPU:1, one launch (start us, length us, event | category | flops | bytes accessed | tf_op | source)
XLA Modules:
  0.0 127.5 jit_solution(14686385354562256291)
XLA Ops:
  0.0 0.0 copy-start
  0.0 1.4 %broadcast_in_dim.8 = bf16[4,24,192]{2,1,0:T(8,128)(2,1)} broadcast(bf16[24,192]{1,0:T(8,128)(2,1)} %param.6), dimensions={1,2} | broadcast | bytes 46080 | tf_op jit(solution)/shard_map/broadcast_in_dim | solution.py:38
  1.5 10.8 %all-to-all-start = ((bf16[4,24,192]{2,1,0:T(8,128)(2,1)}), bf16[4,24,192]{2,1,0:T(8,128)(2,1)S(1)}, u32[]{:S(2)}, u32[]{:S(2)}) async-start(bf16[4,24,192]{2,1,0:T(8,128)(2,1)} %broadcast_in_dim.8), calls=%async_computation | async-start | bytes 98304 | tf_op jit(solution)/shard_map/all_to_all | solution.py:37
  12.3 0.8 copy.44
  13.0 0.1 eq.73
  13.1 0.1 fusion.22
  13.2 0.1 reduce_window_sum.11
  13.3 0.2 select_reduce_fusion
  13.5 0.1 eq.77
  13.6 0.1 copy.45
  13.7 0.7 multiply_add_fusion
  14.4 0.1 fusion.27
  14.4 4.9 %all-to-all-done = bf16[4,24,192]{2,1,0:T(8,128)(2,1)S(1)} async-done(((bf16[4,24,192]{2,1,0:T(8,128)(2,1)}), bf16[4,24,192]{2,1,0:T(8,128)(2,1)S(1)}, u32[]{:S(2)}, u32[]{:S(2)}) %all-to-all-start) | async-done | bytes 36896 | tf_op jit(solution)/shard_map/all_to_all | solution.py:37
  19.3 0.2 convolution_convert_fusion.1
  19.6 0.1 copy.47
  19.7 0.2 reshape.103
  19.9 16.6 %all_to_all.25 = bf16[16,10,768]{2,1,0:T(8,128)(2,1)S(1)} all-to-all(bf16[16,10,768]{2,1,0:T(8,128)(2,1)S(1)} %bitcast.36), channel_id=1, replica_groups=mesh['zl'=2,'yh'=4,'yl'=2,'c'=2,'zh'=4,'x'=4] {'zl','yh','yl'}, dimensions={0} | all-to-all | bytes 491520 | tf_op jit(solution)/shard_map/all_to_all | solution.py:42
  36.5 0.1 broadcast_in_dim.10
  36.6 0.1 broadcast_in_dim.11
  36.7 13.3 %all_to_all.26 = bf16[4,160,768]{2,1,0:T(8,128)(2,1)S(1)} all-to-all(bf16[4,160,768]{2,1,0:T(8,128)(2,1)S(1)} %broadcast_in_dim.11), channel_id=1, replica_groups=mesh['zl'=2,'yh'=4,'yl'=2,'c'=2,'zh'=4,'x'=4] {'x'}, dimensions={0} | all-to-all | bytes 1966080 | tf_op jit(solution)/shard_map/all_to_all | solution.py:45
  50.0 7.7 %collective-permute-start = (bf16[4,160,768]{2,1,0:T(8,128)(2,1)S(1)}, bf16[4,160,768]{2,1,0:T(8,128)(2,1)S(1)}, u32[]{:S(2)}, u32[]{:S(2)}) collective-permute-start(bf16[4,160,768]{2,1,0:T(8,128)(2,1)S(1)} %all_to_all.26), channel_id=1, source_target_pairs={{0,16},{16,0},{1,17},{17,1},{2,18},{18,2},{3,19},{19,3},{4,20},{20... | collective-permute-start | bytes 2949128 | tf_op jit(solution)/shard_map/ppermute | solution.py:21
  57.7 2.2 %collective-permute-done = bf16[4,160,768]{2,1,0:T(8,128)(2,1)S(1)} collective-permute-done((bf16[4,160,768]{2,1,0:T(8,128)(2,1)S(1)}, bf16[4,160,768]{2,1,0:T(8,128)(2,1)S(1)}, u32[]{:S(2)}, u32[]{:S(2)}) %collective-permute-start) | collective-permute-done | bytes 983072 | tf_op jit(solution)/shard_map/ppermute | solution.py:21
  59.9 0.1 pad_maximum_fusion
  60.0 2.4 %copy.48 = bf16[4,320,768]{1,2,0:T(8,128)(2,1)} copy(bf16[4,320,768]{2,1,0:T(8,128)(2,1)S(1)} %pad_maximum_fusion) | data formatting | bytes 3932160 | tf_op jit(solution)/shard_map/concatenate | solution.py:49
  62.5 3.1 %fusion.9 = f32[320,256]{1,0:T(8,128)S(1)} fusion(bf16[4,320,4,192]{1,3,2,0:T(8,128)(2,1)} %bitcast.33, bf16[4,4,192,256]{3,2,1,0:T(8,128)(2,1)} %bitcast.35), kind=kOutput, calls=%fused_computation.11 | convolution fusion | flops 503316480 | bytes 3866624 | tf_op jit(solution)/shard_map/xrzf,zxfh->rh/dot_general | solution.py:51
  65.6 0.0 copy-done.1
  65.6 0.2 copy-done.4
  65.8 0.9 multiply_convert_fusion
  66.7 0.0 copy-done
  66.7 0.4 fusion
  67.2 2.3 %collective-permute-start.1 = (bf16[3072,160]{0,1:T(8,128)(2,1)S(1)}, bf16[3072,160]{0,1:T(8,128)(2,1)S(1)}, u32[]{:S(2)}, u32[]{:S(2)}) collective-permute-start(bf16[3072,160]{0,1:T(8,128)(2,1)S(1)} %fusion), channel_id=1, source_target_pairs={{0,16},{16,0},{1,17},{17,1},{2,18},{18,2},{3,19},{19,3},{4,20},{20... | collective-permute-start | bytes 2949128 | tf_op jit(solution)/shard_map/ppermute | solution.py:21
  69.5 2.2 %collective-permute-done.1 = bf16[3072,160]{0,1:T(8,128)(2,1)S(1)} collective-permute-done((bf16[3072,160]{0,1:T(8,128)(2,1)S(1)}, bf16[3072,160]{0,1:T(8,128)(2,1)S(1)}, u32[]{:S(2)}, u32[]{:S(2)}) %collective-permute-start.1) | collective-permute-done | bytes 983072 | tf_op jit(solution)/shard_map/ppermute | solution.py:21
  71.6 1.4 %add_convert_fusion = bf16[3072,160]{0,1:T(8,128)(2,1)} fusion(bf16[3072,160]{0,1:T(8,128)(2,1)S(1)} %collective-permute-done.1, bf16[1,256,3072]{2,1,0:T(8,128)(2,1)S(1)} %copy-done, bf16[320,256]{1,0:T(8,128)(2,1)S(1)} %multiply_convert_fusion), kind=kOutput, calls=%fused_computation.4 | convolution fusion | flops 253132800 | bytes 3620864 | tf_op jit(solution)/shard_map/dot_general | solution.py:59
  73.0 1.6 %copy.51 = bf16[3072,160]{1,0:T(8,128)(2,1)S(1)} copy(bf16[3072,160]{0,1:T(8,128)(2,1)} %add_convert_fusion) | data formatting | bytes 1966080 | tf_op jit(solution)/shard_map/convert_element_type | solution.py:62
  74.6 0.0 copy-start.2
  74.7 3.4 %reshape.106 = bf16[16,240,128]{2,1,0:T(8,128)(2,1)} reshape(bf16[3072,160]{1,0:T(8,128)(2,1)S(1)} %copy.51) | data formatting | bytes 1966080 | tf_op jit(solution)/shard_map/reshape | solution.py:64
  78.1 3.8 %all-to-all-start.3 = ((bf16[16,240,128]{2,1,0:T(8,128)(2,1)}), bf16[16,240,128]{2,1,0:T(8,128)(2,1)S(1)}, u32[]{:S(2)}, u32[]{:S(2)}) async-start(bf16[16,240,128]{2,1,0:T(8,128)(2,1)} %reshape.106), calls=%async_computation.3 | async-start | bytes 1966080 | tf_op jit(solution)/shard_map/all_to_all | solution.py:65
  81.8 0.0 copy-done.2
  81.9 27.4 %all-to-all-done.3 = bf16[16,240,128]{2,1,0:T(8,128)(2,1)S(1)} async-done(((bf16[16,240,128]{2,1,0:T(8,128)(2,1)}), bf16[16,240,128]{2,1,0:T(8,128)(2,1)S(1)}, u32[]{:S(2)}, u32[]{:S(2)}) %all-to-all-start.3) | async-done | bytes 983072 | tf_op jit(solution)/shard_map/all_to_all | solution.py:65
  109.3 0.1 reduce_sum.44
  109.4 0.1 convert_element_type.47
  109.5 0.1 copy.52
  109.7 0.7 reshape.114
  110.4 8.6 %all-to-all-start.4 = ((bf16[16,2,960]{2,1,0:T(2,128)(2,1)}), bf16[16,2,960]{2,1,0:T(2,128)(2,1)S(1)}, u32[]{:S(2)}, u32[]{:S(2)}) async-start(bf16[16,2,960]{2,1,0:T(2,128)(2,1)} %reshape.114), calls=%async_computation.4 | async-start | bytes 131072 | tf_op jit(solution)/shard_map/all_to_all | solution.py:68
  119.0 7.4 %all-to-all-done.4 = bf16[16,2,960]{2,1,0:T(2,128)(2,1)S(1)} async-done(((bf16[16,2,960]{2,1,0:T(2,128)(2,1)}), bf16[16,2,960]{2,1,0:T(2,128)(2,1)S(1)}, u32[]{:S(2)}, u32[]{:S(2)}) %all-to-all-start.4) | async-done | bytes 61472 | tf_op jit(solution)/shard_map/all_to_all | solution.py:68
  126.5 0.1 reshape.115
  126.6 0.1 reshape.112
  126.7 0.8 fusion.15
  (9 shorter events, 0.1 us)
Async XLA Ops:
  0.0 66.7 %copy-start = (bf16[1,256,3072]{2,1,0:T(8,128)(2,1)S(1)}, bf16[1,256,3072]{2,1,0:T(8,128)(2,1)}, u32[]{:S(2)}) copy-start(bf16[1,256,3072]{2,1,0:T(8,128)(2,1)} %param.11) | copy-start | bytes 4718596
  1.5 17.9 %all-to-all-start = ((bf16[4,24,192]{2,1,0:T(8,128)(2,1)}), bf16[4,24,192]{2,1,0:T(8,128)(2,1)S(1)}, u32[]{:S(2)}, u32[]{:S(2)}) async-start(bf16[4,24,192]{2,1,0:T(8,128)(2,1)} %broadcast_in_dim.8), calls=%async_computation | async-start | bytes 98304 | tf_op jit(solution)/shard_map/all_to_all | solution.py:37
  50.0 9.9 %collective-permute-start = (bf16[4,160,768]{2,1,0:T(8,128)(2,1)S(1)}, bf16[4,160,768]{2,1,0:T(8,128)(2,1)S(1)}, u32[]{:S(2)}, u32[]{:S(2)}) collective-permute-start(bf16[4,160,768]{2,1,0:T(8,128)(2,1)S(1)} %all_to_all.26), channel_id=1, source_target_pairs={{0,16},{16,0},{1,17},{17,1},{2,18},{18,2},{3,19},{19,3},{4,20},{20... | collective-permute-start | bytes 2949128 | tf_op jit(solution)/shard_map/ppermute | solution.py:21
  62.5 3.1 %copy-start.1 = (bf16[4,320,768]{1,2,0:T(8,128)(2,1)S(1)}, bf16[4,320,768]{1,2,0:T(8,128)(2,1)}, u32[]{:S(2)}) copy-start(bf16[4,320,768]{1,2,0:T(8,128)(2,1)} %copy.48) | copy-start | bytes 5898244
  62.5 3.3 %copy-start.4 = (bf16[1,3072,256]{2,1,0:T(8,128)(2,1)S(1)}, bf16[1,3072,256]{2,1,0:T(8,128)(2,1)}, u32[]{:S(2)}) copy-start(bf16[1,3072,256]{2,1,0:T(8,128)(2,1)} %param.10) | copy-start | bytes 4718596
  67.2 4.5 %collective-permute-start.1 = (bf16[3072,160]{0,1:T(8,128)(2,1)S(1)}, bf16[3072,160]{0,1:T(8,128)(2,1)S(1)}, u32[]{:S(2)}, u32[]{:S(2)}) collective-permute-start(bf16[3072,160]{0,1:T(8,128)(2,1)S(1)} %fusion), channel_id=1, source_target_pairs={{0,16},{16,0},{1,17},{17,1},{2,18},{18,2},{3,19},{19,3},{4,20},{20... | collective-permute-start | bytes 2949128 | tf_op jit(solution)/shard_map/ppermute | solution.py:21
  74.6 7.2 %copy-start.2 = (f32[24,2]{0,1:T(2,128)S(1)}, f32[24,2]{0,1:T(2,128)}, u32[]{:S(2)}) copy-start(f32[24,2]{0,1:T(2,128)} %param.8) | copy-start | bytes 580
  78.0 48.6 %copy-start.3 = (s32[24,2]{0,1:T(2,128)S(1)}, s32[24,2]{0,1:T(2,128)}, u32[]{:S(2)}) copy-start(s32[24,2]{0,1:T(2,128)} %param.7) | copy-start | bytes 580
  78.1 31.2 %all-to-all-start.3 = ((bf16[16,240,128]{2,1,0:T(8,128)(2,1)}), bf16[16,240,128]{2,1,0:T(8,128)(2,1)S(1)}, u32[]{:S(2)}, u32[]{:S(2)}) async-start(bf16[16,240,128]{2,1,0:T(8,128)(2,1)} %reshape.106), calls=%async_computation.3 | async-start | bytes 1966080 | tf_op jit(solution)/shard_map/all_to_all | solution.py:65
  110.4 16.0 %all-to-all-start.4 = ((bf16[16,2,960]{2,1,0:T(2,128)(2,1)}), bf16[16,2,960]{2,1,0:T(2,128)(2,1)S(1)}, u32[]{:S(2)}, u32[]{:S(2)}) async-start(bf16[16,2,960]{2,1,0:T(2,128)(2,1)} %reshape.114), calls=%async_computation.4 | async-start | bytes 131072 | tf_op jit(solution)/shard_map/all_to_all | solution.py:68

commit v9 on v6

--- a/solution.py
+++ b/solution.py
@@ -35,15 +35,15 @@
     picker = picker.reshape(EXPERTS * CAP, tok_count, 2).sum(axis=2)
     packed = jnp.dot(picker, tokens, preferred_element_type=jnp.float32).astype(jnp.bfloat16)
     packed = packed.reshape(EXPERTS, CAP, slice_width)
+    n_z, n_x = lax.axis_size(LOOP_AXES[0]), lax.axis_size(LOOP_AXES[1])
+    outgoing = jnp.broadcast_to(
+        jnp.repeat(packed, halves, axis=0)[:, None], (peers, n_z, CAP, slice_width)
+    ).reshape(peers * n_z, CAP, slice_width)
     arrived = lax.all_to_all(
-        jnp.repeat(packed, halves, axis=0), GROUP_AXES, split_axis=0, concat_axis=0, tiled=True
-    )
+        outgoing, GROUP_AXES + LOOP_AXES[:1], split_axis=0, concat_axis=0, tiled=True
+    ).reshape(peers, n_z, CAP, slice_width)
     lane = 128
-    dense = arrived.reshape(rows * slice_width // lane, lane)
-    n_z, n_x = lax.axis_size(LOOP_AXES[0]), lax.axis_size(LOOP_AXES[1])
-    planes = lax.all_to_all(
-        jnp.broadcast_to(dense[None], (n_z,) + dense.shape), LOOP_AXES[0], 0, 0, tiled=True
-    )
+    planes = arrived.transpose(1, 0, 2, 3).reshape(n_z, rows * slice_width // lane, lane)
     spread = lax.all_to_all(
         jnp.broadcast_to(planes[None], (n_x,) + planes.shape), LOOP_AXES[1], 0, 0, tiled=True
     )

time: 126 us -> 124 us (0.984)
  blocking collectives: 48.1 us -> 43.3 us
    all_to_all x2 -> x1, blocking collectives: 33.9 us -> 28.5 us  [body(): lax.all_to_all(outgoing, GROUP_AXES + LOOP_AXES[:1], split_axis=0, concat...]
    all_to_all x1, starting transfers between devices: 3.77 us -> 5.19 us  [body(): summed = lax.all_to_all(by_slice, LOOP_AXES, 0, 0, tiled=True)]
where the time goes in v9:
time: 124 us; the launch traced here: 123 us
  blocking collectives  43.3 us (35%)
  waiting for transfers between devices  37.7 us (30%)
  starting transfers between devices  20.9 us (17%)
  local copies, waits for them, and re-layouts  12.5 us (10%)
  matrix products  7.3 us (6%)
  other arithmetic  1.39 us (1%)
    all_to_all x1, blocking collectives, body(): lax.all_to_all(outgoing, GROUP_AXES + LOOP_AXES[:1], split_axis=0, concat...  28.5 us
    all_to_all x1, waiting for transfers between devices, body(): summed = lax.all_to_all(by_slice, LOOP_AXES, 0, 0, tiled=True)  25.9 us
    all_to_all x1, blocking collectives, body(): lax.all_to_all(jnp.broadcast_to(planes[None], (n_x,) + planes.shape), LOO...  14.8 us
    ppermute x2, starting transfers between devices, swap_cores(): return lax.ppermute(x, 'c', [(0, 1), (1, 0)])  8.53 us
    all_to_all x1, waiting for transfers between devices, body(): lax.all_to_all(expert_out, GROUP_AXES, split_axis=0, concat_axis=0, tiled...  7.44 us
    all_to_all x1, starting transfers between devices, body(): lax.all_to_all(expert_out, GROUP_AXES, split_axis=0, concat_axis=0, tiled...  7.19 us
    all_to_all x1, starting transfers between devices, body(): summed = lax.all_to_all(by_slice, LOOP_AXES, 0, 0, tiled=True)  5.19 us
    ppermute x2, waiting for transfers between devices, swap_cores(): return lax.ppermute(x, 'c', [(0, 1), (1, 0)])  4.34 us
  transfers between devices with their start and end apart: 4, of which 4 were waited for; matrix products, arithmetic and copies ran while one was open for 0% of the time, Pallas kernels for 0%

profile of v9, /device:TPU:1, one launch (start us, length us, event | category | flops | bytes accessed | tf_op | source)
XLA Modules:
  0.0 123.4 jit_solution(6861194691829874570)
XLA Ops:
  0.0 0.0 copy-start
  0.0 0.9 copy.60
  0.9 0.1 eq.73
  1.0 0.1 fusion.22
  1.1 0.1 reduce_window_sum.11
  1.1 0.2 select_reduce_fusion
  1.3 0.1 eq.77
  1.4 0.1 copy.61
  1.5 0.7 multiply_add_fusion
  2.2 0.1 fusion.27
  2.3 0.9 convolution_convert_fusion.1
  3.3 0.4 reshape.117
  3.7 28.5 %all_to_all.20 = bf16[64,2,960]{2,1,0:T(2,128)(2,1)S(1)} all-to-all(bf16[64,2,960]{2,1,0:T(2,128)(2,1)S(1)} %reshape.117), channel_id=1, replica_groups=mesh['zl'=2,'yh'=4,'yl'=2,'c'=2,'zh'=4,'x'=4] {'zl','yh','yl','zh'}, dimensions={0} | all-to-all | bytes 491520 | tf_op jit(solution)/shard_map/all_to_all | solution.py:42
  32.2 0.4 reshape.118
  32.5 0.2 copy.87
  32.7 0.2 copy.64
  32.9 0.5 broadcast_in_dim.13
  33.4 0.1 broadcast_in_dim.28
  33.5 14.8 %all_to_all.21 = bf16[4,4,240,128]{3,2,1,0:T(8,128)(2,1)S(1)} all-to-all(bf16[4,4,240,128]{3,2,1,0:T(8,128)(2,1)S(1)} %broadcast_in_dim.28), channel_id=1, replica_groups=mesh['zl'=2,'yh'=4,'yl'=2,'c'=2,'zh'=4,'x'=4] {'x'}, dimensions={0} | all-to-all | bytes 1966080 | tf_op jit(solution)/shard_map/all_to_all | solution.py:47
  48.3 6.3 %collective-permute-start = (bf16[4,4,240,128]{3,2,1,0:T(8,128)(2,1)S(1)}, bf16[4,4,240,128]{3,2,1,0:T(8,128)(2,1)S(1)}, u32[]{:S(2)}, u32[]{:S(2)}) collective-permute-start(bf16[4,4,240,128]{3,2,1,0:T(8,128)(2,1)S(1)} %all_to_all.21), channel_id=1, source_target_pairs={{0,16},{16,0},{1,17},{17,1},{2,18},{18,2},{3,19},{19,3},{4,20},{20... | collective-permute-start | bytes 2949128 | tf_op jit(solution)/shard_map/ppermute | solution.py:21
  54.6 2.2 %collective-permute-done = bf16[4,4,240,128]{3,2,1,0:T(8,128)(2,1)S(1)} collective-permute-done((bf16[4,4,240,128]{3,2,1,0:T(8,128)(2,1)S(1)}, bf16[4,4,240,128]{3,2,1,0:T(8,128)(2,1)S(1)}, u32[]{:S(2)}, u32[]{:S(2)}) %collective-permute-start) | collective-permute-done | bytes 983072 | tf_op jit(solution)/shard_map/ppermute | solution.py:21
  56.8 0.1 pad_maximum_fusion
  56.9 2.9 %reshape.109 = bf16[4,4,320,192]{3,2,1,0:T(8,128)(2,1)} reshape(bf16[4,4,480,128]{3,2,1,0:T(8,128)(2,1)S(1)} %pad_maximum_fusion) | data formatting | bytes 3932160 | tf_op jit(solution)/shard_map/reshape | solution.py:51
  59.8 3.1 %fusion.9 = f32[320,256]{1,0:T(8,128)S(1)} fusion(bf16[4,4,320,192]{3,2,1,0:T(8,128)(2,1)} %reshape.109, bf16[4,4,192,256]{3,2,1,0:T(8,128)(2,1)} %bitcast.42), kind=kOutput, calls=%fused_computation.11 | convolution fusion | flops 503316480 | bytes 3866624 | tf_op jit(solution)/shard_map/xzrf,zxfh->rh/dot_general | solution.py:53
  62.9 0.0 copy-done.1
  62.9 0.4 copy-done.4
  63.3 0.7 multiply_convert_fusion
  64.0 0.0 copy-done
  64.0 0.4 fusion
  64.5 2.3 %collective-permute-start.1 = (bf16[3072,160]{0,1:T(8,128)(2,1)S(1)}, bf16[3072,160]{0,1:T(8,128)(2,1)S(1)}, u32[]{:S(2)}, u32[]{:S(2)}) collective-permute-start(bf16[3072,160]{0,1:T(8,128)(2,1)S(1)} %fusion), channel_id=1, source_target_pairs={{0,16},{16,0},{1,17},{17,1},{2,18},{18,2},{3,19},{19,3},{4,20},{20... | collective-permute-start | bytes 2949128 | tf_op jit(solution)/shard_map/ppermute | solution.py:21
  66.8 2.2 %collective-permute-done.1 = bf16[3072,160]{0,1:T(8,128)(2,1)S(1)} collective-permute-done((bf16[3072,160]{0,1:T(8,128)(2,1)S(1)}, bf16[3072,160]{0,1:T(8,128)(2,1)S(1)}, u32[]{:S(2)}, u32[]{:S(2)}) %collective-permute-start.1) | collective-permute-done | bytes 983072 | tf_op jit(solution)/shard_map/ppermute | solution.py:21
  68.9 1.4 %add_convert_fusion = bf16[3072,160]{0,1:T(8,128)(2,1)} fusion(bf16[3072,160]{0,1:T(8,128)(2,1)S(1)} %collective-permute-done.1, bf16[1,256,3072]{2,1,0:T(8,128)(2,1)S(1)} %copy-done, bf16[320,256]{1,0:T(8,128)(2,1)S(1)} %multiply_convert_fusion), kind=kOutput, calls=%fused_computation.4 | convolution fusion | flops 253132800 | bytes 3620864 | tf_op jit(solution)/shard_map/dot_general | solution.py:61
  70.3 1.6 %copy.69 = bf16[3072,160]{1,0:T(8,128)(2,1)S(1)} copy(bf16[3072,160]{0,1:T(8,128)(2,1)} %add_convert_fusion) | data formatting | bytes 1966080 | tf_op jit(solution)/shard_map/convert_element_type | solution.py:64
  71.9 0.0 copy-start.2
  71.9 3.4 %reshape.110 = bf16[16,240,128]{2,1,0:T(8,128)(2,1)} reshape(bf16[3072,160]{1,0:T(8,128)(2,1)S(1)} %copy.69) | data formatting | bytes 1966080 | tf_op jit(solution)/shard_map/reshape | solution.py:65
  75.3 5.2 %all-to-all-start.2 = ((bf16[16,240,128]{2,1,0:T(8,128)(2,1)}), bf16[16,240,128]{2,1,0:T(8,128)(2,1)S(1)}, u32[]{:S(2)}, u32[]{:S(2)}) async-start(bf16[16,240,128]{2,1,0:T(8,128)(2,1)} %reshape.110), calls=%async_computation.2 | async-start | bytes 1966080 | tf_op jit(solution)/shard_map/all_to_all | solution.py:66
  80.5 0.0 copy-done.2
  80.6 25.9 %all-to-all-done.2 = bf16[16,240,128]{2,1,0:T(8,128)(2,1)S(1)} async-done(((bf16[16,240,128]{2,1,0:T(8,128)(2,1)}), bf16[16,240,128]{2,1,0:T(8,128)(2,1)S(1)}, u32[]{:S(2)}, u32[]{:S(2)}) %all-to-all-start.2) | async-done | bytes 983072 | tf_op jit(solution)/shard_map/all_to_all | solution.py:66
  106.5 0.1 reduce_sum.44
  106.7 0.1 convert_element_type.47
  106.8 0.1 copy.70
  107.0 0.7 reshape.119
  107.7 7.2 %all-to-all-start.3 = ((bf16[16,2,960]{2,1,0:T(2,128)(2,1)}), bf16[16,2,960]{2,1,0:T(2,128)(2,1)S(1)}, u32[]{:S(2)}, u32[]{:S(2)}) async-start(bf16[16,2,960]{2,1,0:T(2,128)(2,1)} %reshape.119), calls=%async_computation.3 | async-start | bytes 131072 | tf_op jit(solution)/shard_map/all_to_all | solution.py:69
  114.9 7.4 %all-to-all-done.3 = bf16[16,2,960]{2,1,0:T(2,128)(2,1)S(1)} async-done(((bf16[16,2,960]{2,1,0:T(2,128)(2,1)}), bf16[16,2,960]{2,1,0:T(2,128)(2,1)S(1)}, u32[]{:S(2)}, u32[]{:S(2)}) %all-to-all-start.3) | async-done | bytes 61472 | tf_op jit(solution)/shard_map/all_to_all | solution.py:69
  122.4 0.1 reshape.120
  122.5 0.1 reshape.115
  122.6 0.0 copy-done.3
  122.6 0.8 fusion.15
  (10 shorter events, 0.2 us)
Async XLA Ops:
  0.0 64.0 %copy-start = (bf16[1,256,3072]{2,1,0:T(8,128)(2,1)S(1)}, bf16[1,256,3072]{2,1,0:T(8,128)(2,1)}, u32[]{:S(2)}) copy-start(bf16[1,256,3072]{2,1,0:T(8,128)(2,1)} %param.11) | copy-start | bytes 4718596
  48.3 8.4 %collective-permute-start = (bf16[4,4,240,128]{3,2,1,0:T(8,128)(2,1)S(1)}, bf16[4,4,240,128]{3,2,1,0:T(8,128)(2,1)S(1)}, u32[]{:S(2)}, u32[]{:S(2)}) collective-permute-start(bf16[4,4,240,128]{3,2,1,0:T(8,128)(2,1)S(1)} %all_to_all.21), channel_id=1, source_target_pairs={{0,16},{16,0},{1,17},{17,1},{2,18},{18,2},{3,19},{19,3},{4,20},{20... | collective-permute-start | bytes 2949128 | tf_op jit(solution)/shard_map/ppermute | solution.py:21
  59.8 3.1 %copy-start.1 = (bf16[4,4,320,192]{3,2,1,0:T(8,128)(2,1)S(1)}, bf16[4,4,320,192]{3,2,1,0:T(8,128)(2,1)}, u32[]{:S(2)}) copy-start(bf16[4,4,320,192]{3,2,1,0:T(8,128)(2,1)} %reshape.109) | copy-start | bytes 5898244
  59.8 3.5 %copy-start.4 = (bf16[1,3072,256]{2,1,0:T(8,128)(2,1)S(1)}, bf16[1,3072,256]{2,1,0:T(8,128)(2,1)}, u32[]{:S(2)}) copy-start(bf16[1,3072,256]{2,1,0:T(8,128)(2,1)} %param.10) | copy-start | bytes 4718596
  64.5 4.5 %collective-permute-start.1 = (bf16[3072,160]{0,1:T(8,128)(2,1)S(1)}, bf16[3072,160]{0,1:T(8,128)(2,1)S(1)}, u32[]{:S(2)}, u32[]{:S(2)}) collective-permute-start(bf16[3072,160]{0,1:T(8,128)(2,1)S(1)} %fusion), channel_id=1, source_target_pairs={{0,16},{16,0},{1,17},{17,1},{2,18},{18,2},{3,19},{19,3},{4,20},{20... | collective-permute-start | bytes 2949128 | tf_op jit(solution)/shard_map/ppermute | solution.py:21
  71.9 8.6 %copy-start.2 = (f32[24,2]{0,1:T(2,128)S(1)}, f32[24,2]{0,1:T(2,128)}, u32[]{:S(2)}) copy-start(f32[24,2]{0,1:T(2,128)} %param.8) | copy-start | bytes 580
  75.3 47.2 %copy-start.3 = (s32[24,2]{0,1:T(2,128)S(1)}, s32[24,2]{0,1:T(2,128)}, u32[]{:S(2)}) copy-start(s32[24,2]{0,1:T(2,128)} %param.7) | copy-start | bytes 580
  75.3 31.2 %all-to-all-start.2 = ((bf16[16,240,128]{2,1,0:T(8,128)(2,1)}), bf16[16,240,128]{2,1,0:T(8,128)(2,1)S(1)}, u32[]{:S(2)}, u32[]{:S(2)}) async-start(bf16[16,240,128]{2,1,0:T(8,128)(2,1)} %reshape.110), calls=%async_computation.2 | async-start | bytes 1966080 | tf_op jit(solution)/shard_map/all_to_all | solution.py:66
  107.7 14.7 %all-to-all-start.3 = ((bf16[16,2,960]{2,1,0:T(2,128)(2,1)}), bf16[16,2,960]{2,1,0:T(2,128)(2,1)S(1)}, u32[]{:S(2)}, u32[]{:S(2)}) async-start(bf16[16,2,960]{2,1,0:T(2,128)(2,1)} %reshape.119), calls=%async_computation.3 | async-start | bytes 131072 | tf_op jit(solution)/shard_map/all_to_all | solution.py:69

commit v10 on v9

--- a/solution.py
+++ b/solution.py
@@ -62,13 +62,15 @@
     other_t = lax.dot_general(down_weight[0], hidden[rows:], down_t, preferred_element_type=jnp.float32)
     partner_t = swap_cores(other_t.astype(jnp.bfloat16))
     pair_t = (own_t + partner_t.astype(jnp.float32)).astype(jnp.bfloat16)
-    by_slice = pair_t.reshape(n_loop, slice_width * rows // lane, lane)
-    summed = lax.all_to_all(by_slice, LOOP_AXES, 0, 0, tiled=True)
-    summed = summed.astype(jnp.float32).sum(axis=0).reshape(slice_width, rows).T
-    expert_out = summed.astype(jnp.bfloat16).reshape(peers, CAP, slice_width)
-    returned = lax.all_to_all(expert_out, GROUP_AXES, split_axis=0, concat_axis=0, tiled=True).reshape(
-        rows, slice_width
+    by_slice = pair_t.reshape(n_z, n_x, slice_width * rows // lane, lane)
+    x_sum = lax.all_to_all(by_slice, LOOP_AXES[1], 1, 1, tiled=True)
+    x_sum = x_sum.astype(jnp.float32).sum(axis=1).astype(jnp.bfloat16)
+    x_sum = x_sum.reshape(n_z, slice_width, peers, CAP).transpose(2, 0, 3, 1)
+    back = lax.all_to_all(
+        x_sum.reshape(peers * n_z, CAP, slice_width), GROUP_AXES + LOOP_AXES[:1], 0, 0, tiled=True
     )
+    returned = back.reshape(peers, n_z, CAP, slice_width).astype(jnp.float32).sum(axis=1)
+    returned = returned.astype(jnp.bfloat16).reshape(rows, slice_width)
     column_index = jnp.arange(rows, dtype=jnp.int32)
     same_expert = (column_index // CAP // halves)[None, :] == assigned[:, None]
     same_slot = (column_index % CAP)[None, :] == position[:, None]

time: 124 us -> 129 us (1.040); the launches traced: 123 us -> 126 us
  waiting for transfers between devices: 37.7 us -> 15.6 us
  blocking collectives: 43.3 us -> 59.5 us
  local copies, waits for them, and re-layouts: 12.5 us -> 26.6 us
  starting transfers between devices: 20.9 us -> 15.6 us
    all_to_all x2 -> x1, waiting for transfers between devices: 33.4 us -> 11.3 us  [body(): lax.all_to_all(x_sum.reshape(peers * n_z, CAP, slice_width), GROUP_AXES +...]
    all_to_all x0 -> x1, blocking collectives: none -> 16.2 us  [body(): x_sum = lax.all_to_all(by_slice, LOOP_AXES[1], 1, 1, tiled=True)]
    reshape x3 -> x5, local copies, waits for them, and re-layouts: 3.48 us -> 17.3 us  [the longest x1 8.12 us: body(): x_sum = x_sum.reshape(n_z, slice_width, peers, CAP).transpose(2, 0, 3, 1)]
    all_to_all x2 -> x1, starting transfers between devices: 12.4 us -> 7.09 us  [body(): lax.all_to_all(x_sum.reshape(peers * n_z, CAP, slice_width), GROUP_AXES +...]
  transfers between devices with their start and end apart: 4 -> 3, of which waited for: 4 -> 3; matrix products, arithmetic and copies ran while one was open for 0% -> 0% of each run, Pallas kernels for 0% -> 0%
where the time goes in v10:
time: 129 us; the launch traced here: 126 us
  blocking collectives  59.5 us (46%)
  local copies, waits for them, and re-layouts  26.6 us (21%)
  starting transfers between devices  15.6 us (12%)
  waiting for transfers between devices  15.6 us (12%)
  matrix products  7.31 us (6%)
  other arithmetic  1.57 us (1%)
    all_to_all x1, blocking collectives, body(): lax.all_to_all(outgoing, GROUP_AXES + LOOP_AXES[:1], split_axis=0, concat...  28.5 us
    all_to_all x1, blocking collectives, body(): x_sum = lax.all_to_all(by_slice, LOOP_AXES[1], 1, 1, tiled=True)  16.2 us
    all_to_all x1, blocking collectives, body(): lax.all_to_all(jnp.broadcast_to(planes[None], (n_x,) + planes.shape), LOO...  14.8 us
    all_to_all x1, waiting for transfers between devices, body(): lax.all_to_all(x_sum.reshape(peers * n_z, CAP, slice_width), GROUP_AXES +...  11.3 us
    ppermute x2, starting transfers between devices, swap_cores(): return lax.ppermute(x, 'c', [(0, 1), (1, 0)])  8.54 us
    reshape x1, local copies, waits for them, and re-layouts, body(): x_sum = x_sum.reshape(n_z, slice_width, peers, CAP).transpose(2, 0, 3, 1)  8.12 us
    all_to_all x1, starting transfers between devices, body(): lax.all_to_all(x_sum.reshape(peers * n_z, CAP, slice_width), GROUP_AXES +...  7.09 us
    reshape x2, local copies, waits for them, and re-layouts, body(): by_slice = pair_t.reshape(n_z, n_x, slice_width * rows // lane, lane)  4.66 us
  transfers between devices with their start and end apart: 3, of which 3 were waited for; matrix products, arithmetic and copies ran while one was open for 0% of the time, Pallas kernels for 0%

profile of v10, /device:TPU:1, one launch (start us, length us, event | category | flops | bytes accessed | tf_op | source)
XLA Modules:
  0.0 126.5 jit_solution(12825758524344705109)
XLA Ops:
  0.0 0.0 copy-start
  0.0 0.9 copy.68
  0.9 0.1 eq.73
  1.0 0.1 fusion.22
  1.1 0.1 reduce_window_sum.11
  1.1 0.2 select_reduce_fusion
  1.3 0.1 eq.77
  1.4 0.1 copy.69
  1.5 0.7 multiply_add_fusion
  2.2 0.1 fusion.27
  2.3 0.9 convolution_convert_fusion.1
  3.3 0.4 reshape.123
  3.6 28.5 %all_to_all.20 = bf16[64,2,960]{2,1,0:T(2,128)(2,1)S(1)} all-to-all(bf16[64,2,960]{2,1,0:T(2,128)(2,1)S(1)} %reshape.123), channel_id=1, replica_groups=mesh['zl'=2,'yh'=4,'yl'=2,'c'=2,'zh'=4,'x'=4] {'zl','yh','yl','zh'}, dimensions={0} | all-to-all | bytes 491520 | tf_op jit(solution)/shard_map/all_to_all | solution.py:42
  32.1 0.4 reshape.124
  32.5 0.2 copy.102
  32.7 0.2 copy.72
  32.9 0.5 broadcast_in_dim.13
  33.4 0.1 broadcast_in_dim.28
  33.5 14.8 %all_to_all.21 = bf16[4,4,240,128]{3,2,1,0:T(8,128)(2,1)S(1)} all-to-all(bf16[4,4,240,128]{3,2,1,0:T(8,128)(2,1)S(1)} %broadcast_in_dim.28), channel_id=1, replica_groups=mesh['zl'=2,'yh'=4,'yl'=2,'c'=2,'zh'=4,'x'=4] {'x'}, dimensions={0} | all-to-all | bytes 1966080 | tf_op jit(solution)/shard_map/all_to_all | solution.py:47
  48.3 6.3 %collective-permute-start = (bf16[4,4,240,128]{3,2,1,0:T(8,128)(2,1)S(1)}, bf16[4,4,240,128]{3,2,1,0:T(8,128)(2,1)S(1)}, u32[]{:S(2)}, u32[]{:S(2)}) collective-permute-start(bf16[4,4,240,128]{3,2,1,0:T(8,128)(2,1)S(1)} %all_to_all.21), channel_id=1, source_target_pairs={{0,16},{16,0},{1,17},{17,1},{2,18},{18,2},{3,19},{19,3},{4,20},{20... | collective-permute-start | bytes 2949128 | tf_op jit(solution)/shard_map/ppermute | solution.py:21
  54.6 2.2 %collective-permute-done = bf16[4,4,240,128]{3,2,1,0:T(8,128)(2,1)S(1)} collective-permute-done((bf16[4,4,240,128]{3,2,1,0:T(8,128)(2,1)S(1)}, bf16[4,4,240,128]{3,2,1,0:T(8,128)(2,1)S(1)}, u32[]{:S(2)}, u32[]{:S(2)}) %collective-permute-start) | collective-permute-done | bytes 983072 | tf_op jit(solution)/shard_map/ppermute | solution.py:21
  56.8 0.1 pad_maximum_fusion
  56.9 2.9 %reshape.113 = bf16[4,4,320,192]{3,2,1,0:T(8,128)(2,1)} reshape(bf16[4,4,480,128]{3,2,1,0:T(8,128)(2,1)S(1)} %pad_maximum_fusion) | data formatting | bytes 3932160 | tf_op jit(solution)/shard_map/reshape | solution.py:51
  59.8 3.1 %fusion.9 = f32[320,256]{1,0:T(8,128)S(1)} fusion(bf16[4,4,320,192]{3,2,1,0:T(8,128)(2,1)} %reshape.113, bf16[4,4,192,256]{3,2,1,0:T(8,128)(2,1)} %bitcast.46), kind=kOutput, calls=%fused_computation.11 | convolution fusion | flops 503316480 | bytes 3866624 | tf_op jit(solution)/shard_map/xzrf,zxfh->rh/dot_general | solution.py:53
  62.9 0.0 copy-done.1
  62.9 0.4 copy-done.4
  63.2 0.7 multiply_convert_fusion
  64.0 0.0 copy-done
  64.0 0.4 fusion
  64.4 2.3 %collective-permute-start.1 = (bf16[3072,160]{0,1:T(8,128)(2,1)S(1)}, bf16[3072,160]{0,1:T(8,128)(2,1)S(1)}, u32[]{:S(2)}, u32[]{:S(2)}) collective-permute-start(bf16[3072,160]{0,1:T(8,128)(2,1)S(1)} %fusion), channel_id=1, source_target_pairs={{0,16},{16,0},{1,17},{17,1},{2,18},{18,2},{3,19},{19,3},{4,20},{20... | collective-permute-start | bytes 2949128 | tf_op jit(solution)/shard_map/ppermute | solution.py:21
  66.7 2.2 %collective-permute-done.1 = bf16[3072,160]{0,1:T(8,128)(2,1)S(1)} collective-permute-done((bf16[3072,160]{0,1:T(8,128)(2,1)S(1)}, bf16[3072,160]{0,1:T(8,128)(2,1)S(1)}, u32[]{:S(2)}, u32[]{:S(2)}) %collective-permute-start.1) | collective-permute-done | bytes 983072 | tf_op jit(solution)/shard_map/ppermute | solution.py:21
  68.9 1.4 %add_convert_fusion = bf16[3072,160]{0,1:T(8,128)(2,1)} fusion(bf16[3072,160]{0,1:T(8,128)(2,1)S(1)} %collective-permute-done.1, bf16[1,256,3072]{2,1,0:T(8,128)(2,1)S(1)} %copy-done, bf16[320,256]{1,0:T(8,128)(2,1)S(1)} %multiply_convert_fusion), kind=kOutput, calls=%fused_computation.4 | convolution fusion | flops 253132800 | bytes 3620864 | tf_op jit(solution)/shard_map/dot_general | solution.py:61
  70.3 1.6 %copy.77 = bf16[3072,160]{1,0:T(8,128)(2,1)S(1)} copy(bf16[3072,160]{0,1:T(8,128)(2,1)} %add_convert_fusion) | data formatting | bytes 1966080 | tf_op jit(solution)/shard_map/convert_element_type | solution.py:64
  71.9 3.4 %reshape.114 = bf16[4,4,240,128]{3,2,1,0:T(8,128)(2,1)} reshape(bf16[3072,160]{1,0:T(8,128)(2,1)S(1)} %copy.77) | data formatting | bytes 1966080 | tf_op jit(solution)/shard_map/reshape | solution.py:65
  75.3 1.3 %copy.78 = bf16[4,4,240,128]{3,2,0,1:T(8,128)(2,1)S(1)} copy(bf16[4,4,240,128]{3,2,1,0:T(8,128)(2,1)} %reshape.114) | data formatting | bytes 1966080 | tf_op jit(solution)/shard_map/reshape | solution.py:65
  76.5 16.2 %all_to_all.22 = bf16[4,4,240,128]{3,2,0,1:T(8,128)(2,1)S(1)} all-to-all(bf16[4,4,240,128]{3,2,0,1:T(8,128)(2,1)S(1)} %copy.78), channel_id=1, replica_groups=mesh['zl'=2,'yh'=4,'yl'=2,'c'=2,'zh'=4,'x'=4] {'x'}, dimensions={1} | all-to-all | bytes 1966080 | tf_op jit(solution)/shard_map/all_to_all | solution.py:66
  92.8 0.2 reduce_sum.56
  93.0 8.1 %reshape.115 = bf16[4,192,16,10]{3,2,1,0:T(8,128)(2,1)} reshape(bf16[4,240,128]{2,1,0:T(8,128)(2,1)S(1)} %reduce_sum.56) | data formatting | bytes 491520 | tf_op jit(solution)/shard_map/reshape | solution.py:68
  101.1 4.5 %copy.88 = bf16[16,4,10,192]{3,2,1,0:T(8,128)(2,1)S(1)} copy(bf16[16,4,10,192]{2,0,3,1:T(8,128)(2,1)} %bitcast.40) | data formatting | bytes 491520 | tf_op jit(solution)/shard_map/reshape | solution.py:70
  105.6 0.0 copy-start.3
  105.6 1.1 reshape.125
  106.7 7.1 %all-to-all-start.3 = ((bf16[64,2,960]{2,1,0:T(2,128)(2,1)}), bf16[64,2,960]{2,1,0:T(2,128)(2,1)S(1)}, u32[]{:S(2)}, u32[]{:S(2)}) async-start(bf16[64,2,960]{2,1,0:T(2,128)(2,1)} %reshape.125), calls=%async_computation.3 | async-start | bytes 524288 | tf_op jit(solution)/shard_map/all_to_all | solution.py:69
  113.8 0.0 copy-done.2
  113.8 11.3 %all-to-all-done.3 = bf16[64,2,960]{2,1,0:T(2,128)(2,1)S(1)} async-done(((bf16[64,2,960]{2,1,0:T(2,128)(2,1)}), bf16[64,2,960]{2,1,0:T(2,128)(2,1)S(1)}, u32[]{:S(2)}, u32[]{:S(2)}) %all-to-all-start.3) | async-done | bytes 245792 | tf_op jit(solution)/shard_map/all_to_all | solution.py:69
  125.1 0.4 reshape.126
  125.5 0.1 bitcast_reduce_fusion
  125.6 0.1 reshape.121
  125.7 0.8 fusion.15
  (10 shorter events, 0.1 us)
Async XLA Ops:
  0.0 64.0 %copy-start = (bf16[1,256,3072]{2,1,0:T(8,128)(2,1)S(1)}, bf16[1,256,3072]{2,1,0:T(8,128)(2,1)}, u32[]{:S(2)}) copy-start(bf16[1,256,3072]{2,1,0:T(8,128)(2,1)} %param.11) | copy-start | bytes 4718596
  48.3 8.4 %collective-permute-start = (bf16[4,4,240,128]{3,2,1,0:T(8,128)(2,1)S(1)}, bf16[4,4,240,128]{3,2,1,0:T(8,128)(2,1)S(1)}, u32[]{:S(2)}, u32[]{:S(2)}) collective-permute-start(bf16[4,4,240,128]{3,2,1,0:T(8,128)(2,1)S(1)} %all_to_all.21), channel_id=1, source_target_pairs={{0,16},{16,0},{1,17},{17,1},{2,18},{18,2},{3,19},{19,3},{4,20},{20... | collective-permute-start | bytes 2949128 | tf_op jit(solution)/shard_map/ppermute | solution.py:21
  59.8 3.1 %copy-start.1 = (bf16[4,4,320,192]{3,2,1,0:T(8,128)(2,1)S(1)}, bf16[4,4,320,192]{3,2,1,0:T(8,128)(2,1)}, u32[]{:S(2)}) copy-start(bf16[4,4,320,192]{3,2,1,0:T(8,128)(2,1)} %reshape.113) | copy-start | bytes 5898244
  59.8 3.5 %copy-start.4 = (bf16[1,3072,256]{2,1,0:T(8,128)(2,1)S(1)}, bf16[1,3072,256]{2,1,0:T(8,128)(2,1)}, u32[]{:S(2)}) copy-start(bf16[1,3072,256]{2,1,0:T(8,128)(2,1)} %param.10) | copy-start | bytes 4718596
  64.4 4.5 %collective-permute-start.1 = (bf16[3072,160]{0,1:T(8,128)(2,1)S(1)}, bf16[3072,160]{0,1:T(8,128)(2,1)S(1)}, u32[]{:S(2)}, u32[]{:S(2)}) collective-permute-start(bf16[3072,160]{0,1:T(8,128)(2,1)S(1)} %fusion), channel_id=1, source_target_pairs={{0,16},{16,0},{1,17},{17,1},{2,18},{18,2},{3,19},{19,3},{4,20},{20... | collective-permute-start | bytes 2949128 | tf_op jit(solution)/shard_map/ppermute | solution.py:21
  101.1 12.7 %copy-start.2 = (f32[24,2]{0,1:T(2,128)S(1)}, f32[24,2]{0,1:T(2,128)}, u32[]{:S(2)}) copy-start(f32[24,2]{0,1:T(2,128)} %param.8) | copy-start | bytes 580
  105.6 20.1 %copy-start.3 = (s32[24,2]{0,1:T(2,128)S(1)}, s32[24,2]{0,1:T(2,128)}, u32[]{:S(2)}) copy-start(s32[24,2]{0,1:T(2,128)} %param.7) | copy-start | bytes 580
  106.7 18.4 %all-to-all-start.3 = ((bf16[64,2,960]{2,1,0:T(2,128)(2,1)}), bf16[64,2,960]{2,1,0:T(2,128)(2,1)S(1)}, u32[]{:S(2)}, u32[]{:S(2)}) async-start(bf16[64,2,960]{2,1,0:T(2,128)(2,1)} %reshape.125), calls=%async_computation.3 | async-start | bytes 524288 | tf_op jit(solution)/shard_map/all_to_all | solution.py:69

commit v11 on v10

--- a/solution.py
+++ b/solution.py
@@ -57,17 +57,19 @@
         "xzrf,zxfh->rh", segment, up_weight[0].reshape(by_block), preferred_element_type=jnp.float32
     )
     hidden = (jax.nn.silu(gate_sum) * up_sum).astype(jnp.bfloat16)
-    down_t = (((0,), (1,)), ((), ()))
-    own_t = lax.dot_general(down_weight[0], hidden[:rows], down_t, preferred_element_type=jnp.float32)
-    other_t = lax.dot_general(down_weight[0], hidden[rows:], down_t, preferred_element_type=jnp.float32)
-    partner_t = swap_cores(other_t.astype(jnp.bfloat16))
-    pair_t = (own_t + partner_t.astype(jnp.float32)).astype(jnp.bfloat16)
-    by_slice = pair_t.reshape(n_z, n_x, slice_width * rows // lane, lane)
-    x_sum = lax.all_to_all(by_slice, LOOP_AXES[1], 1, 1, tiled=True)
-    x_sum = x_sum.astype(jnp.float32).sum(axis=1).astype(jnp.bfloat16)
-    x_sum = x_sum.reshape(n_z, slice_width, peers, CAP).transpose(2, 0, 3, 1)
+    down_cols = down_weight[0].reshape(hidden_width, n_z, n_x, slice_width).transpose(0, 2, 1, 3)
+    down_cols = down_cols.reshape(hidden_width, model_width)
+    own = jnp.dot(hidden[:rows], down_cols, preferred_element_type=jnp.float32)
+    partner = swap_cores(
+        jnp.dot(hidden[rows:], down_cols, preferred_element_type=jnp.float32).astype(jnp.bfloat16)
+    )
+    pair = (own + partner.astype(jnp.float32)).astype(jnp.bfloat16)
+    by_x = pair.reshape(rows, n_x, n_z * slice_width).transpose(1, 0, 2)
+    x_sum = lax.all_to_all(by_x, LOOP_AXES[1], 0, 0, tiled=True)
+    x_sum = x_sum.astype(jnp.float32).sum(axis=0).astype(jnp.bfloat16)
+    chunks = x_sum.reshape(peers, CAP, n_z, slice_width).transpose(0, 2, 1, 3)
     back = lax.all_to_all(
-        x_sum.reshape(peers * n_z, CAP, slice_width), GROUP_AXES + LOOP_AXES[:1], 0, 0, tiled=True
+        chunks.reshape(peers * n_z, CAP, slice_width), GROUP_AXES + LOOP_AXES[:1], 0, 0, tiled=True
     )
     returned = back.reshape(peers, n_z, CAP, slice_width).astype(jnp.float32).sum(axis=1)
     returned = returned.astype(jnp.bfloat16).reshape(rows, slice_width)

time: 129 us -> 116 us (0.90)
  local copies, waits for them, and re-layouts: 26.6 us -> 13.4 us
  other arithmetic: 1.57 us -> 4.3 us
  waiting for transfers between devices: 15.6 us -> 14 us
    reshape x4 -> x3, local copies, waits for them, and re-layouts: 17.2 us -> 0.44 us  [the longest x1 0.3 us: body(): chunks = x_sum.reshape(peers, CAP, n_z, slice_width).transpose(0, 2, 1, 3)]
    concatenate x1, other arithmetic: 0.13 us -> 2.91 us  [body(): jnp.concatenate([spread, other], axis=2)]
    reshape x1, local copies, waits for them, and re-layouts: 2.89 us -> 5.05 us  [body(): jnp.concatenate([spread, other], axis=2)]
    ppermute x2, waiting for transfers between devices: 4.34 us -> 2.53 us  [swap_cores(): return lax.ppermute(x, 'c', [(0, 1), (1, 0)])]
    convert_element_type x1 -> x0, local copies, waits for them, and re-layouts: 1.6 us -> none  [body(): pair_t = (own_t + partner_t.astype(jnp.float32)).astype(jnp.bfloat16)]
    unnamed x15 -> x18, local copies, waits for them, and re-layouts: 3.47 us -> 5.06 us
    transpose x0 -> x1, local copies, waits for them, and re-layouts: none -> 1.51 us  [body(): down_weight[0].reshape(hidden_width, n_z, n_x, slice_width)]
  transfers between devices with their start and end apart: 3 -> 3, of which waited for: 3 -> 2; matrix products, arithmetic and copies ran while one was open for 0% -> 3% of each run, Pallas kernels for 0% -> 0%
where the time goes in v11:
time: 116 us; the launch traced here: 114 us
  blocking collectives  60.3 us (52%)
  starting transfers between devices  15.3 us (13%)
  waiting for transfers between devices  14 us (12%)
  local copies, waits for them, and re-layouts  13.4 us (12%)
  matrix products  6.37 us (5%)
  other arithmetic  4.3 us (4%)
    all_to_all x1, blocking collectives, body(): lax.all_to_all(outgoing, GROUP_AXES + LOOP_AXES[:1], split_axis=0, concat...  28.5 us
    all_to_all x1, blocking collectives, body(): x_sum = lax.all_to_all(by_x, LOOP_AXES[1], 0, 0, tiled=True)  16.8 us
    all_to_all x1, blocking collectives, body(): lax.all_to_all(jnp.broadcast_to(planes[None], (n_x,) + planes.shape), LOO...  15 us
    all_to_all x1, waiting for transfers between devices, body(): lax.all_to_all(chunks.reshape(peers * n_z, CAP, slice_width), GROUP_AXES...  11.4 us
    ppermute x2, starting transfers between devices, swap_cores(): return lax.ppermute(x, 'c', [(0, 1), (1, 0)])  8.17 us
    all_to_all x1, starting transfers between devices, body(): lax.all_to_all(chunks.reshape(peers * n_z, CAP, slice_width), GROUP_AXES...  7.09 us
    unnamed x18, local copies, waits for them, and re-layouts  5.06 us
    reshape x1, local copies, waits for them, and re-layouts, body(): jnp.concatenate([spread, other], axis=2)  5.05 us
  transfers between devices with their start and end apart: 3, of which 2 were waited for; matrix products, arithmetic and copies ran while one was open for 3% of the time, Pallas kernels for 0%

profile of v11, /device:TPU:1, one launch (start us, length us, event | category | flops | bytes accessed | tf_op | source)
XLA Modules:
  0.0 113.9 jit_solution(7091969106011536506)
XLA Ops:
  0.0 0.0 copy-start
  0.0 0.9 copy.71
  0.9 0.1 eq.73
  1.0 0.1 fusion.20
  1.1 0.1 reduce_window_sum.11
  1.1 0.2 select_reduce_fusion
  1.3 0.1 eq.77
  1.4 0.1 copy.72
  1.5 0.7 multiply_add_fusion
  2.2 0.1 fusion.25
  2.3 0.9 convolution_convert_fusion.1
  3.3 0.4 reshape.127
  3.6 28.5 %all_to_all.20 = bf16[64,2,960]{2,1,0:T(2,128)(2,1)S(1)} all-to-all(bf16[64,2,960]{2,1,0:T(2,128)(2,1)S(1)} %reshape.127), channel_id=1, replica_groups=mesh['zl'=2,'yh'=4,'yl'=2,'c'=2,'zh'=4,'x'=4] {'zl','yh','yl','zh'}, dimensions={0} | all-to-all | bytes 491520 | tf_op jit(solution)/shard_map/all_to_all | solution.py:42
  32.1 0.4 reshape.128
  32.5 0.2 copy.109
  32.7 0.2 copy.75
  32.9 0.5 broadcast_in_dim.13
  33.4 0.0 copy-start.2
  33.4 0.1 broadcast_in_dim.28
  33.5 15.0 %all_to_all.21 = bf16[4,4,240,128]{3,2,1,0:T(8,128)(2,1)} all-to-all(bf16[4,4,240,128]{3,2,1,0:T(8,128)(2,1)S(1)} %broadcast_in_dim.28), channel_id=1, replica_groups=mesh['zl'=2,'yh'=4,'yl'=2,'c'=2,'zh'=4,'x'=4] {'x'}, dimensions={0} | all-to-all | bytes 1966080 | tf_op jit(solution)/shard_map/all_to_all | solution.py:47
  48.6 6.3 %collective-permute-start = (bf16[4,4,240,128]{3,2,1,0:T(8,128)(2,1)}, bf16[4,4,240,128]{3,2,1,0:T(8,128)(2,1)}, u32[]{:S(2)}, u32[]{:S(2)}) collective-permute-start(bf16[4,4,240,128]{3,2,1,0:T(8,128)(2,1)} %all_to_all.21), channel_id=1, source_target_pairs={{0,16},{16,0},{1,17},{17,1},{2,18},{18,2},{3,19},{19,3},{4,20},{20... | collective-permute-start | bytes 2949128 | tf_op jit(solution)/shard_map/ppermute | solution.py:21
  54.8 1.6 %copy.80 = bf16[1,256,3072]{1,2,0:T(8,128)(2,1)} copy(bf16[1,256,3072]{2,1,0:T(8,128)(2,1)S(1)} %copy-done.2) | data formatting | bytes 3145728 | tf_op args[5]
  56.4 1.5 %copy.81 = bf16[256,4,4,192]{0,3,2,1:T(8,128)(2,1)S(1)} copy(bf16[256,4,4,192]{0,3,1,2:T(8,128)(2,1)} %bitcast.43) | data formatting | bytes 3145728 | tf_op jit(solution)/shard_map/transpose | solution.py:60
  57.9 0.0 collective-permute-done
  58.0 2.9 %pad_maximum_fusion = bf16[4,4,480,128]{3,2,1,0:T(8,128)(2,1)} fusion(bf16[4,4,240,128]{3,2,1,0:T(8,128)(2,1)} %collective-permute-done, bf16[4,4,240,128]{3,2,1,0:T(8,128)(2,1)} %all_to_all.21), kind=kLoop, calls=%fused_computation.1 | loop fusion | flops 3932160 | bytes 3932160 | tf_op jit(solution)/shard_map/concatenate | solution.py:51
  60.9 5.0 %reshape.116 = bf16[4,4,320,192]{3,2,1,0:T(8,128)(2,1)} reshape(bf16[4,4,480,128]{3,2,1,0:T(8,128)(2,1)} %pad_maximum_fusion) | data formatting | bytes 3932160 | tf_op jit(solution)/shard_map/reshape | solution.py:51
  65.9 2.6 %fusion.4 = f32[320,256]{1,0:T(8,128)S(1)} fusion(bf16[4,4,320,192]{3,2,1,0:T(8,128)(2,1)} %reshape.116, bf16[4,4,192,256]{3,2,1,0:T(8,128)(2,1)S(1)} %bitcast.40), kind=kOutput, calls=%fused_computation.7 | convolution fusion | flops 503316480 | bytes 3866624 | tf_op jit(solution)/shard_map/xzrf,zxfh->rh/dot_general | solution.py:53
  68.6 0.4 copy-done.5
  68.9 0.7 multiply_convert_fusion
  69.6 0.7 convolution_convert_fusion
  70.3 1.9 %collective-permute-start.1 = (bf16[160,3072]{1,0:T(8,128)(2,1)S(1)}, bf16[160,3072]{1,0:T(8,128)(2,1)S(1)}, u32[]{:S(2)}, u32[]{:S(2)}) collective-permute-start(bf16[160,3072]{1,0:T(8,128)(2,1)S(1)} %convolution_convert_fusion), channel_id=1, source_target_pairs={{0,16},{16,0},{1,17},{17,1},{2,18},{18,2},{3,19},{19,3},{4,20},{20... | collective-permute-start | bytes 2949128 | tf_op jit(solution)/shard_map/ppermute | solution.py:21
  72.2 2.5 %collective-permute-done.1 = bf16[160,3072]{1,0:T(8,128)(2,1)S(1)} collective-permute-done((bf16[160,3072]{1,0:T(8,128)(2,1)S(1)}, bf16[160,3072]{1,0:T(8,128)(2,1)S(1)}, u32[]{:S(2)}, u32[]{:S(2)}) %collective-permute-start.1) | collective-permute-done | bytes 983072 | tf_op jit(solution)/shard_map/ppermute | solution.py:21
  74.8 0.7 add_convert_fusion
  75.4 0.1 copy.108
  75.5 16.8 %all_to_all.22 = bf16[4,160,768]{2,1,0:T(8,128)(2,1)S(1)} all-to-all(bf16[4,160,768]{2,1,0:T(8,128)(2,1)S(1)} %bitcast.45), channel_id=1, replica_groups=mesh['zl'=2,'yh'=4,'yl'=2,'c'=2,'zh'=4,'x'=4] {'x'}, dimensions={0} | all-to-all | bytes 1966080 | tf_op jit(solution)/shard_map/all_to_all | solution.py:68
  92.3 0.1 reduce_sum.56
  92.4 0.0 copy-start.3
  92.4 0.3 reshape.119
  92.7 0.1 copy.92
  92.8 0.0 copy-start.4
  92.8 1.1 reshape.129
  93.9 7.1 %all-to-all-start.3 = ((bf16[64,2,960]{2,1,0:T(2,128)(2,1)}), bf16[64,2,960]{2,1,0:T(2,128)(2,1)S(1)}, u32[]{:S(2)}, u32[]{:S(2)}) async-start(bf16[64,2,960]{2,1,0:T(2,128)(2,1)} %reshape.129), calls=%async_computation.3 | async-start | bytes 524288 | tf_op jit(solution)/shard_map/all_to_all | solution.py:71
  101.1 11.4 %all-to-all-done.3 = bf16[64,2,960]{2,1,0:T(2,128)(2,1)S(1)} async-done(((bf16[64,2,960]{2,1,0:T(2,128)(2,1)}), bf16[64,2,960]{2,1,0:T(2,128)(2,1)S(1)}, u32[]{:S(2)}, u32[]{:S(2)}) %all-to-all-start.3) | async-done | bytes 245792 | tf_op jit(solution)/shard_map/all_to_all | solution.py:71
  112.5 0.4 reshape.130
  112.9 0.1 bitcast_reduce_fusion
  113.0 0.1 reshape.125
  113.1 0.0 copy-done.4
  113.1 0.8 fusion.10
  (12 shorter events, 0.1 us)
Async XLA Ops:
  0.0 65.9 %copy-start = (bf16[1,3072,256]{2,1,0:T(8,128)(2,1)S(1)}, bf16[1,3072,256]{2,1,0:T(8,128)(2,1)}, u32[]{:S(2)}) copy-start(bf16[1,3072,256]{2,1,0:T(8,128)(2,1)} %param.9) | copy-start | bytes 4718596
  33.4 21.5 %copy-start.2 = (bf16[1,256,3072]{2,1,0:T(8,128)(2,1)S(1)}, bf16[1,256,3072]{2,1,0:T(8,128)(2,1)}, u32[]{:S(2)}) copy-start(bf16[1,256,3072]{2,1,0:T(8,128)(2,1)} %param.11) | copy-start | bytes 4718596
  48.6 9.4 %collective-permute-start = (bf16[4,4,240,128]{3,2,1,0:T(8,128)(2,1)}, bf16[4,4,240,128]{3,2,1,0:T(8,128)(2,1)}, u32[]{:S(2)}, u32[]{:S(2)}) collective-permute-start(bf16[4,4,240,128]{3,2,1,0:T(8,128)(2,1)} %all_to_all.21), channel_id=1, source_target_pairs={{0,16},{16,0},{1,17},{17,1},{2,18},{18,2},{3,19},{19,3},{4,20},{20... | collective-permute-start | bytes 2949128 | tf_op jit(solution)/shard_map/ppermute | solution.py:21
  65.9 2.6 %copy-start.1 = (bf16[4,4,320,192]{3,2,1,0:T(8,128)(2,1)S(1)}, bf16[4,4,320,192]{3,2,1,0:T(8,128)(2,1)}, u32[]{:S(2)}) copy-start(bf16[4,4,320,192]{3,2,1,0:T(8,128)(2,1)} %reshape.116) | copy-start | bytes 5898244
  65.9 3.0 %copy-start.5 = (bf16[1,3072,256]{2,1,0:T(8,128)(2,1)S(1)}, bf16[1,3072,256]{2,1,0:T(8,128)(2,1)}, u32[]{:S(2)}) copy-start(bf16[1,3072,256]{2,1,0:T(8,128)(2,1)} %param.10) | copy-start | bytes 4718596
  70.3 4.5 %collective-permute-start.1 = (bf16[160,3072]{1,0:T(8,128)(2,1)S(1)}, bf16[160,3072]{1,0:T(8,128)(2,1)S(1)}, u32[]{:S(2)}, u32[]{:S(2)}) collective-permute-start(bf16[160,3072]{1,0:T(8,128)(2,1)S(1)} %convolution_convert_fusion), channel_id=1, source_target_pairs={{0,16},{16,0},{1,17},{17,1},{2,18},{18,2},{3,19},{19,3},{4,20},{20... | collective-permute-start | bytes 2949128 | tf_op jit(solution)/shard_map/ppermute | solution.py:21
  92.4 8.6 %copy-start.3 = (f32[24,2]{0,1:T(2,128)S(1)}, f32[24,2]{0,1:T(2,128)}, u32[]{:S(2)}) copy-start(f32[24,2]{0,1:T(2,128)} %param.8) | copy-start | bytes 580
  92.8 20.2 %copy-start.4 = (s32[24,2]{0,1:T(2,128)S(1)}, s32[24,2]{0,1:T(2,128)}, u32[]{:S(2)}) copy-start(s32[24,2]{0,1:T(2,128)} %param.7) | copy-start | bytes 580
  93.9 18.6 %all-to-all-start.3 = ((bf16[64,2,960]{2,1,0:T(2,128)(2,1)}), bf16[64,2,960]{2,1,0:T(2,128)(2,1)S(1)}, u32[]{:S(2)}, u32[]{:S(2)}) async-start(bf16[64,2,960]{2,1,0:T(2,128)(2,1)} %reshape.129), calls=%async_computation.3 | async-start | bytes 524288 | tf_op jit(solution)/shard_map/all_to_all | solution.py:71

commit v12 on v11

--- a/solution.py
+++ b/solution.py
@@ -57,14 +57,13 @@
         "xzrf,zxfh->rh", segment, up_weight[0].reshape(by_block), preferred_element_type=jnp.float32
     )
     hidden = (jax.nn.silu(gate_sum) * up_sum).astype(jnp.bfloat16)
-    down_cols = down_weight[0].reshape(hidden_width, n_z, n_x, slice_width).transpose(0, 2, 1, 3)
-    down_cols = down_cols.reshape(hidden_width, model_width)
-    own = jnp.dot(hidden[:rows], down_cols, preferred_element_type=jnp.float32)
+    own = jnp.dot(hidden[:rows], down_weight[0], preferred_element_type=jnp.float32)
     partner = swap_cores(
-        jnp.dot(hidden[rows:], down_cols, preferred_element_type=jnp.float32).astype(jnp.bfloat16)
+        jnp.dot(hidden[rows:], down_weight[0], preferred_element_type=jnp.float32).astype(jnp.bfloat16)
     )
     pair = (own + partner.astype(jnp.float32)).astype(jnp.bfloat16)
-    by_x = pair.reshape(rows, n_x, n_z * slice_width).transpose(1, 0, 2)
+    by_x = pair.reshape(rows, n_z, n_x, slice_width).transpose(2, 0, 1, 3)
+    by_x = by_x.reshape(n_x, rows, n_z * slice_width)
     x_sum = lax.all_to_all(by_x, LOOP_AXES[1], 0, 0, tiled=True)
     x_sum = x_sum.astype(jnp.float32).sum(axis=0).astype(jnp.bfloat16)
     chunks = x_sum.reshape(peers, CAP, n_z, slice_width).transpose(0, 2, 1, 3)

time: 116 us -> 117 us (level)
  other arithmetic: 4.3 us -> 1.52 us
  local copies, waits for them, and re-layouts: 13.4 us -> 15.2 us
  waiting for transfers between devices: 14 us -> 15.6 us
    reshape x1 -> x3, local copies, waits for them, and re-layouts: 0.07 us -> 6.95 us  [the longest x2 4.15 us: body(): by_x = pair.reshape(rows, n_z, n_x, slice_width).transpose(2, 0, 1, 3)]
    concatenate x1, other arithmetic: 2.91 us -> 0.13 us  [body(): jnp.concatenate([spread, other], axis=2)]
    reshape x1, local copies, waits for them, and re-layouts: 5.05 us -> 2.93 us  [body(): jnp.concatenate([spread, other], axis=2)]
    ppermute x2, waiting for transfers between devices: 2.53 us -> 4.34 us  [swap_cores(): return lax.ppermute(x, 'c', [(0, 1), (1, 0)])]
    unnamed x18 -> x15, local copies, waits for them, and re-layouts: 5.06 us -> 3.52 us
    transpose x1 -> x0, local copies, waits for them, and re-layouts: 1.51 us -> none  [body(): down_weight[0].reshape(hidden_width, n_z, n_x, slice_width)]
  transfers between devices with their start and end apart: 3 -> 3, of which waited for: 2 -> 3; matrix products, arithmetic and copies ran while one was open for 3% -> 0% of each run, Pallas kernels for 0% -> 0%
where the time goes in v12:
time: 117 us; the launch traced here: 115 us
  blocking collectives  59.5 us (51%)
  starting transfers between devices  15.6 us (13%)
  waiting for transfers between devices  15.6 us (13%)
  local copies, waits for them, and re-layouts  15.2 us (13%)
  matrix products  7.3 us (6%)
  other arithmetic  1.52 us (1%)
    all_to_all x1, blocking collectives, body(): lax.all_to_all(outgoing, GROUP_AXES + LOOP_AXES[:1], split_axis=0, concat...  28.5 us
    all_to_all x1, blocking collectives, body(): x_sum = lax.all_to_all(by_x, LOOP_AXES[1], 0, 0, tiled=True)  16.2 us
    all_to_all x1, blocking collectives, body(): lax.all_to_all(jnp.broadcast_to(planes[None], (n_x,) + planes.shape), LOO...  14.8 us
    all_to_all x1, waiting for transfers between devices, body(): lax.all_to_all(chunks.reshape(peers * n_z, CAP, slice_width), GROUP_AXES...  11.3 us
    ppermute x2, starting transfers between devices, swap_cores(): return lax.ppermute(x, 'c', [(0, 1), (1, 0)])  8.53 us
    all_to_all x1, starting transfers between devices, body(): lax.all_to_all(chunks.reshape(peers * n_z, CAP, slice_width), GROUP_AXES...  7.09 us
    ppermute x2, waiting for transfers between devices, swap_cores(): return lax.ppermute(x, 'c', [(0, 1), (1, 0)])  4.34 us
    reshape x2, local copies, waits for them, and re-layouts, body(): by_x = pair.reshape(rows, n_z, n_x, slice_width).transpose(2, 0, 1, 3)  4.15 us
  transfers between devices with their start and end apart: 3, of which 3 were waited for; matrix products, arithmetic and copies ran while one was open for 0% of the time, Pallas kernels for 0%

profile of v12, /device:TPU:1, one launch (start us, length us, event | category | flops | bytes accessed | tf_op | source)
XLA Modules:
  0.0 115.0 jit_solution(11730332960973805763)
XLA Ops:
  0.0 0.0 copy-start
  0.0 0.9 copy.65
  0.9 0.1 eq.73
  1.0 0.1 fusion.22
  1.1 0.1 reduce_window_sum.11
  1.1 0.2 select_reduce_fusion
  1.3 0.1 eq.77
  1.4 0.1 copy.66
  1.5 0.7 multiply_add_fusion
  2.2 0.1 fusion.27
  2.3 0.9 convolution_convert_fusion.1
  3.3 0.4 reshape.127
  3.7 28.5 %all_to_all.20 = bf16[64,2,960]{2,1,0:T(2,128)(2,1)S(1)} all-to-all(bf16[64,2,960]{2,1,0:T(2,128)(2,1)S(1)} %reshape.127), channel_id=1, replica_groups=mesh['zl'=2,'yh'=4,'yl'=2,'c'=2,'zh'=4,'x'=4] {'zl','yh','yl','zh'}, dimensions={0} | all-to-all | bytes 491520 | tf_op jit(solution)/shard_map/all_to_all | solution.py:42
  32.2 0.4 reshape.128
  32.5 0.2 copy.100
  32.7 0.2 copy.69
  32.9 0.5 broadcast_in_dim.13
  33.4 0.1 broadcast_in_dim.28
  33.5 14.8 %all_to_all.21 = bf16[4,4,240,128]{3,2,1,0:T(8,128)(2,1)S(1)} all-to-all(bf16[4,4,240,128]{3,2,1,0:T(8,128)(2,1)S(1)} %broadcast_in_dim.28), channel_id=1, replica_groups=mesh['zl'=2,'yh'=4,'yl'=2,'c'=2,'zh'=4,'x'=4] {'x'}, dimensions={0} | all-to-all | bytes 1966080 | tf_op jit(solution)/shard_map/all_to_all | solution.py:47
  48.3 6.3 %collective-permute-start = (bf16[4,4,240,128]{3,2,1,0:T(8,128)(2,1)S(1)}, bf16[4,4,240,128]{3,2,1,0:T(8,128)(2,1)S(1)}, u32[]{:S(2)}, u32[]{:S(2)}) collective-permute-start(bf16[4,4,240,128]{3,2,1,0:T(8,128)(2,1)S(1)} %all_to_all.21), channel_id=1, source_target_pairs={{0,16},{16,0},{1,17},{17,1},{2,18},{18,2},{3,19},{19,3},{4,20},{20... | collective-permute-start | bytes 2949128 | tf_op jit(solution)/shard_map/ppermute | solution.py:21
  54.6 2.2 %collective-permute-done = bf16[4,4,240,128]{3,2,1,0:T(8,128)(2,1)S(1)} collective-permute-done((bf16[4,4,240,128]{3,2,1,0:T(8,128)(2,1)S(1)}, bf16[4,4,240,128]{3,2,1,0:T(8,128)(2,1)S(1)}, u32[]{:S(2)}, u32[]{:S(2)}) %collective-permute-start) | collective-permute-done | bytes 983072 | tf_op jit(solution)/shard_map/ppermute | solution.py:21
  56.8 0.1 pad_maximum_fusion
  56.9 2.9 %reshape.116 = bf16[4,4,320,192]{3,2,1,0:T(8,128)(2,1)} reshape(bf16[4,4,480,128]{3,2,1,0:T(8,128)(2,1)S(1)} %pad_maximum_fusion) | data formatting | bytes 3932160 | tf_op jit(solution)/shard_map/reshape | solution.py:51
  59.8 3.1 %fusion.9 = f32[320,256]{1,0:T(8,128)S(1)} fusion(bf16[4,4,320,192]{3,2,1,0:T(8,128)(2,1)} %reshape.116, bf16[4,4,192,256]{3,2,1,0:T(8,128)(2,1)} %bitcast.44), kind=kOutput, calls=%fused_computation.11 | convolution fusion | flops 503316480 | bytes 3866624 | tf_op jit(solution)/shard_map/xzrf,zxfh->rh/dot_general | solution.py:53
  62.9 0.0 copy-done.1
  62.9 0.4 copy-done.4
  63.3 0.7 multiply_convert_fusion
  64.0 0.0 copy-done
  64.0 0.4 convolution_convert_fusion
  64.5 2.3 %collective-permute-start.1 = (bf16[160,3072]{1,0:T(8,128)(2,1)S(1)}, bf16[160,3072]{1,0:T(8,128)(2,1)S(1)}, u32[]{:S(2)}, u32[]{:S(2)}) collective-permute-start(bf16[160,3072]{1,0:T(8,128)(2,1)S(1)} %convolution_convert_fusion), channel_id=1, source_target_pairs={{0,16},{16,0},{1,17},{17,1},{2,18},{18,2},{3,19},{19,3},{4,20},{20... | collective-permute-start | bytes 2949128 | tf_op jit(solution)/shard_map/ppermute | solution.py:21
  66.8 2.2 %collective-permute-done.1 = bf16[160,3072]{1,0:T(8,128)(2,1)S(1)} collective-permute-done((bf16[160,3072]{1,0:T(8,128)(2,1)S(1)}, bf16[160,3072]{1,0:T(8,128)(2,1)S(1)}, u32[]{:S(2)}, u32[]{:S(2)}) %collective-permute-start.1) | collective-permute-done | bytes 983072 | tf_op jit(solution)/shard_map/ppermute | solution.py:21
  68.9 1.4 %add_convert_fusion = bf16[160,3072]{1,0:T(8,128)(2,1)} fusion(bf16[160,3072]{1,0:T(8,128)(2,1)S(1)} %collective-permute-done.1, bf16[1,256,3072]{2,1,0:T(8,128)(2,1)S(1)} %copy-done, bf16[320,256]{1,0:T(8,128)(2,1)S(1)} %multiply_convert_fusion), kind=kOutput, calls=%fused_computation.2 | convolution fusion | flops 253132800 | bytes 3620864 | tf_op jit(solution)/shard_map/dot_general | solution.py:60
  70.3 2.6 %reshape.117 = bf16[160,4,4,192]{3,2,1,0:T(4,128)(2,1)S(1)} reshape(bf16[160,3072]{1,0:T(8,128)(2,1)} %add_convert_fusion) | data formatting | bytes 1966080 | tf_op jit(solution)/shard_map/reshape | solution.py:65
  72.9 1.6 %copy.99 = bf16[160,4,4,192]{3,1,0,2:T(4,128)(2,1)} copy(bf16[160,4,4,192]{3,2,1,0:T(4,128)(2,1)S(1)} %reshape.117) | data formatting | bytes 1966080 | tf_op jit(solution)/shard_map/reshape | solution.py:65
  74.5 2.8 %reshape.118 = bf16[4,160,768]{2,1,0:T(8,128)(2,1)S(1)} reshape(bf16[4,160,4,192]{3,2,1,0:T(4,128)(2,1)} %bitcast.37) | data formatting | bytes 1966080 | tf_op jit(solution)/shard_map/reshape | solution.py:66
  77.3 16.2 %all_to_all.22 = bf16[4,160,768]{2,1,0:T(8,128)(2,1)S(1)} all-to-all(bf16[4,160,768]{2,1,0:T(8,128)(2,1)S(1)} %reshape.118), channel_id=1, replica_groups=mesh['zl'=2,'yh'=4,'yl'=2,'c'=2,'zh'=4,'x'=4] {'x'}, dimensions={0} | all-to-all | bytes 1966080 | tf_op jit(solution)/shard_map/all_to_all | solution.py:67
  93.5 0.2 reduce_sum.56
  93.7 0.0 copy-start.2
  93.7 0.3 reshape.119
  94.0 0.1 copy.84
  94.1 0.0 copy-start.3
  94.1 1.1 reshape.129
  95.2 7.1 %all-to-all-start.3 = ((bf16[64,2,960]{2,1,0:T(2,128)(2,1)}), bf16[64,2,960]{2,1,0:T(2,128)(2,1)S(1)}, u32[]{:S(2)}, u32[]{:S(2)}) async-start(bf16[64,2,960]{2,1,0:T(2,128)(2,1)} %reshape.129), calls=%async_computation.3 | async-start | bytes 524288 | tf_op jit(solution)/shard_map/all_to_all | solution.py:70
  102.4 11.3 %all-to-all-done.3 = bf16[64,2,960]{2,1,0:T(2,128)(2,1)S(1)} async-done(((bf16[64,2,960]{2,1,0:T(2,128)(2,1)}), bf16[64,2,960]{2,1,0:T(2,128)(2,1)S(1)}, u32[]{:S(2)}, u32[]{:S(2)}) %all-to-all-start.3) | async-done | bytes 245792 | tf_op jit(solution)/shard_map/all_to_all | solution.py:70
  113.6 0.4 reshape.130
  114.0 0.1 bitcast_reduce_fusion
  114.1 0.1 reshape.125
  114.2 0.8 fusion.15
  (10 shorter events, 0.1 us)
Async XLA Ops:
  0.0 64.0 %copy-start = (bf16[1,256,3072]{2,1,0:T(8,128)(2,1)S(1)}, bf16[1,256,3072]{2,1,0:T(8,128)(2,1)}, u32[]{:S(2)}) copy-start(bf16[1,256,3072]{2,1,0:T(8,128)(2,1)} %param.11) | copy-start | bytes 4718596
  48.3 8.4 %collective-permute-start = (bf16[4,4,240,128]{3,2,1,0:T(8,128)(2,1)S(1)}, bf16[4,4,240,128]{3,2,1,0:T(8,128)(2,1)S(1)}, u32[]{:S(2)}, u32[]{:S(2)}) collective-permute-start(bf16[4,4,240,128]{3,2,1,0:T(8,128)(2,1)S(1)} %all_to_all.21), channel_id=1, source_target_pairs={{0,16},{16,0},{1,17},{17,1},{2,18},{18,2},{3,19},{19,3},{4,20},{20... | collective-permute-start | bytes 2949128 | tf_op jit(solution)/shard_map/ppermute | solution.py:21
  59.8 3.1 %copy-start.1 = (bf16[4,4,320,192]{3,2,1,0:T(8,128)(2,1)S(1)}, bf16[4,4,320,192]{3,2,1,0:T(8,128)(2,1)}, u32[]{:S(2)}) copy-start(bf16[4,4,320,192]{3,2,1,0:T(8,128)(2,1)} %reshape.116) | copy-start | bytes 5898244
  59.8 3.5 %copy-start.4 = (bf16[1,3072,256]{2,1,0:T(8,128)(2,1)S(1)}, bf16[1,3072,256]{2,1,0:T(8,128)(2,1)}, u32[]{:S(2)}) copy-start(bf16[1,3072,256]{2,1,0:T(8,128)(2,1)} %param.10) | copy-start | bytes 4718596
  64.5 4.5 %collective-permute-start.1 = (bf16[160,3072]{1,0:T(8,128)(2,1)S(1)}, bf16[160,3072]{1,0:T(8,128)(2,1)S(1)}, u32[]{:S(2)}, u32[]{:S(2)}) collective-permute-start(bf16[160,3072]{1,0:T(8,128)(2,1)S(1)} %convolution_convert_fusion), channel_id=1, source_target_pairs={{0,16},{16,0},{1,17},{17,1},{2,18},{18,2},{3,19},{19,3},{4,20},{20... | collective-permute-start | bytes 2949128 | tf_op jit(solution)/shard_map/ppermute | solution.py:21
  93.7 8.6 %copy-start.2 = (f32[24,2]{0,1:T(2,128)S(1)}, f32[24,2]{0,1:T(2,128)}, u32[]{:S(2)}) copy-start(f32[24,2]{0,1:T(2,128)} %param.8) | copy-start | bytes 580
  94.1 20.1 %copy-start.3 = (s32[24,2]{0,1:T(2,128)S(1)}, s32[24,2]{0,1:T(2,128)}, u32[]{:S(2)}) copy-start(s32[24,2]{0,1:T(2,128)} %param.7) | copy-start | bytes 580
  95.2 18.4 %all-to-all-start.3 = ((bf16[64,2,960]{2,1,0:T(2,128)(2,1)}), bf16[64,2,960]{2,1,0:T(2,128)(2,1)S(1)}, u32[]{:S(2)}, u32[]{:S(2)}) async-start(bf16[64,2,960]{2,1,0:T(2,128)(2,1)} %reshape.129), calls=%async_computation.3 | async-start | bytes 524288 | tf_op jit(solution)/shard_map/all_to_all | solution.py:70
